TPU v7x, 512 devices: a whole 4x8x8 slice. The times are simulated.
512 devices in a mesh: ctx: 128 (over z_hi, x, y), head: 4 (over z_lo, core).
Axes of the slice: x: 4, y: 8, z: 8 (z_hi: 4, z_lo: 2; z = z_hi * 2 + z_lo), core: 2. Of those that a mesh axis runs over, the one named last changes fastest.
Arguments:
- queries: bfloat16 [32768, 4096], P(('ctx', 'head')), may hold values from -200 to 200
- normed_key_state: bfloat16 [32768, 2048], P(('ctx', 'head')), may hold values from -5 to 5
- value_state_rows: bfloat16 [32768, 2048], P(('ctx', 'head')), may hold values from -6 to 6
- output_gradient: bfloat16 [32768, 4096], P(('ctx', 'head')), may hold values from -6 to 6
- doc_start: int32 [32768], P('ctx'), may hold values from 0 to 32767, as said below
Outputs:
- grad_queries: bfloat16 [32768, 4096], P(('ctx', 'head'))
- key_gradient: bfloat16 [32768, 2048], P(('ctx', 'head'))
- value_gradient: bfloat16 [32768, 2048], P(('ctx', 'head'))
Inputs may be any that keep to these rules, and one draw needn't show every extreme that they name: doc_start[t] is the first position of the document that holds token t: doc_start[0] = 0, each doc_start[t] equals t or doc_start[t - 1], and the last token, position 32767, begins a document of its own.
All inputs are finite; a program needn't handle non-finite values.
Results may differ from a plain program's by a relative error of at most 0.007.
Values may be sent and summed in bfloat16 or wider, within the bound.
No kernel may reach another device: no remote copies, remote signals or barrier semaphores. Data moves between devices by JAX's collectives and lax.ppermute only.
A program may use at most 64 MiB of HBM per device.

v0:
```python
import jax
import jax.numpy as jnp
from jax import lax
from jax.sharding import PartitionSpec as P

QUERY_HEADS = 32
KEY_VALUE_HEADS = 16
HEAD_SIZE = 128
WINDOW = 512
SPAN = 2


score_scale = 168.0 ** (-0.5)


def passed_along(block, axis, distance):
    devices = range(lax.axis_size(axis))
    route = [(i - distance, i) for i in devices if i - distance in devices]
    return lax.ppermute(block, axis, route)


def pair_scores(query_heads, key_block):
    return score_scale * jnp.einsum(
        "tgjd,kgd->gjtk", query_heads, key_block, preferred_element_type=jnp.float32
    )


def local(queries, normed_key_state, value_state_rows, output_gradient, doc_start):
    query_loc, key_loc, value_loc, grad_loc = (
        lax.all_to_all(queries, "head", split_axis=1, concat_axis=0, tiled=True),
        lax.all_to_all(normed_key_state, "head", split_axis=1, concat_axis=0, tiled=True),
        lax.all_to_all(value_state_rows, "head", split_axis=1, concat_axis=0, tiled=True),
        lax.all_to_all(output_gradient, "head", split_axis=1, concat_axis=0, tiled=True),
    )
    tok_rows = query_loc.shape[0]
    kv_groups = key_loc.shape[1] // HEAD_SIZE
    group_share = QUERY_HEADS // KEY_VALUE_HEADS
    query_heads = query_loc.reshape(tok_rows, kv_groups, group_share, HEAD_SIZE)
    grad_heads = grad_loc.reshape(tok_rows, kv_groups, group_share, HEAD_SIZE)
    kv_local = jnp.stack([key_loc, value_loc])
    kv_blocks = [kv_local]
    for distance in range(1, SPAN + 1):
        kv_blocks.append(passed_along(kv_local, "ctx", distance))
    shard_index = lax.axis_index("ctx")
    local_iota = jnp.arange(tok_rows, dtype=jnp.int32)
    query_pos = shard_index * tok_rows + local_iota

    def visible(distance):
        key_pos = (shard_index - distance) * tok_rows + local_iota
        return (
            (key_pos[None, :] >= doc_start[:, None])
            & (key_pos[None, :] <= query_pos[:, None])
            & (query_pos[:, None] - key_pos[None, :] < WINDOW)
        )

    def unpack(kv_block):
        return (
            kv_block[0].reshape(tok_rows, kv_groups, HEAD_SIZE),
            kv_block[1].reshape(tok_rows, kv_groups, HEAD_SIZE),
        )

    masks = [visible(distance) for distance in range(SPAN + 1)]
    stat_shape = (kv_groups, group_share, tok_rows)
    running = (
        jnp.full(stat_shape, -jnp.inf, jnp.float32),
        jnp.zeros(stat_shape, jnp.float32),
        jnp.zeros(stat_shape, jnp.float32),
    )
    for distance in range(SPAN + 1):
        gather_key_block, gather_value_block = unpack(kv_blocks[distance])
        gather_masked = jnp.where(
            masks[distance], pair_scores(query_heads, gather_key_block), -jnp.inf
        )
        gather_dprob = jnp.einsum(
            "tgjd,kgd->gjtk", grad_heads, gather_value_block, preferred_element_type=jnp.float32
        )
        new_max = jnp.maximum(running[0], jnp.max(gather_masked, axis=-1))
        factor = jnp.exp(running[0] - new_max)
        weights = jnp.exp(gather_masked - new_max[..., None])
        running = (
            new_max,
            running[1] * factor + jnp.sum(weights, axis=-1),
            running[2] * factor + jnp.sum(weights * gather_dprob, axis=-1),
        )
    log_total = running[0] + jnp.log(running[1])
    delta = running[2] / running[1]
    zero_parts = (
        jnp.zeros((tok_rows, kv_groups, group_share, HEAD_SIZE), jnp.float32),
        jnp.zeros((2, tok_rows, kv_groups * HEAD_SIZE), jnp.float32),
    )
    query_total = zero_parts[0]
    kv_parts = []
    for distance in range(SPAN + 1):
        key_block, value_block = unpack(kv_blocks[distance])
        masked = jnp.where(masks[distance], pair_scores(query_heads, key_block), -jnp.inf)
        prob = jnp.exp(masked - log_total[..., None])
        dprob = jnp.einsum(
            "tgjd,kgd->gjtk", grad_heads, value_block, preferred_element_type=jnp.float32
        )
        dscore = (prob * (dprob - delta[..., None])).astype(jnp.bfloat16)
        prob_half = prob.astype(jnp.bfloat16)
        query_part = score_scale * jnp.einsum(
            "gjtk,kgd->tgjd", dscore, key_block, preferred_element_type=jnp.float32
        )
        key_part = score_scale * jnp.einsum(
            "gjtk,tgjd->kgd", dscore, query_heads, preferred_element_type=jnp.float32
        )
        value_part = jnp.einsum(
            "gjtk,tgjd->kgd", prob_half, grad_heads, preferred_element_type=jnp.float32
        )
        query_part, kv_part = (
            query_part,
            jnp.stack([key_part, value_part]).reshape(2, tok_rows, kv_groups * HEAD_SIZE),
        )
        query_total = query_total + query_part
        kv_parts.append(kv_part)
    kv_total = kv_parts[0]
    for distance in range(1, SPAN + 1):
        kv_total = kv_total + passed_along(kv_parts[distance], "ctx", -distance)
    grad_query_loc = query_total.reshape(tok_rows, kv_groups * group_share * HEAD_SIZE).astype(
        jnp.bfloat16
    )
    grad_key_loc = kv_total[0].astype(jnp.bfloat16)
    grad_value_loc = kv_total[1].astype(jnp.bfloat16)
    return (
        lax.all_to_all(grad_query_loc, "head", split_axis=0, concat_axis=1, tiled=True),
        lax.all_to_all(grad_key_loc, "head", split_axis=0, concat_axis=1, tiled=True),
        lax.all_to_all(grad_value_loc, "head", split_axis=0, concat_axis=1, tiled=True),
    )


def solution(mesh):
    placed = (
        P(("ctx", "head"), None),
        P(("ctx", "head"), None),
        P(("ctx", "head"), None),
        P(("ctx", "head"), None),
        P("ctx"),
    )
    return jax.shard_map(
        local,
        mesh=mesh,
        in_specs=placed,
        out_specs=(P(("ctx", "head"), None), P(("ctx", "head"), None), P(("ctx", "head"), None)),
        check_vma=False,
    )
```

profile of v0, /device:TPU:54, one launch (start us, length us, event | category | flops | bytes accessed | tf_op | source)
XLA Modules:
  0.0 253.9 jit_solution(12213496482902532726)
XLA Ops:
  0.7 1.8 copy.234
  2.4 3.6 %all-to-all-start = ((bf16[64,4,512]{2,0,1:T(8,128)(2,1)}), bf16[64,4,512]{2,0,1:T(8,128)(2,1)S(1)}, u32[]{:S(2)}, u32[]{:S(2)}) async-start(bf16[64,4,512]{2,0,1:T(8,128)(2,1)} %bitcast.174), calls=%async_computation | async-start | bytes 524288 | tf_op jit(solution)/shard_map/all_to_all | solution.py:31
  6.1 1.7 copy.233
  7.7 4.3 %all-to-all-done = bf16[64,4,512]{2,0,1:T(8,128)(2,1)S(1)} async-done(((bf16[64,4,512]{2,0,1:T(8,128)(2,1)}), bf16[64,4,512]{2,0,1:T(8,128)(2,1)S(1)}, u32[]{:S(2)}, u32[]{:S(2)}) %all-to-all-start) | async-done | bytes 262176 | tf_op jit(solution)/shard_map/all_to_all | solution.py:31
  12.1 3.4 %all-to-all-start.2 = ((bf16[64,4,512]{2,0,1:T(8,128)(2,1)}), bf16[64,4,512]{2,0,1:T(8,128)(2,1)S(1)}, u32[]{:S(2)}, u32[]{:S(2)}) async-start(bf16[64,4,512]{2,0,1:T(8,128)(2,1)} %bitcast.173), calls=%async_computation.2 | async-start | bytes 524288 | tf_op jit(solution)/shard_map/all_to_all | solution.py:32
  16.3 5.1 %all-to-all-done.2 = bf16[64,4,512]{2,0,1:T(8,128)(2,1)S(1)} async-done(((bf16[64,4,512]{2,0,1:T(8,128)(2,1)}), bf16[64,4,512]{2,0,1:T(8,128)(2,1)S(1)}, u32[]{:S(2)}, u32[]{:S(2)}) %all-to-all-start.2) | async-done | bytes 262176 | tf_op jit(solution)/shard_map/all_to_all | solution.py:32
  21.4 3.5 %all-to-all-start.1 = ((bf16[64,4,1024]{2,0,1:T(8,128)(2,1)}), bf16[64,4,1024]{2,0,1:T(8,128)(2,1)S(1)}, u32[]{:S(2)}, u32[]{:S(2)}) async-start(bf16[64,4,1024]{2,0,1:T(8,128)(2,1)} %bitcast.172), calls=%async_computation.1 | async-start | bytes 1048576 | tf_op jit(solution)/shard_map/all_to_all | solution.py:30
  25.8 7.9 %all-to-all-done.1 = bf16[64,4,1024]{2,0,1:T(8,128)(2,1)S(1)} async-done(((bf16[64,4,1024]{2,0,1:T(8,128)(2,1)}), bf16[64,4,1024]{2,0,1:T(8,128)(2,1)S(1)}, u32[]{:S(2)}, u32[]{:S(2)}) %all-to-all-start.1) | async-done | bytes 524320 | tf_op jit(solution)/shard_map/all_to_all | solution.py:30
  33.7 3.5 %all-to-all-start.3 = ((bf16[64,4,1024]{2,0,1:T(8,128)(2,1)}), bf16[64,4,1024]{2,0,1:T(8,128)(2,1)S(1)}, u32[]{:S(2)}, u32[]{:S(2)}) async-start(bf16[64,4,1024]{2,0,1:T(8,128)(2,1)} %bitcast.171), calls=%async_computation.3 | async-start | bytes 1048576 | tf_op jit(solution)/shard_map/all_to_all | solution.py:33
  37.2 0.9 fusion.38
  38.1 0.8 pad_maximum_fusion.2
  38.9 5.3 %collective-permute-start.1 = (bf16[2,256,512]{2,1,0:T(8,128)(2,1)}, bf16[2,256,512]{2,1,0:T(8,128)(2,1)}, u32[]{:S(2)}, u32[]{:S(2)}) collective-permute-start(bf16[2,256,512]{2,1,0:T(8,128)(2,1)} %pad_maximum_fusion.2), channel_id=1, source_target_pairs={{0,8},{4,12},{8,16},{12,20},{16,24},{20,28},{24,32},{28,36},{32,40... | collective-permute-start | bytes 1572872 | tf_op jit(solution)/shard_map/ppermute | solution.py:19
  44.3 3.5 %collective-permute-start = (bf16[2,256,512]{2,1,0:T(8,128)(2,1)}, bf16[2,256,512]{2,1,0:T(8,128)(2,1)}, u32[]{:S(2)}, u32[]{:S(2)}) collective-permute-start(bf16[2,256,512]{2,1,0:T(8,128)(2,1)} %pad_maximum_fusion.2), channel_id=1, source_target_pairs={{0,4},{4,8},{8,12},{12,16},{16,20},{20,24},{24,28},{28,32},{32,36}... | collective-permute-start | bytes 1572872 | tf_op jit(solution)/shard_map/ppermute | solution.py:19
  50.4 1.3 fusion.47
  51.8 2.4 fusion.6
  54.2 14.3 %collective-permute-done.1 = bf16[2,256,512]{2,1,0:T(8,128)(2,1)} collective-permute-done((bf16[2,256,512]{2,1,0:T(8,128)(2,1)}, bf16[2,256,512]{2,1,0:T(8,128)(2,1)}, u32[]{:S(2)}, u32[]{:S(2)}) %collective-permute-start.1) | collective-permute-done | bytes 524320 | tf_op jit(solution)/shard_map/ppermute | solution.py:19
  68.5 1.9 fusion.45
  70.4 1.8 copy.139
  72.2 1.8 copy.130
  74.0 5.3 %collective-permute-done = bf16[2,256,512]{2,1,0:T(8,128)(2,1)} collective-permute-done((bf16[2,256,512]{2,1,0:T(8,128)(2,1)}, bf16[2,256,512]{2,1,0:T(8,128)(2,1)}, u32[]{:S(2)}, u32[]{:S(2)}) %collective-permute-start) | collective-permute-done | bytes 524320 | tf_op jit(solution)/shard_map/ppermute | solution.py:19
  79.2 1.9 fusion.44
  81.1 1.8 copy.136
  82.9 1.8 copy.127
  84.7 1.5 fusion.48
  87.3 1.9 fusion
  89.3 1.9 fusion.3
  91.3 1.3 fusion.28
  92.5 1.3 fusion.26
  93.9 1.3 fusion.24
  95.2 2.1 copy.167
  97.2 1.2 copy.161
  98.5 2.1 copy.155
  100.6 6.8 %fusion.2 = (bf16[4,2,256,256]{2,3,1,0:T(8,128)(2,1)S(1)}, bf16[4,2,256,256]{2,3,1,0:T(8,128)(2,1)}, bf16[4,2,256,256]{2,3,1,0:T(8,128)(2,1)}) fusion(f32[4,256,256,2]{2,1,3,0:T(8,128)} %get-tuple-element.31, f32[4,2,256,256]{2,3,1,0:T(8,128)} %copy-done.1, f32[4,2,256]{2,1,0:T(2,128)S(1)} %add_divide_fusion, f32[4,2,256]{2,1,0:T(2,128)S(1)} %get-tuple-element.9, ...), kind=kLoop, calls=%fused_computation.4 | loop fusion | flops 6291456 | bytes 15745024 | tf_op jit(solution)/shard_map/convert_element_type | solution.py:100
  107.4 1.0 copy-done.4
  108.8 1.0 copy.166
  110.3 1.0 copy.160
  111.3 2.2 pad_maximum_fusion
  113.5 2.3 collective-permute-start.2
  115.8 2.2 pad_maximum_fusion.1
  118.1 5.2 %collective-permute-start.3 = (f32[2,256,512]{2,1,0:T(8,128)}, f32[2,256,512]{2,1,0:T(8,128)}, u32[]{:S(2)}, u32[]{:S(2)}) collective-permute-start(f32[2,256,512]{2,1,0:T(8,128)} %pad_maximum_fusion.1), channel_id=1, source_target_pairs={{8,0},{12,4},{16,8},{20,12},{24,16},{28,20},{32,24},{36,28},{40,32... | collective-permute-start | bytes 3145736 | tf_op jit(solution)/shard_map/ppermute | solution.py:19
  126.2 1.2 convert_element_type.39
  127.4 3.6 %all-to-all-start.4 = ((bf16[4,64,1024]{2,1,0:T(8,128)(2,1)}), bf16[4,64,1024]{2,1,0:T(8,128)(2,1)S(1)}, u32[]{:S(2)}, u32[]{:S(2)}) async-start(bf16[4,64,1024]{2,1,0:T(8,128)(2,1)} %convert_element_type.39), calls=%async_computation.4 | async-start | bytes 1048576 | tf_op jit(solution)/shard_map/all_to_all | solution.py:126
  131.7 42.0 %collective-permute-done.2 = f32[2,256,512]{2,1,0:T(8,128)} collective-permute-done((f32[2,256,512]{2,1,0:T(8,128)}, f32[2,256,512]{2,1,0:T(8,128)}, u32[]{:S(2)}, u32[]{:S(2)}) %collective-permute-start.2) | collective-permute-done | bytes 1048608 | tf_op jit(solution)/shard_map/ppermute | solution.py:19
  173.7 57.3 %collective-permute-done.3 = f32[2,256,512]{2,1,0:T(8,128)} collective-permute-done((f32[2,256,512]{2,1,0:T(8,128)}, f32[2,256,512]{2,1,0:T(8,128)}, u32[]{:S(2)}, u32[]{:S(2)}) %collective-permute-start.3) | collective-permute-done | bytes 1048608 | tf_op jit(solution)/shard_map/ppermute | solution.py:19
  231.0 1.8 fusion.31
  233.5 10.2 %all_to_all.112 = bf16[4,64,512]{2,1,0:T(8,128)(2,1)S(1)} all-to-all(bf16[4,64,512]{2,1,0:T(8,128)(2,1)S(1)} %bitcast.204), channel_id=1, replica_groups=mesh['ctx'=128,'head'=4] {'head'}, dimensions={0} | all-to-all | bytes 524288 | tf_op jit(solution)/shard_map/all_to_all | solution.py:127
  243.8 3.4 %all-to-all-start.6 = ((bf16[4,64,512]{2,1,0:T(8,128)(2,1)}), bf16[4,64,512]{2,1,0:T(8,128)(2,1)S(1)}, u32[]{:S(2)}, u32[]{:S(2)}) async-start(bf16[4,64,512]{2,1,0:T(8,128)(2,1)} %bitcast.57), calls=%async_computation.6 | async-start | bytes 524288 | tf_op jit(solution)/shard_map/all_to_all | solution.py:128
  248.8 4.4 %all-to-all-done.6 = bf16[4,64,512]{2,1,0:T(8,128)(2,1)S(1)} async-done(((bf16[4,64,512]{2,1,0:T(8,128)(2,1)}), bf16[4,64,512]{2,1,0:T(8,128)(2,1)S(1)}, u32[]{:S(2)}, u32[]{:S(2)}) %all-to-all-start.6) | async-done | bytes 262176 | tf_op jit(solution)/shard_map/all_to_all | solution.py:128
  (61 shorter events, 13.0 us)
Async XLA Ops:
  0.6 14.8 %copy-start.13 = (bf16[64,4096]{1,0:T(8,128)(2,1)S(1)}, bf16[64,4096]{1,0:T(8,128)(2,1)}, u32[]{:S(2)}) copy-start(bf16[64,4096]{1,0:T(8,128)(2,1)} %param.5) | copy-start | bytes 1572868
  0.6 24.3 %copy-start.14 = (bf16[64,4096]{1,0:T(8,128)(2,1)S(1)}, bf16[64,4096]{1,0:T(8,128)(2,1)}, u32[]{:S(2)}) copy-start(bf16[64,4096]{1,0:T(8,128)(2,1)} %param.8) | copy-start | bytes 1572868
  2.4 9.6 %all-to-all-start = ((bf16[64,4,512]{2,0,1:T(8,128)(2,1)}), bf16[64,4,512]{2,0,1:T(8,128)(2,1)S(1)}, u32[]{:S(2)}, u32[]{:S(2)}) async-start(bf16[64,4,512]{2,0,1:T(8,128)(2,1)} %bitcast.174), calls=%async_computation | async-start | bytes 524288 | tf_op jit(solution)/shard_map/all_to_all | solution.py:31
  12.1 9.4 %all-to-all-start.2 = ((bf16[64,4,512]{2,0,1:T(8,128)(2,1)}), bf16[64,4,512]{2,0,1:T(8,128)(2,1)S(1)}, u32[]{:S(2)}, u32[]{:S(2)}) async-start(bf16[64,4,512]{2,0,1:T(8,128)(2,1)} %bitcast.173), calls=%async_computation.2 | async-start | bytes 524288 | tf_op jit(solution)/shard_map/all_to_all | solution.py:32
  15.5 21.7 %copy-start.16 = (s32[256]{0:T(256)S(1)}, s32[256]{0:T(256)}, u32[]{:S(2)}) copy-start(s32[256]{0:T(256)} %param.9) | copy-start | bytes 3076
  21.4 12.3 %all-to-all-start.1 = ((bf16[64,4,1024]{2,0,1:T(8,128)(2,1)}), bf16[64,4,1024]{2,0,1:T(8,128)(2,1)S(1)}, u32[]{:S(2)}, u32[]{:S(2)}) async-start(bf16[64,4,1024]{2,0,1:T(8,128)(2,1)} %bitcast.172), calls=%async_computation.1 | async-start | bytes 1048576 | tf_op jit(solution)/shard_map/all_to_all | solution.py:30
  33.7 15.8 %all-to-all-start.3 = ((bf16[64,4,1024]{2,0,1:T(8,128)(2,1)}), bf16[64,4,1024]{2,0,1:T(8,128)(2,1)S(1)}, u32[]{:S(2)}, u32[]{:S(2)}) async-start(bf16[64,4,1024]{2,0,1:T(8,128)(2,1)} %bitcast.171), calls=%async_computation.3 | async-start | bytes 1048576 | tf_op jit(solution)/shard_map/all_to_all | solution.py:33
  38.9 29.6 %collective-permute-start.1 = (bf16[2,256,512]{2,1,0:T(8,128)(2,1)}, bf16[2,256,512]{2,1,0:T(8,128)(2,1)}, u32[]{:S(2)}, u32[]{:S(2)}) collective-permute-start(bf16[2,256,512]{2,1,0:T(8,128)(2,1)} %pad_maximum_fusion.2), channel_id=1, source_target_pairs={{0,8},{4,12},{8,16},{12,20},{16,24},{20,28},{24,32},{28,36},{32,40... | collective-permute-start | bytes 1572872 | tf_op jit(solution)/shard_map/ppermute | solution.py:19
  44.3 35.0 %collective-permute-start = (bf16[2,256,512]{2,1,0:T(8,128)(2,1)}, bf16[2,256,512]{2,1,0:T(8,128)(2,1)}, u32[]{:S(2)}, u32[]{:S(2)}) collective-permute-start(bf16[2,256,512]{2,1,0:T(8,128)(2,1)} %pad_maximum_fusion.2), channel_id=1, source_target_pairs={{0,4},{4,8},{8,12},{12,16},{16,20},{20,24},{24,28},{28,32},{32,36}... | collective-permute-start | bytes 1572872 | tf_op jit(solution)/shard_map/ppermute | solution.py:19
  50.4 1.4 copy-start.12
  84.7 1.5 copy-start.6
  86.2 6.4 %copy-start = (f32[4,2,256,256]{2,3,1,0:T(8,128)}, f32[4,2,256,256]{2,3,1,0:T(8,128)S(1)}, u32[]{:S(2)}) copy-start(f32[4,2,256,256]{2,3,1,0:T(8,128)S(1)} %get-tuple-element.30) | copy-start | bytes 6291460
  86.2 1.1 copy-start.10
  86.7 7.1 %copy-start.1 = (f32[4,2,256,256]{2,3,1,0:T(8,128)}, f32[4,2,256,256]{2,3,1,0:T(8,128)S(1)}, u32[]{:S(2)}) copy-start(f32[4,2,256,256]{2,3,1,0:T(8,128)S(1)} %get-tuple-element.26) | copy-start | bytes 6291460
  87.3 1.9 copy-start.11
  89.3 2.0 copy-start.15
  107.4 1.0 copy-start.4
  107.4 2.5 copy-start.3
  111.3 11.9 %copy-start.2 = (bf16[4,2,256,256]{2,3,1,0:T(8,128)(2,1)S(1)}, bf16[4,2,256,256]{2,3,1,0:T(8,128)(2,1)}, u32[]{:S(2)}) copy-start(bf16[4,2,256,256]{2,3,1,0:T(8,128)(2,1)} %get-tuple-element.21) | copy-start | bytes 3145732
  113.5 10.3 %copy-start.8 = (bf16[1,256,512]{1,2,0:T(8,128)(2,1)S(1)}, bf16[1,256,512]{1,2,0:T(8,128)(2,1)}, u32[]{:S(2)}) copy-start(bf16[1,256,512]{1,2,0:T(8,128)(2,1)} %copy.127) | copy-start | bytes 786436
  113.5 60.1 %collective-permute-start.2 = (f32[2,256,512]{2,1,0:T(8,128)}, f32[2,256,512]{2,1,0:T(8,128)}, u32[]{:S(2)}, u32[]{:S(2)}) collective-permute-start(f32[2,256,512]{2,1,0:T(8,128)} %pad_maximum_fusion), channel_id=1, source_target_pairs={{4,0},{8,4},{12,8},{16,12},{20,16},{24,20},{28,24},{32,28},{36,32}... | collective-permute-start | bytes 3145736 | tf_op jit(solution)/shard_map/ppermute | solution.py:19
  118.1 112.9 %collective-permute-start.3 = (f32[2,256,512]{2,1,0:T(8,128)}, f32[2,256,512]{2,1,0:T(8,128)}, u32[]{:S(2)}, u32[]{:S(2)}) collective-permute-start(f32[2,256,512]{2,1,0:T(8,128)} %pad_maximum_fusion.1), channel_id=1, source_target_pairs={{8,0},{12,4},{16,8},{20,12},{24,16},{28,20},{32,24},{36,28},{40,32... | collective-permute-start | bytes 3145736 | tf_op jit(solution)/shard_map/ppermute | solution.py:19
  123.8 1.2 copy-start.5
  123.9 1.3 copy-start.7
  127.4 103.6 %copy-start.9 = (f32[1,256,512]{2,1,0:T(8,128)S(1)}, f32[1,256,512]{2,1,0:T(8,128)}, u32[]{:S(2)}) copy-start(f32[1,256,512]{2,1,0:T(8,128)} %copy.155) | copy-start | bytes 1572868
  127.4 106.2 %all-to-all-start.4 = ((bf16[4,64,1024]{2,1,0:T(8,128)(2,1)}), bf16[4,64,1024]{2,1,0:T(8,128)(2,1)S(1)}, u32[]{:S(2)}, u32[]{:S(2)}) async-start(bf16[4,64,1024]{2,1,0:T(8,128)(2,1)} %convert_element_type.39), calls=%async_computation.4 | async-start | bytes 1048576 | tf_op jit(solution)/shard_map/all_to_all | solution.py:126
  243.8 9.4 %all-to-all-start.6 = ((bf16[4,64,512]{2,1,0:T(8,128)(2,1)}), bf16[4,64,512]{2,1,0:T(8,128)(2,1)S(1)}, u32[]{:S(2)}, u32[]{:S(2)}) async-start(bf16[4,64,512]{2,1,0:T(8,128)(2,1)} %bitcast.57), calls=%async_computation.6 | async-start | bytes 524288 | tf_op jit(solution)/shard_map/all_to_all | solution.py:128
where the time goes:
time: 255 us; the launch traced here: 254 us
  waiting for transfers between devices  141 us (55%)
  starting transfers between devices  37.3 us (15%)
  local copies, waits for them, and re-layouts  33.3 us (13%)
  matrix products  16.5 us (6%)
  other arithmetic  14.8 us (6%)
  blocking collectives  10.2 us (4%)
    ppermute x4, waiting for transfers between devices, passed_along(): return lax.ppermute(block, axis, route)  119 us
    ppermute x4, starting transfers between devices, passed_along(): return lax.ppermute(block, axis, route)  16.3 us
    all_to_all x1, blocking collectives, local(): lax.all_to_all(grad_key_loc, 'head', split_axis=0, concat_axis=1, tiled=T...  10.2 us
    all_to_all x1, waiting for transfers between devices, local(): lax.all_to_all(queries, 'head', split_axis=1, concat_axis=0, tiled=True)  7.94 us
    another operation x6, local copies, waits for them, and re-layouts, local(): jnp.stack([key_part, value_part])  7.59 us
    slice x4, local copies, waits for them, and re-layouts, unpack(): kv_block[1].reshape(tok_rows, kv_groups, HEAD_SIZE)  7.31 us
    convert_element_type x1, other arithmetic, local(): dscore = (prob * (dprob - delta[..., None])).astype(jnp.bfloat16)  6.79 us
    all_to_all x1, waiting for transfers between devices, local(): lax.all_to_all(value_state_rows, 'head', split_axis=1, concat_axis=0, til...  5.12 us
  transfers between devices with their start and end apart: 10, of which 8 were waited for; matrix products, arithmetic and copies ran while one was open for 11% of the time, Pallas kernels for 0%

commit v1 on v0

--- a/solution.py
+++ b/solution.py
@@ -26,21 +26,35 @@
 
 
 def local(queries, normed_key_state, value_state_rows, output_gradient, doc_start):
-    query_loc, key_loc, value_loc, grad_loc = (
-        lax.all_to_all(queries, "head", split_axis=1, concat_axis=0, tiled=True),
-        lax.all_to_all(normed_key_state, "head", split_axis=1, concat_axis=0, tiled=True),
-        lax.all_to_all(value_state_rows, "head", split_axis=1, concat_axis=0, tiled=True),
-        lax.all_to_all(output_gradient, "head", split_axis=1, concat_axis=0, tiled=True),
+    heads_ax = lax.axis_size("head")
+    rows_in = queries.shape[0]
+    kv_cols = normed_key_state.shape[1] // heads_ax
+    q_cols = queries.shape[1] // heads_ax
+    kv_in = jnp.stack(
+        [
+            normed_key_state.reshape(rows_in, heads_ax, kv_cols),
+            value_state_rows.reshape(rows_in, heads_ax, kv_cols),
+        ],
+        axis=2,
     )
-    tok_rows = query_loc.shape[0]
-    kv_groups = key_loc.shape[1] // HEAD_SIZE
+    kv_all = lax.all_to_all(kv_in, "head", split_axis=1, concat_axis=0, tiled=True)
+    tok_rows = kv_all.shape[0]
+    kv_groups = kv_cols // HEAD_SIZE
     group_share = QUERY_HEADS // KEY_VALUE_HEADS
-    query_heads = query_loc.reshape(tok_rows, kv_groups, group_share, HEAD_SIZE)
-    grad_heads = grad_loc.reshape(tok_rows, kv_groups, group_share, HEAD_SIZE)
-    kv_local = jnp.stack([key_loc, value_loc])
+    kv_local = jnp.moveaxis(kv_all[:, 0], 1, 0)
     kv_blocks = [kv_local]
     for distance in range(1, SPAN + 1):
-        kv_blocks.append(passed_along(kv_local, "ctx", distance))
+        kv_blocks.append(passed_along(kv_blocks[-1], "ctx", 1))
+    qg_in = jnp.stack(
+        [
+            queries.reshape(rows_in, heads_ax, q_cols),
+            output_gradient.reshape(rows_in, heads_ax, q_cols),
+        ],
+        axis=2,
+    )
+    qg_all = lax.all_to_all(qg_in, "head", split_axis=1, concat_axis=0, tiled=True)
+    query_heads = qg_all[:, 0, 0].reshape(tok_rows, kv_groups, group_share, HEAD_SIZE)
+    grad_heads = qg_all[:, 0, 1].reshape(tok_rows, kv_groups, group_share, HEAD_SIZE)
     shard_index = lax.axis_index("ctx")
     local_iota = jnp.arange(tok_rows, dtype=jnp.int32)
     query_pos = shard_index * tok_rows + local_iota
@@ -84,13 +98,9 @@
         )
     log_total = running[0] + jnp.log(running[1])
     delta = running[2] / running[1]
-    zero_parts = (
-        jnp.zeros((tok_rows, kv_groups, group_share, HEAD_SIZE), jnp.float32),
-        jnp.zeros((2, tok_rows, kv_groups * HEAD_SIZE), jnp.float32),
-    )
-    query_total = zero_parts[0]
-    kv_parts = []
-    for distance in range(SPAN + 1):
+    query_total = jnp.zeros((tok_rows, kv_groups, group_share, HEAD_SIZE), jnp.float32)
+    kv_parts = {}
+    for distance in reversed(range(SPAN + 1)):
         key_block, value_block = unpack(kv_blocks[distance])
         masked = jnp.where(masks[distance], pair_scores(query_heads, key_block), -jnp.inf)
         prob = jnp.exp(masked - log_total[..., None])
@@ -108,25 +118,23 @@
         value_part = jnp.einsum(
             "gjtk,tgjd->kgd", prob_half, grad_heads, preferred_element_type=jnp.float32
         )
-        query_part, kv_part = (
-            query_part,
-            jnp.stack([key_part, value_part]).reshape(2, tok_rows, kv_groups * HEAD_SIZE),
+        query_total = query_total + query_part
+        kv_parts[distance] = jnp.stack([key_part, value_part]).reshape(
+            2, tok_rows, kv_groups * HEAD_SIZE
         )
-        query_total = query_total + query_part
-        kv_parts.append(kv_part)
-    kv_total = kv_parts[0]
-    for distance in range(1, SPAN + 1):
-        kv_total = kv_total + passed_along(kv_parts[distance], "ctx", -distance)
+    carried = passed_along(kv_parts[2].astype(jnp.bfloat16), "ctx", -1)
+    carried = passed_along((kv_parts[1] + carried).astype(jnp.bfloat16), "ctx", -1)
+    kv_total = kv_parts[0] + carried
     grad_query_loc = query_total.reshape(tok_rows, kv_groups * group_share * HEAD_SIZE).astype(
         jnp.bfloat16
     )
-    grad_key_loc = kv_total[0].astype(jnp.bfloat16)
-    grad_value_loc = kv_total[1].astype(jnp.bfloat16)
-    return (
-        lax.all_to_all(grad_query_loc, "head", split_axis=0, concat_axis=1, tiled=True),
-        lax.all_to_all(grad_key_loc, "head", split_axis=0, concat_axis=1, tiled=True),
-        lax.all_to_all(grad_value_loc, "head", split_axis=0, concat_axis=1, tiled=True),
-    )
+    grad_q = lax.all_to_all(grad_query_loc, "head", split_axis=0, concat_axis=1, tiled=True)
+    kv_out = jnp.moveaxis(kv_total.astype(jnp.bfloat16), 0, 1)[:, None]
+    kv_back = lax.all_to_all(kv_out, "head", split_axis=0, concat_axis=1, tiled=True)
+    rows_out = kv_back.shape[0]
+    grad_k = kv_back[:, :, 0].reshape(rows_out, heads_ax * kv_cols)
+    grad_v = kv_back[:, :, 1].reshape(rows_out, heads_ax * kv_cols)
+    return grad_q, grad_k, grad_v
 
 
 def solution(mesh):

time: 255 us -> 193 us (0.76)
  the two profiles are of different devices: /device:TPU:54 before, /device:TPU:190 now
where the time goes in v1:
time: 193 us; the launch traced here: 192 us
  waiting for transfers between devices  79.6 us (41%)
  starting transfers between devices  38.6 us (20%)
  local copies, waits for them, and re-layouts  34.5 us (18%)
  matrix products  21.9 us (11%)
  other arithmetic  16.5 us (9%)
    ppermute x4, waiting for transfers between devices, passed_along(): return lax.ppermute(block, axis, route)  66.7 us
    ppermute x4, starting transfers between devices, passed_along(): return lax.ppermute(block, axis, route)  23.8 us
    another operation x6, local copies, waits for them, and re-layouts, local(): jnp.stack([key_part, value_part])  9.45 us
    all_to_all x1, waiting for transfers between devices, local(): lax.all_to_all(kv_out, 'head', split_axis=0, concat_axis=1, tiled=True)  6.9 us
    convert_element_type x1, other arithmetic, local(): dscore = (prob * (dprob - delta[..., None])).astype(jnp.bfloat16)  6.74 us
    slice x6, local copies, waits for them, and re-layouts, unpack(): kv_block[1].reshape(tok_rows, kv_groups, HEAD_SIZE)  6.43 us
    all_to_all x1, waiting for transfers between devices, local(): lax.all_to_all(kv_in, 'head', split_axis=1, concat_axis=0, tiled=True)  6 us
    dot_general x3, matrix products, local(): jnp.einsum('gjtk,tgjd->kgd', dscore, query_heads, preferred_element_type=...  5.38 us
  transfers between devices with their start and end apart: 8, of which 6 were waited for; matrix products, arithmetic and copies ran while one was open for 17% of the time, Pallas kernels for 0%

profile of v1, /device:TPU:190, one launch (start us, length us, event | category | flops | bytes accessed | tf_op | source)
XLA Modules:
  0.0 192.1 jit_solution(15562650888935743916)
XLA Ops:
  0.6 1.2 stack_reshape.12
  1.8 1.1 stack_reshape.13
  4.3 3.6 %all-to-all-start = ((bf16[64,4,2,512]{3,0,2,1:T(8,128)(2,1)}), bf16[64,4,2,512]{3,0,2,1:T(8,128)(2,1)S(1)}, u32[]{:S(2)}, u32[]{:S(2)}) async-start(bf16[64,4,2,512]{3,0,2,1:T(8,128)(2,1)} %copy.105), calls=%async_computation | async-start | bytes 1048576 | tf_op jit(solution)/shard_map/all_to_all | solution.py:40
  9.4 1.3 copy.108
  10.7 6.0 %all-to-all-done = bf16[64,4,2,512]{3,0,2,1:T(8,128)(2,1)S(1)} async-done(((bf16[64,4,2,512]{3,0,2,1:T(8,128)(2,1)}), bf16[64,4,2,512]{3,0,2,1:T(8,128)(2,1)S(1)}, u32[]{:S(2)}, u32[]{:S(2)}) %all-to-all-start) | async-done | bytes 524320 | tf_op jit(solution)/shard_map/all_to_all | solution.py:40
  16.7 3.5 %all-to-all-start.1 = ((bf16[64,4,2,1024]{3,0,2,1:T(8,128)(2,1)}), bf16[64,4,2,1024]{3,0,2,1:T(8,128)(2,1)S(1)}, u32[]{:S(2)}, u32[]{:S(2)}) async-start(bf16[64,4,2,1024]{3,0,2,1:T(8,128)(2,1)} %copy.108), calls=%async_computation.1 | async-start | bytes 2097152 | tf_op jit(solution)/shard_map/all_to_all | solution.py:55
  20.3 6.2 %collective-permute-start = (bf16[2,256,512]{2,1,0:T(8,128)(2,1)S(1)}, bf16[2,256,512]{2,1,0:T(8,128)(2,1)}, u32[]{:S(2)}, u32[]{:S(2)}) collective-permute-start(bf16[2,256,512]{2,1,0:T(8,128)(2,1)S(1)} %bitcast.205), channel_id=1, source_target_pairs={{0,4},{4,8},{8,12},{12,16},{16,20},{20,24},{24,28},{28,32},{32,36}... | collective-permute-start | bytes 1572872 | tf_op jit(solution)/shard_map/ppermute | solution.py:19
  27.9 19.2 %collective-permute-done = bf16[2,256,512]{2,1,0:T(8,128)(2,1)} collective-permute-done((bf16[2,256,512]{2,1,0:T(8,128)(2,1)S(1)}, bf16[2,256,512]{2,1,0:T(8,128)(2,1)}, u32[]{:S(2)}, u32[]{:S(2)}) %collective-permute-start) | collective-permute-done | bytes 524320 | tf_op jit(solution)/shard_map/ppermute | solution.py:19
  47.1 1.1 fusion.41
  49.2 13.5 %collective-permute-start.1 = (bf16[2,256,512]{2,1,0:T(8,128)(2,1)}, bf16[2,256,512]{2,1,0:T(8,128)(2,1)}, u32[]{:S(2)}, u32[]{:S(2)}) collective-permute-start(bf16[2,256,512]{2,1,0:T(8,128)(2,1)} %collective-permute-done), channel_id=1, source_target_pairs={{0,4},{4,8},{8,12},{12,16},{16,20},{20,24},{24,28},{28,32},{32,36}... | collective-permute-start | bytes 1572872 | tf_op jit(solution)/shard_map/ppermute | solution.py:19
  63.3 1.8 fusion.46
  66.1 1.9 fusion.3
  68.0 14.3 %collective-permute-done.1 = bf16[2,256,512]{2,1,0:T(8,128)(2,1)} collective-permute-done((bf16[2,256,512]{2,1,0:T(8,128)(2,1)}, bf16[2,256,512]{2,1,0:T(8,128)(2,1)}, u32[]{:S(2)}, u32[]{:S(2)}) %collective-permute-start.1) | collective-permute-done | bytes 524320 | tf_op jit(solution)/shard_map/ppermute | solution.py:19
  82.2 1.9 fusion.42
  84.1 1.8 copy.119
  85.9 1.8 copy.107
  87.7 1.5 fusion.44
  89.2 1.9 fusion.6
  91.1 1.2 copy-done
  92.3 1.9 fusion
  94.2 1.2 fusion.23
  95.4 1.3 fusion.26
  96.7 2.0 %copy.141 = f32[1,256,512]{2,0,1:T(1,128)} copy(f32[1,256,512]{1,2,0:T(8,128)} %bitcast.211) | data formatting | bytes 1048576 | tf_op jit(solution)/shard_map/stack | solution.py:122
  98.7 2.0 %copy.145 = bf16[1,256,512]{2,0,1:T(2,128)(2,1)} copy(bf16[1,256,512]{1,2,0:T(8,128)(2,1)} %bitcast.218) | data formatting | bytes 524288 | tf_op jit(solution)/shard_map/stack | solution.py:122
  100.7 6.7 %fusion.8 = (bf16[4,2,256,256]{2,3,1,0:T(8,128)(2,1)S(1)}, bf16[4,2,256,256]{2,3,1,0:T(8,128)(2,1)}, bf16[4,2,256,256]{2,3,1,0:T(8,128)(2,1)}) fusion(f32[4,256,256,2]{2,1,3,0:T(8,128)} %get-tuple-element.35, f32[4,2,256,256]{2,3,1,0:T(8,128)} %copy-done.1, f32[4,2,256]{2,1,0:T(2,128)S(1)} %add_divide_fusion, f32[4,2,256]{2,1,0:T(2,128)S(1)} %get-tuple-element.9, ...), kind=kLoop, calls=%fused_computation.14 | loop fusion | flops 6291456 | bytes 15745024 | tf_op jit(solution)/shard_map/convert_element_type | solution.py:110
  107.4 1.0 copy-done.3
  108.4 1.2 fusion.22
  109.6 2.0 %copy.144 = bf16[1,256,512]{2,0,1:T(2,128)(2,1)} copy(bf16[1,256,512]{1,2,0:T(8,128)(2,1)} %bitcast.212) | data formatting | bytes 524288 | tf_op jit(solution)/shard_map/stack | solution.py:122
  111.5 1.8 fusion.47
  113.7 2.0 %pad_maximum_fusion.2 = bf16[2,256,512]{2,0,1:T(2,128)(2,1)} fusion(bf16[1,256,512]{2,0,1:T(2,128)(2,1)S(1)} %copy-done.7, bf16[1,256,512]{2,0,1:T(2,128)(2,1)S(1)} %copy-done.8), kind=kLoop, calls=%fused_computation.55 | loop fusion | flops 1048576 | bytes 1048576 | tf_op jit(solution)/shard_map/stack | solution.py:122
  115.7 1.9 collective-permute-start.2
  117.6 1.1 fusion.18
  118.7 2.0 %copy.132 = bf16[256,4,2,128]{3,2,1,0:T(2,128)(2,1)} copy(bf16[256,4,2,128]{0,3,2,1:T(8,128)(2,1)} %fusion.18) | data formatting | bytes 1048576 | tf_op jit(solution)/shard_map/convert_element_type | solution.py:128
  120.7 2.2 %convert_element_type.46 = bf16[4,64,1024]{2,1,0:T(8,128)(2,1)} reshape(bf16[256,4,2,128]{3,2,1,0:T(2,128)(2,1)} %copy.132) | data formatting | bytes 1048576 | tf_op jit(solution)/shard_map/convert_element_type | solution.py:128
  122.9 2.5 %fusion.20 = f32[4,128,256]{2,1,0:T(8,128)} fusion(bf16[256,4,2,128]{0,3,2,1:T(8,128)(2,1)S(1)} %bitcast.196, bf16[4,2,256,256]{2,3,1,0:T(8,128)(2,1)} %get-tuple-element.24), kind=kOutput, calls=%fused_computation.39 | convolution fusion | flops 134348800 | bytes 2097152 | tf_op jit(solution)/shard_map/gjtk,tgjd->kgd/dot_general | solution.py:115
  125.4 1.9 %copy.140 = f32[1,256,512]{2,0,1:T(1,128)} copy(f32[1,256,512]{1,2,0:T(8,128)} %bitcast.210) | data formatting | bytes 1048576 | tf_op jit(solution)/shard_map/stack | solution.py:122
  127.4 4.1 %all-to-all-start.2 = ((bf16[4,64,1024]{2,1,0:T(8,128)(2,1)}), bf16[4,64,1024]{2,1,0:T(8,128)(2,1)}, u32[]{:S(2)}, u32[]{:S(2)}) async-start(bf16[4,64,1024]{2,1,0:T(8,128)(2,1)} %convert_element_type.46), calls=%async_computation.2 | async-start | bytes 1048576 | tf_op jit(solution)/shard_map/all_to_all | solution.py:131
  131.5 16.8 %collective-permute-done.2 = bf16[2,256,512]{2,0,1:T(2,128)(2,1)} collective-permute-done((bf16[2,256,512]{2,0,1:T(2,128)(2,1)}, bf16[2,256,512]{2,0,1:T(2,128)(2,1)}, u32[]{:S(2)}, u32[]{:S(2)}) %collective-permute-start.2) | collective-permute-done | bytes 524320 | tf_op jit(solution)/shard_map/ppermute | solution.py:19
  148.3 3.3 %fusion.30 = bf16[2,256,512]{2,0,1:T(2,128)(2,1)} fusion(f32[1,256,512]{2,0,1:T(1,128)} %copy.141, f32[1,256,512]{2,0,1:T(1,128)} %copy.140, bf16[2,256,512]{2,0,1:T(2,128)(2,1)} %collective-permute-done.2), kind=kLoop, calls=%fused_computation.50 | loop fusion | flops 1048576 | bytes 2097152 | tf_op jit(solution)/shard_map/convert_element_type | solution.py:126
  151.6 2.1 %collective-permute-start.3 = (bf16[2,256,512]{2,0,1:T(2,128)(2,1)}, bf16[2,256,512]{2,0,1:T(2,128)(2,1)}, u32[]{:S(2)}, u32[]{:S(2)}) collective-permute-start(bf16[2,256,512]{2,0,1:T(2,128)(2,1)} %fusion.30), channel_id=1, source_target_pairs={{4,0},{8,4},{12,8},{16,12},{20,16},{24,20},{28,24},{32,28},{36,32}... | collective-permute-start | bytes 1572872 | tf_op jit(solution)/shard_map/ppermute | solution.py:19
  153.7 1.3 fusion.24
  155.0 1.3 copy.137
  156.3 1.7 fusion.21
  158.4 16.5 %collective-permute-done.3 = bf16[2,256,512]{2,0,1:T(2,128)(2,1)} collective-permute-done((bf16[2,256,512]{2,0,1:T(2,128)(2,1)}, bf16[2,256,512]{2,0,1:T(2,128)(2,1)}, u32[]{:S(2)}, u32[]{:S(2)}) %collective-permute-start.3) | collective-permute-done | bytes 524320 | tf_op jit(solution)/shard_map/ppermute | solution.py:19
  174.8 3.0 %fusion.34 = bf16[256,1,2,512]{3,2,1,0:T(2,128)(2,1)} fusion(bf16[2,256,512]{2,0,1:T(2,128)(2,1)} %collective-permute-done.3, f32[1,256,512]{2,0,1:T(1,128)S(1)} %copy.137, f32[1,256,512]{2,0,1:T(1,128)S(1)} %copy.136), kind=kLoop, calls=%fused_computation.56 | loop fusion | flops 1048576 | bytes 2097152 | tf_op jit(solution)/shard_map/broadcast_in_dim | solution.py:132
  177.8 3.5 %all-to-all-start.3 = ((bf16[256,1,2,512]{3,2,1,0:T(2,128)(2,1)}), bf16[256,1,2,512]{3,2,1,0:T(2,128)(2,1)S(1)}, u32[]{:S(2)}, u32[]{:S(2)}) async-start(bf16[256,1,2,512]{3,2,1,0:T(2,128)(2,1)} %fusion.34), calls=%async_computation.3 | async-start | bytes 1048576 | tf_op jit(solution)/shard_map/all_to_all | solution.py:133
  181.3 1.9 copy.191
  183.2 6.9 %all-to-all-done.3 = bf16[256,1,2,512]{3,2,1,0:T(2,128)(2,1)S(1)} async-done(((bf16[256,1,2,512]{3,2,1,0:T(2,128)(2,1)}), bf16[256,1,2,512]{3,2,1,0:T(2,128)(2,1)S(1)}, u32[]{:S(2)}, u32[]{:S(2)}) %all-to-all-start.3) | async-done | bytes 524320 | tf_op jit(solution)/shard_map/all_to_all | solution.py:133
  (60 shorter events, 9.4 us)
Async XLA Ops:
  0.6 7.3 %copy-start.12 = (bf16[64,4096]{1,0:T(8,128)(2,1)S(1)}, bf16[64,4096]{1,0:T(8,128)(2,1)}, u32[]{:S(2)}) copy-start(bf16[64,4096]{1,0:T(8,128)(2,1)} %param.5) | copy-start | bytes 1572868
  3.0 5.3 %copy-start.13 = (bf16[64,4096]{1,0:T(8,128)(2,1)S(1)}, bf16[64,4096]{1,0:T(8,128)(2,1)}, u32[]{:S(2)}) copy-start(bf16[64,4096]{1,0:T(8,128)(2,1)} %param.8) | copy-start | bytes 1572868
  4.3 12.5 %all-to-all-start = ((bf16[64,4,2,512]{3,0,2,1:T(8,128)(2,1)}), bf16[64,4,2,512]{3,0,2,1:T(8,128)(2,1)S(1)}, u32[]{:S(2)}, u32[]{:S(2)}) async-start(bf16[64,4,2,512]{3,0,2,1:T(8,128)(2,1)} %copy.105), calls=%async_computation | async-start | bytes 1048576 | tf_op jit(solution)/shard_map/all_to_all | solution.py:40
  10.7 15.8 %copy-start.14 = (s32[256]{0:T(256)S(1)}, s32[256]{0:T(256)}, u32[]{:S(2)}) copy-start(s32[256]{0:T(256)} %param.9) | copy-start | bytes 3076
  16.7 46.0 %all-to-all-start.1 = ((bf16[64,4,2,1024]{3,0,2,1:T(8,128)(2,1)}), bf16[64,4,2,1024]{3,0,2,1:T(8,128)(2,1)S(1)}, u32[]{:S(2)}, u32[]{:S(2)}) async-start(bf16[64,4,2,1024]{3,0,2,1:T(8,128)(2,1)} %copy.108), calls=%async_computation.1 | async-start | bytes 2097152 | tf_op jit(solution)/shard_map/all_to_all | solution.py:55
  20.3 26.8 %collective-permute-start = (bf16[2,256,512]{2,1,0:T(8,128)(2,1)S(1)}, bf16[2,256,512]{2,1,0:T(8,128)(2,1)}, u32[]{:S(2)}, u32[]{:S(2)}) collective-permute-start(bf16[2,256,512]{2,1,0:T(8,128)(2,1)S(1)} %bitcast.205), channel_id=1, source_target_pairs={{0,4},{4,8},{8,12},{12,16},{16,20},{20,24},{24,28},{28,32},{32,36}... | collective-permute-start | bytes 1572872 | tf_op jit(solution)/shard_map/ppermute | solution.py:19
  49.2 14.1 %copy-start.5 = (bf16[1,256,512]{1,2,0:T(8,128)(2,1)}, bf16[1,256,512]{1,2,0:T(8,128)(2,1)S(1)}, u32[]{:S(2)}) copy-start(bf16[1,256,512]{1,2,0:T(8,128)(2,1)S(1)} %copy.116) | copy-start | bytes 786436
  49.2 33.0 %collective-permute-start.1 = (bf16[2,256,512]{2,1,0:T(8,128)(2,1)}, bf16[2,256,512]{2,1,0:T(8,128)(2,1)}, u32[]{:S(2)}, u32[]{:S(2)}) collective-permute-start(bf16[2,256,512]{2,1,0:T(8,128)(2,1)} %collective-permute-done), channel_id=1, source_target_pairs={{0,4},{4,8},{8,12},{12,16},{16,20},{20,24},{24,28},{28,32},{32,36}... | collective-permute-start | bytes 1572872 | tf_op jit(solution)/shard_map/ppermute | solution.py:19
  65.1 0.9 copy-start.10
  87.7 1.5 copy-start.11
  89.2 5.1 %copy-start.1 = (f32[4,2,256,256]{2,3,1,0:T(8,128)}, f32[4,2,256,256]{2,3,1,0:T(8,128)S(1)}, u32[]{:S(2)}) copy-start(f32[4,2,256,256]{2,3,1,0:T(8,128)S(1)} %get-tuple-element.30) | copy-start | bytes 6291460
  89.2 3.1 %copy-start = (f32[4,2,256,256]{2,3,1,0:T(8,128)S(1)}, f32[4,2,256,256]{2,3,1,0:T(8,128)}, u32[]{:S(2)}) copy-start(f32[4,2,256,256]{2,3,1,0:T(8,128)} %get-tuple-element.34) | copy-start | bytes 6291460
  89.2 3.1 %copy-start.9 = (bf16[1,256,512]{1,2,0:T(8,128)(2,1)S(1)}, bf16[1,256,512]{1,2,0:T(8,128)(2,1)}, u32[]{:S(2)}) copy-start(bf16[1,256,512]{1,2,0:T(8,128)(2,1)} %copy.126) | copy-start | bytes 786436
  107.4 1.0 copy-start.3
  111.5 1.8 copy-start.2
  111.5 2.1 %copy-start.7 = (bf16[1,256,512]{2,0,1:T(2,128)(2,1)S(1)}, bf16[1,256,512]{2,0,1:T(2,128)(2,1)}, u32[]{:S(2)}) copy-start(bf16[1,256,512]{2,0,1:T(2,128)(2,1)} %copy.145) | copy-start | bytes 786436
  111.5 2.1 %copy-start.8 = (bf16[1,256,512]{2,0,1:T(2,128)(2,1)S(1)}, bf16[1,256,512]{2,0,1:T(2,128)(2,1)}, u32[]{:S(2)}) copy-start(bf16[1,256,512]{2,0,1:T(2,128)(2,1)} %copy.144) | copy-start | bytes 786436
  113.3 4.3 %copy-start.4 = (bf16[4,2,256,256]{2,3,1,0:T(8,128)(2,1)S(1)}, bf16[4,2,256,256]{2,3,1,0:T(8,128)(2,1)}, u32[]{:S(2)}) copy-start(bf16[4,2,256,256]{2,3,1,0:T(8,128)(2,1)} %copy-done.3) | copy-start | bytes 3145732
  113.3 4.3 %copy-start.6 = (bf16[1,256,512]{1,2,0:T(8,128)(2,1)S(1)}, bf16[1,256,512]{1,2,0:T(8,128)(2,1)}, u32[]{:S(2)}) copy-start(bf16[1,256,512]{1,2,0:T(8,128)(2,1)} %copy.107) | copy-start | bytes 786436
  115.7 32.6 %collective-permute-start.2 = (bf16[2,256,512]{2,0,1:T(2,128)(2,1)}, bf16[2,256,512]{2,0,1:T(2,128)(2,1)}, u32[]{:S(2)}, u32[]{:S(2)}) collective-permute-start(bf16[2,256,512]{2,0,1:T(2,128)(2,1)} %pad_maximum_fusion.2), channel_id=1, source_target_pairs={{4,0},{8,4},{12,8},{16,12},{20,16},{24,20},{28,24},{32,28},{36,32}... | collective-permute-start | bytes 1572872 | tf_op jit(solution)/shard_map/ppermute | solution.py:19
  127.4 50.5 %all-to-all-start.2 = ((bf16[4,64,1024]{2,1,0:T(8,128)(2,1)}), bf16[4,64,1024]{2,1,0:T(8,128)(2,1)}, u32[]{:S(2)}, u32[]{:S(2)}) async-start(bf16[4,64,1024]{2,1,0:T(8,128)(2,1)} %convert_element_type.46), calls=%async_computation.2 | async-start | bytes 1048576 | tf_op jit(solution)/shard_map/all_to_all | solution.py:131
  151.6 23.3 %collective-permute-start.3 = (bf16[2,256,512]{2,0,1:T(2,128)(2,1)}, bf16[2,256,512]{2,0,1:T(2,128)(2,1)}, u32[]{:S(2)}, u32[]{:S(2)}) collective-permute-start(bf16[2,256,512]{2,0,1:T(2,128)(2,1)} %fusion.30), channel_id=1, source_target_pairs={{4,0},{8,4},{12,8},{16,12},{20,16},{24,20},{28,24},{32,28},{36,32}... | collective-permute-start | bytes 1572872 | tf_op jit(solution)/shard_map/ppermute | solution.py:19
  177.8 12.3 %all-to-all-start.3 = ((bf16[256,1,2,512]{3,2,1,0:T(2,128)(2,1)}), bf16[256,1,2,512]{3,2,1,0:T(2,128)(2,1)S(1)}, u32[]{:S(2)}, u32[]{:S(2)}) async-start(bf16[256,1,2,512]{3,2,1,0:T(2,128)(2,1)} %fusion.34), calls=%async_computation.3 | async-start | bytes 1048576 | tf_op jit(solution)/shard_map/all_to_all | solution.py:133

commit v2 on v1

--- a/solution.py
+++ b/solution.py
@@ -8,6 +8,8 @@
 HEAD_SIZE = 128
 WINDOW = 512
 SPAN = 2
+CHUNKS = 2
+CHAIN = False
 
 
 score_scale = 168.0 ** (-0.5)
@@ -25,33 +27,19 @@
     )
 
 
-def local(queries, normed_key_state, value_state_rows, output_gradient, doc_start):
-    heads_ax = lax.axis_size("head")
-    rows_in = queries.shape[0]
-    kv_cols = normed_key_state.shape[1] // heads_ax
-    q_cols = queries.shape[1] // heads_ax
-    kv_in = jnp.stack(
-        [
-            normed_key_state.reshape(rows_in, heads_ax, kv_cols),
-            value_state_rows.reshape(rows_in, heads_ax, kv_cols),
-        ],
-        axis=2,
-    )
+def attend_chunk(kv_in, qg_in, doc_start):
     kv_all = lax.all_to_all(kv_in, "head", split_axis=1, concat_axis=0, tiled=True)
     tok_rows = kv_all.shape[0]
+    kv_cols = kv_all.shape[-1]
     kv_groups = kv_cols // HEAD_SIZE
     group_share = QUERY_HEADS // KEY_VALUE_HEADS
     kv_local = jnp.moveaxis(kv_all[:, 0], 1, 0)
     kv_blocks = [kv_local]
     for distance in range(1, SPAN + 1):
-        kv_blocks.append(passed_along(kv_blocks[-1], "ctx", 1))
-    qg_in = jnp.stack(
-        [
-            queries.reshape(rows_in, heads_ax, q_cols),
-            output_gradient.reshape(rows_in, heads_ax, q_cols),
-        ],
-        axis=2,
-    )
+        if CHAIN:
+            kv_blocks.append(passed_along(kv_blocks[-1], "ctx", 1))
+        else:
+            kv_blocks.append(passed_along(kv_local, "ctx", distance))
     qg_all = lax.all_to_all(qg_in, "head", split_axis=1, concat_axis=0, tiled=True)
     query_heads = qg_all[:, 0, 0].reshape(tok_rows, kv_groups, group_share, HEAD_SIZE)
     grad_heads = qg_all[:, 0, 1].reshape(tok_rows, kv_groups, group_share, HEAD_SIZE)
@@ -119,21 +107,46 @@
             "gjtk,tgjd->kgd", prob_half, grad_heads, preferred_element_type=jnp.float32
         )
         query_total = query_total + query_part
-        kv_parts[distance] = jnp.stack([key_part, value_part]).reshape(
-            2, tok_rows, kv_groups * HEAD_SIZE
-        )
-    carried = passed_along(kv_parts[2].astype(jnp.bfloat16), "ctx", -1)
-    carried = passed_along((kv_parts[1] + carried).astype(jnp.bfloat16), "ctx", -1)
-    kv_total = kv_parts[0] + carried
-    grad_query_loc = query_total.reshape(tok_rows, kv_groups * group_share * HEAD_SIZE).astype(
-        jnp.bfloat16
+        kv_parts[distance] = jnp.stack([key_part, value_part]).reshape(2, tok_rows, kv_cols)
+    if CHAIN:
+        carried = passed_along(kv_parts[2].astype(jnp.bfloat16), "ctx", -1)
+        carried = passed_along((kv_parts[1] + carried).astype(jnp.bfloat16), "ctx", -1)
+        kv_total = kv_parts[0] + carried
+    else:
+        kv_total = kv_parts[0]
+        for distance in range(1, SPAN + 1):
+            kv_total = kv_total + passed_along(
+                kv_parts[distance].astype(jnp.bfloat16), "ctx", -distance
+            )
+    grad_query_loc = query_total.reshape(tok_rows, 1, kv_groups * group_share * HEAD_SIZE)
+    grad_q = lax.all_to_all(
+        grad_query_loc.astype(jnp.bfloat16), "head", split_axis=0, concat_axis=1, tiled=True
     )
-    grad_q = lax.all_to_all(grad_query_loc, "head", split_axis=0, concat_axis=1, tiled=True)
     kv_out = jnp.moveaxis(kv_total.astype(jnp.bfloat16), 0, 1)[:, None]
     kv_back = lax.all_to_all(kv_out, "head", split_axis=0, concat_axis=1, tiled=True)
-    rows_out = kv_back.shape[0]
-    grad_k = kv_back[:, :, 0].reshape(rows_out, heads_ax * kv_cols)
-    grad_v = kv_back[:, :, 1].reshape(rows_out, heads_ax * kv_cols)
+    return grad_q, kv_back
+
+
+def local(queries, normed_key_state, value_state_rows, output_gradient, doc_start):
+    heads_ax = lax.axis_size("head")
+    rows_in = queries.shape[0]
+    kv_cols = normed_key_state.shape[1] // (heads_ax * CHUNKS)
+    q_cols = queries.shape[1] // (heads_ax * CHUNKS)
+    keys = normed_key_state.reshape(rows_in, heads_ax, CHUNKS, kv_cols)
+    values = value_state_rows.reshape(rows_in, heads_ax, CHUNKS, kv_cols)
+    qs = queries.reshape(rows_in, heads_ax, CHUNKS, q_cols)
+    gs = output_gradient.reshape(rows_in, heads_ax, CHUNKS, q_cols)
+    dq_parts, dkv_parts = [], []
+    for chunk in range(CHUNKS):
+        kv_in = jnp.stack([keys[:, :, chunk], values[:, :, chunk]], axis=2)
+        qg_in = jnp.stack([qs[:, :, chunk], gs[:, :, chunk]], axis=2)
+        dq, dkv = attend_chunk(kv_in, qg_in, doc_start)
+        dq_parts.append(dq)
+        dkv_parts.append(dkv)
+    grad_q = jnp.stack(dq_parts, axis=2).reshape(rows_in, heads_ax * CHUNKS * q_cols)
+    dkv = jnp.stack(dkv_parts, axis=3)
+    grad_k = dkv[:, :, 0].reshape(rows_in, heads_ax * CHUNKS * kv_cols)
+    grad_v = dkv[:, :, 1].reshape(rows_in, heads_ax * CHUNKS * kv_cols)
     return grad_q, grad_k, grad_v
 
 

time: 193 us -> 212 us (1.098)
  the two profiles are of different devices: /device:TPU:190 before, /device:TPU:184 now
where the time goes in v2:
time: 212 us; the launch traced here: 211 us
  starting transfers between devices  79.9 us (38%)
  local copies, waits for them, and re-layouts  43.9 us (21%)
  waiting for transfers between devices  36.4 us (17%)
  matrix products  27.9 us (13%)
  other arithmetic  21 us (10%)
    ppermute x8, starting transfers between devices, passed_along(): return lax.ppermute(block, axis, route)  51.8 us
    ppermute x8, waiting for transfers between devices, passed_along(): return lax.ppermute(block, axis, route)  15.7 us
    all_to_all x2, waiting for transfers between devices, attend_chunk(): lax.all_to_all(grad_query_loc.astype(jnp.bfloat16), 'head', split_axis=0,...  14.2 us
    another operation x12, local copies, waits for them, and re-layouts, attend_chunk(): jnp.stack([key_part, value_part]).reshape(2, tok_rows, kv_cols)  10.3 us
    unnamed x116, local copies, waits for them, and re-layouts  10.1 us
    all_to_all x2, starting transfers between devices, attend_chunk(): lax.all_to_all(qg_in, 'head', split_axis=1, concat_axis=0, tiled=True)  7.13 us
    all_to_all x2, starting transfers between devices, attend_chunk(): lax.all_to_all(kv_in, 'head', split_axis=1, concat_axis=0, tiled=True)  7.07 us
    all_to_all x2, starting transfers between devices, attend_chunk(): lax.all_to_all(grad_query_loc.astype(jnp.bfloat16), 'head', split_axis=0,...  7.05 us
  transfers between devices with their start and end apart: 16, of which 7 were waited for; matrix products, arithmetic and copies ran while one was open for 27% of the time, Pallas kernels for 0%

profile of v2, /device:TPU:184, one launch (start us, length us, event | category | flops | bytes accessed | tf_op | source)
XLA Modules:
  0.0 210.7 jit_solution(13500736151918691449)
XLA Ops:
  0.6 1.2 reshape.236
  4.3 3.6 %all-to-all-start = ((bf16[64,4,2,256]{3,2,0,1:T(2,128)(2,1)}), bf16[64,4,2,256]{3,2,0,1:T(2,128)(2,1)S(1)}, u32[]{:S(2)}, u32[]{:S(2)}) async-start(bf16[64,4,2,256]{3,2,0,1:T(2,128)(2,1)} %copy.203), calls=%async_computation | async-start | bytes 524288 | tf_op jit(solution)/shard_map/all_to_all | solution.py:31
  9.3 1.5 fusion.71
  10.8 1.2 pad_maximum_fusion
  12.0 1.2 pad_maximum_fusion.1
  13.3 1.2 copy.206
  17.1 3.4 %all-to-all-start.3 = ((bf16[64,4,2,256]{3,2,0,1:T(2,128)(2,1)}), bf16[64,4,2,256]{3,2,0,1:T(2,128)(2,1)S(1)}, u32[]{:S(2)}, u32[]{:S(2)}) async-start(bf16[64,4,2,256]{3,2,0,1:T(2,128)(2,1)} %copy.231), calls=%async_computation.3 | async-start | bytes 524288 | tf_op jit(solution)/shard_map/all_to_all | solution.py:31
  22.1 3.6 %collective-permute-start = (bf16[2,256,256]{2,1,0:T(8,128)(2,1)S(1)}, bf16[2,256,256]{2,1,0:T(8,128)(2,1)S(1)}, u32[]{:S(2)}, u32[]{:S(2)}) collective-permute-start(bf16[2,256,256]{2,1,0:T(8,128)(2,1)S(1)} %bitcast.375), channel_id=1, source_target_pairs={{0,8},{4,12},{8,16},{12,20},{16,24},{20,28},{24,32},{28,36},{32,40... | collective-permute-start | bytes 786440 | tf_op jit(solution)/shard_map/ppermute | solution.py:21
  25.8 3.5 %collective-permute-start.1 = (bf16[2,256,256]{2,1,0:T(8,128)(2,1)S(1)}, bf16[2,256,256]{2,1,0:T(8,128)(2,1)S(1)}, u32[]{:S(2)}, u32[]{:S(2)}) collective-permute-start(bf16[2,256,256]{2,1,0:T(8,128)(2,1)S(1)} %bitcast.377), channel_id=1, source_target_pairs={{0,4},{4,8},{8,12},{12,16},{16,20},{20,24},{24,28},{28,32},{32,36}... | collective-permute-start | bytes 786440 | tf_op jit(solution)/shard_map/ppermute | solution.py:21
  29.3 3.5 %all-to-all-start.1 = ((bf16[64,4,2,512]{3,2,0,1:T(2,128)(2,1)}), bf16[64,4,2,512]{3,2,0,1:T(2,128)(2,1)S(1)}, u32[]{:S(2)}, u32[]{:S(2)}) async-start(bf16[64,4,2,512]{3,2,0,1:T(2,128)(2,1)} %copy.206), calls=%async_computation.1 | async-start | bytes 1048576 | tf_op jit(solution)/shard_map/all_to_all | solution.py:43
  32.8 3.5 %collective-permute-start.3 = (bf16[2,256,256]{2,1,0:T(8,128)(2,1)S(1)}, bf16[2,256,256]{2,1,0:T(8,128)(2,1)S(1)}, u32[]{:S(2)}, u32[]{:S(2)}) collective-permute-start(bf16[2,256,256]{2,1,0:T(8,128)(2,1)S(1)} %bitcast.373), channel_id=1, source_target_pairs={{0,4},{4,8},{8,12},{12,16},{16,20},{20,24},{24,28},{28,32},{32,36}... | collective-permute-start | bytes 786440 | tf_op jit(solution)/shard_map/ppermute | solution.py:21
  36.3 4.8 %collective-permute-start.2 = (bf16[2,256,256]{2,1,0:T(8,128)(2,1)S(1)}, bf16[2,256,256]{2,1,0:T(8,128)(2,1)S(1)}, u32[]{:S(2)}, u32[]{:S(2)}) collective-permute-start(bf16[2,256,256]{2,1,0:T(8,128)(2,1)S(1)} %bitcast.374), channel_id=1, source_target_pairs={{0,8},{4,12},{8,16},{12,20},{16,24},{20,28},{24,32},{28,36},{32,40... | collective-permute-start | bytes 786440 | tf_op jit(solution)/shard_map/ppermute | solution.py:21
  42.9 1.6 collective-permute-done.1
  47.0 3.4 %collective-permute-done.3 = bf16[2,256,256]{2,1,0:T(8,128)(2,1)S(1)} collective-permute-done((bf16[2,256,256]{2,1,0:T(8,128)(2,1)S(1)}, bf16[2,256,256]{2,1,0:T(8,128)(2,1)S(1)}, u32[]{:S(2)}, u32[]{:S(2)}) %collective-permute-start.3) | collective-permute-done | bytes 262176 | tf_op jit(solution)/shard_map/ppermute | solution.py:21
  51.1 10.6 %collective-permute-done.2 = bf16[2,256,256]{2,1,0:T(8,128)(2,1)S(1)} collective-permute-done((bf16[2,256,256]{2,1,0:T(8,128)(2,1)S(1)}, bf16[2,256,256]{2,1,0:T(8,128)(2,1)S(1)}, u32[]{:S(2)}, u32[]{:S(2)}) %collective-permute-start.2) | collective-permute-done | bytes 262176 | tf_op jit(solution)/shard_map/ppermute | solution.py:21
  64.0 3.7 %all-to-all-start.4 = ((bf16[64,4,2,512]{3,2,0,1:T(2,128)(2,1)}), bf16[64,4,2,512]{3,2,0,1:T(2,128)(2,1)S(1)}, u32[]{:S(2)}, u32[]{:S(2)}) async-start(bf16[64,4,2,512]{3,2,0,1:T(2,128)(2,1)} %copy.234), calls=%async_computation.4 | async-start | bytes 1048576 | tf_op jit(solution)/shard_map/all_to_all | solution.py:43
  70.8 1.9 multiply_reduce_fusion.5
  72.7 1.9 multiply_reduce_fusion.4
  74.6 1.9 multiply_reduce_fusion.3
  81.1 1.2 fusion.83
  82.4 1.3 fusion.84
  83.8 1.9 fusion.82
  85.7 1.8 copy.246
  88.2 1.5 multiply_reduce_fusion.2
  94.1 1.4 multiply_convert_fusion.5
  103.5 1.3 pad_maximum_fusion.6
  104.8 2.0 collective-permute-start.4
  110.0 1.3 pad_maximum_fusion.7
  111.3 6.5 %collective-permute-start.5 = (bf16[2,256,256]{2,0,1:T(2,128)(2,1)}, bf16[2,256,256]{2,0,1:T(2,128)(2,1)}, u32[]{:S(2)}, u32[]{:S(2)}) collective-permute-start(bf16[2,256,256]{2,0,1:T(2,128)(2,1)} %pad_maximum_fusion.7), channel_id=1, source_target_pairs={{8,0},{12,4},{16,8},{20,12},{24,16},{28,20},{32,24},{36,28},{40,32... | collective-permute-start | bytes 786440 | tf_op jit(solution)/shard_map/ppermute | solution.py:21
  117.9 1.8 copy.262
  121.0 1.3 pad_maximum_fusion.8
  122.3 2.1 %collective-permute-start.6 = (bf16[2,256,256]{2,0,1:T(2,128)(2,1)}, bf16[2,256,256]{2,0,1:T(2,128)(2,1)}, u32[]{:S(2)}, u32[]{:S(2)}) collective-permute-start(bf16[2,256,256]{2,0,1:T(2,128)(2,1)} %pad_maximum_fusion.8), channel_id=1, source_target_pairs={{4,0},{8,4},{12,8},{16,12},{20,16},{24,20},{28,24},{32,28},{36,32}... | collective-permute-start | bytes 786440 | tf_op jit(solution)/shard_map/ppermute | solution.py:21
  124.4 1.8 copy.285
  127.1 1.8 copy.284
  128.9 2.3 %pad_maximum_fusion.9 = bf16[2,256,256]{2,0,1:T(2,128)(2,1)} fusion(bf16[1,256,256]{2,0,1:T(2,128)(2,1)} %copy.285, bf16[1,256,256]{2,0,1:T(2,128)(2,1)} %copy.284), kind=kLoop, calls=%fused_computation.118 | loop fusion | flops 524288 | bytes 524288 | tf_op jit(solution)/shard_map/stack | solution.py:110
  131.3 25.7 %collective-permute-start.7 = (bf16[2,256,256]{2,0,1:T(2,128)(2,1)}, bf16[2,256,256]{2,0,1:T(2,128)(2,1)}, u32[]{:S(2)}, u32[]{:S(2)}) collective-permute-start(bf16[2,256,256]{2,0,1:T(2,128)(2,1)} %pad_maximum_fusion.9), channel_id=1, source_target_pairs={{8,0},{12,4},{16,8},{20,12},{24,16},{28,20},{32,24},{36,28},{40,32... | collective-permute-start | bytes 786440 | tf_op jit(solution)/shard_map/ppermute | solution.py:21
  158.6 1.7 reduce.1
  161.3 3.6 %all-to-all-start.2 = ((bf16[4,2,16384]{2,1,0:T(2,128)(2,1)}), bf16[4,2,16384]{2,1,0:T(2,128)(2,1)S(1)}, u32[]{:S(2)}, u32[]{:S(2)}) async-start(bf16[4,2,16384]{2,1,0:T(2,128)(2,1)} %reshape.273), calls=%async_computation.2 | async-start | bytes 524288 | tf_op jit(solution)/shard_map/all_to_all | solution.py:122
  168.1 12.0 %all-to-all-done.2 = bf16[4,2,16384]{2,1,0:T(2,128)(2,1)S(1)} async-done(((bf16[4,2,16384]{2,1,0:T(2,128)(2,1)}), bf16[4,2,16384]{2,1,0:T(2,128)(2,1)S(1)}, u32[]{:S(2)}, u32[]{:S(2)}) %all-to-all-start.2) | async-done | bytes 262176 | tf_op jit(solution)/shard_map/all_to_all | solution.py:122
  180.1 3.4 %all-to-all-start.5 = ((bf16[4,2,16384]{2,1,0:T(2,128)(2,1)}), bf16[4,2,16384]{2,1,0:T(2,128)(2,1)S(1)}, u32[]{:S(2)}, u32[]{:S(2)}) async-start(bf16[4,2,16384]{2,1,0:T(2,128)(2,1)} %reshape.271), calls=%async_computation.5 | async-start | bytes 524288 | tf_op jit(solution)/shard_map/all_to_all | solution.py:122
  184.9 2.4 %fusion.67 = bf16[256,1,2,256]{3,2,1,0:T(2,128)(2,1)} fusion(bf16[2,256,256]{2,0,1:T(2,128)(2,1)} %collective-permute-done.5, bf16[2,256,256]{2,0,1:T(2,128)(2,1)} %collective-permute-done.4, f32[1,256,256]{2,0,1:T(1,128)S(1)} %copy-done.26, f32[1,256,256]{2,0,1:T(1,128)S(1)} %copy-done.27), kind=kLoop, calls=%fused_computation.128 | loop fusion | flops 786432 | bytes 1310720 | tf_op jit(solution)/shard_map/broadcast_in_dim | solution.py:125
  187.3 2.2 %all-to-all-done.5 = bf16[4,2,16384]{2,1,0:T(2,128)(2,1)S(1)} async-done(((bf16[4,2,16384]{2,1,0:T(2,128)(2,1)}), bf16[4,2,16384]{2,1,0:T(2,128)(2,1)S(1)}, u32[]{:S(2)}, u32[]{:S(2)}) %all-to-all-start.5) | async-done | bytes 262176 | tf_op jit(solution)/shard_map/all_to_all | solution.py:122
  189.5 3.4 %all-to-all-start.6 = ((bf16[256,1,2,256]{3,2,1,0:T(2,128)(2,1)}), bf16[256,1,2,256]{3,2,1,0:T(2,128)(2,1)S(1)}, u32[]{:S(2)}, u32[]{:S(2)}) async-start(bf16[256,1,2,256]{3,2,1,0:T(2,128)(2,1)} %fusion.67), calls=%async_computation.6 | async-start | bytes 524288 | tf_op jit(solution)/shard_map/all_to_all | solution.py:126
  193.4 2.4 %fusion.66 = bf16[256,1,2,256]{3,2,1,0:T(2,128)(2,1)} fusion(bf16[2,256,256]{2,0,1:T(2,128)(2,1)} %collective-permute-done.7, bf16[2,256,256]{2,0,1:T(2,128)(2,1)} %collective-permute-done.6, f32[1,256,256]{2,0,1:T(1,128)S(1)} %copy.277, f32[1,256,256]{2,0,1:T(1,128)S(1)} %copy.276), kind=kLoop, calls=%fused_computation.127 | loop fusion | flops 786432 | bytes 1310720 | tf_op jit(solution)/shard_map/broadcast_in_dim | solution.py:125
  195.8 3.1 %all-to-all-done.6 = bf16[256,1,2,256]{3,2,1,0:T(2,128)(2,1)S(1)} async-done(((bf16[256,1,2,256]{3,2,1,0:T(2,128)(2,1)}), bf16[256,1,2,256]{3,2,1,0:T(2,128)(2,1)S(1)}, u32[]{:S(2)}, u32[]{:S(2)}) %all-to-all-start.6) | async-done | bytes 262176 | tf_op jit(solution)/shard_map/all_to_all | solution.py:126
  198.9 3.4 %all-to-all-start.7 = ((bf16[256,1,2,256]{3,2,1,0:T(2,128)(2,1)}), bf16[256,1,2,256]{3,2,1,0:T(2,128)(2,1)S(1)}, u32[]{:S(2)}, u32[]{:S(2)}) async-start(bf16[256,1,2,256]{3,2,1,0:T(2,128)(2,1)} %fusion.66), calls=%async_computation.7 | async-start | bytes 524288 | tf_op jit(solution)/shard_map/all_to_all | solution.py:126
  203.6 1.2 reshape.240
  204.8 3.4 %all-to-all-done.7 = bf16[256,1,2,256]{3,2,1,0:T(2,128)(2,1)S(1)} async-done(((bf16[256,1,2,256]{3,2,1,0:T(2,128)(2,1)}), bf16[256,1,2,256]{3,2,1,0:T(2,128)(2,1)S(1)}, u32[]{:S(2)}, u32[]{:S(2)}) %all-to-all-start.7) | async-done | bytes 262176 | tf_op jit(solution)/shard_map/all_to_all | solution.py:126
  (216 shorter events, 52.2 us)
Async XLA Ops:
  0.6 1.2 copy-start.43
  3.4 4.5 %copy-start.39 = (bf16[64,4096]{1,0:T(8,128)(2,1)S(1)}, bf16[64,4096]{1,0:T(8,128)(2,1)}, u32[]{:S(2)}) copy-start(bf16[64,4096]{1,0:T(8,128)(2,1)} %param.5) | copy-start | bytes 1572868
  4.3 12.8 %all-to-all-start = ((bf16[64,4,2,256]{3,2,0,1:T(2,128)(2,1)}), bf16[64,4,2,256]{3,2,0,1:T(2,128)(2,1)S(1)}, u32[]{:S(2)}, u32[]{:S(2)}) async-start(bf16[64,4,2,256]{3,2,0,1:T(2,128)(2,1)} %copy.203), calls=%async_computation | async-start | bytes 524288 | tf_op jit(solution)/shard_map/all_to_all | solution.py:31
  17.1 12.2 %all-to-all-start.3 = ((bf16[64,4,2,256]{3,2,0,1:T(2,128)(2,1)}), bf16[64,4,2,256]{3,2,0,1:T(2,128)(2,1)S(1)}, u32[]{:S(2)}, u32[]{:S(2)}) async-start(bf16[64,4,2,256]{3,2,0,1:T(2,128)(2,1)} %copy.231), calls=%async_computation.3 | async-start | bytes 524288 | tf_op jit(solution)/shard_map/all_to_all | solution.py:31
  22.1 46.0 %copy-start.33 = (pred[256,256]{0,1:T(8,128)(4,1)}, pred[256,256]{0,1:T(8,128)(4,1)S(1)}, u32[]{:S(2)}) copy-start(pred[256,256]{0,1:T(8,128)(4,1)S(1)} %get-tuple-element.57) | copy-start | bytes 196612
  22.1 20.8 %collective-permute-start = (bf16[2,256,256]{2,1,0:T(8,128)(2,1)S(1)}, bf16[2,256,256]{2,1,0:T(8,128)(2,1)S(1)}, u32[]{:S(2)}, u32[]{:S(2)}) collective-permute-start(bf16[2,256,256]{2,1,0:T(8,128)(2,1)S(1)} %bitcast.375), channel_id=1, source_target_pairs={{0,8},{4,12},{8,16},{12,20},{16,24},{20,28},{24,32},{28,36},{32,40... | collective-permute-start | bytes 786440 | tf_op jit(solution)/shard_map/ppermute | solution.py:21
  25.8 18.8 %collective-permute-start.1 = (bf16[2,256,256]{2,1,0:T(8,128)(2,1)S(1)}, bf16[2,256,256]{2,1,0:T(8,128)(2,1)S(1)}, u32[]{:S(2)}, u32[]{:S(2)}) collective-permute-start(bf16[2,256,256]{2,1,0:T(8,128)(2,1)S(1)} %bitcast.377), channel_id=1, source_target_pairs={{0,4},{4,8},{8,12},{12,16},{16,20},{20,24},{24,28},{28,32},{32,36}... | collective-permute-start | bytes 786440 | tf_op jit(solution)/shard_map/ppermute | solution.py:21
  29.3 34.8 %all-to-all-start.1 = ((bf16[64,4,2,512]{3,2,0,1:T(2,128)(2,1)}), bf16[64,4,2,512]{3,2,0,1:T(2,128)(2,1)S(1)}, u32[]{:S(2)}, u32[]{:S(2)}) async-start(bf16[64,4,2,512]{3,2,0,1:T(2,128)(2,1)} %copy.206), calls=%async_computation.1 | async-start | bytes 1048576 | tf_op jit(solution)/shard_map/all_to_all | solution.py:43
  32.8 17.5 %collective-permute-start.3 = (bf16[2,256,256]{2,1,0:T(8,128)(2,1)S(1)}, bf16[2,256,256]{2,1,0:T(8,128)(2,1)S(1)}, u32[]{:S(2)}, u32[]{:S(2)}) collective-permute-start(bf16[2,256,256]{2,1,0:T(8,128)(2,1)S(1)} %bitcast.373), channel_id=1, source_target_pairs={{0,4},{4,8},{8,12},{12,16},{16,20},{20,24},{24,28},{28,32},{32,36}... | collective-permute-start | bytes 786440 | tf_op jit(solution)/shard_map/ppermute | solution.py:21
  36.3 25.4 %collective-permute-start.2 = (bf16[2,256,256]{2,1,0:T(8,128)(2,1)S(1)}, bf16[2,256,256]{2,1,0:T(8,128)(2,1)S(1)}, u32[]{:S(2)}, u32[]{:S(2)}) collective-permute-start(bf16[2,256,256]{2,1,0:T(8,128)(2,1)S(1)} %bitcast.374), channel_id=1, source_target_pairs={{0,8},{4,12},{8,16},{12,20},{16,24},{20,28},{24,32},{28,36},{32,40... | collective-permute-start | bytes 786440 | tf_op jit(solution)/shard_map/ppermute | solution.py:21
  41.3 26.9 %copy-start.16 = (bf16[1,256,256]{1,2,0:T(8,128)(2,1)}, bf16[1,256,256]{1,2,0:T(8,128)(2,1)S(1)}, u32[]{:S(2)}) copy-start(bf16[1,256,256]{1,2,0:T(8,128)(2,1)S(1)} %copy.211) | copy-start | bytes 393220
  45.4 24.0 %copy-start.20 = (bf16[1,256,256]{1,2,0:T(8,128)(2,1)}, bf16[1,256,256]{1,2,0:T(8,128)(2,1)S(1)}, u32[]{:S(2)}) copy-start(bf16[1,256,256]{1,2,0:T(8,128)(2,1)S(1)} %copy.214) | copy-start | bytes 393220
  64.0 16.1 %all-to-all-start.4 = ((bf16[64,4,2,512]{3,2,0,1:T(2,128)(2,1)}), bf16[64,4,2,512]{3,2,0,1:T(2,128)(2,1)S(1)}, u32[]{:S(2)}, u32[]{:S(2)}) async-start(bf16[64,4,2,512]{3,2,0,1:T(2,128)(2,1)} %copy.234), calls=%async_computation.4 | async-start | bytes 1048576 | tf_op jit(solution)/shard_map/all_to_all | solution.py:43
  68.0 1.5 copy-start.6
  70.2 6.9 %copy-start = (f32[2,2,256,256]{2,3,1,0:T(8,128)}, f32[2,2,256,256]{2,3,1,0:T(8,128)S(1)}, u32[]{:S(2)}) copy-start(f32[2,2,256,256]{2,3,1,0:T(8,128)S(1)} %get-tuple-element.72) | copy-start | bytes 3145732
  70.3 6.3 %copy-start.44 = (f32[2,2,256]{2,1,0:T(2,128)}, f32[2,2,256]{2,1,0:T(2,128)S(1)}, u32[]{:S(2)}) copy-start(f32[2,2,256]{2,1,0:T(2,128)S(1)} %get-tuple-element.17) | copy-start | bytes 12292
  70.3 6.3 %copy-start.46 = (f32[2,2,256]{2,1,0:T(2,128)}, f32[2,2,256]{2,1,0:T(2,128)S(1)}, u32[]{:S(2)}) copy-start(f32[2,2,256]{2,1,0:T(2,128)S(1)} %get-tuple-element.18) | copy-start | bytes 12292
  70.8 2.0 copy-start.38
  72.7 1.9 copy-start.37
  81.1 1.3 copy-start.18
  81.1 1.3 copy-start.32
  82.4 1.4 copy-start.24
  82.4 1.4 copy-start.30
  88.2 1.5 copy-start.2
  88.2 1.5 copy-start.4
  88.2 1.5 copy-start.35
  89.7 1.2 copy-start.3
  89.8 1.2 copy-start.34
  91.0 3.1 %copy-start.11 = (f32[2,2,256,256]{2,3,1,0:T(8,128)S(1)}, f32[2,2,256,256]{2,3,1,0:T(8,128)}, u32[]{:S(2)}) copy-start(f32[2,2,256,256]{2,3,1,0:T(8,128)} %get-tuple-element.74) | copy-start | bytes 3145732
  91.0 3.1 %copy-start.12 = (f32[2,2,256,256]{2,3,1,0:T(8,128)S(1)}, f32[2,2,256,256]{2,3,1,0:T(8,128)}, u32[]{:S(2)}) copy-start(f32[2,2,256,256]{2,3,1,0:T(8,128)} %get-tuple-element.73) | copy-start | bytes 3145732
  91.4 2.7 %copy-start.10 = (f32[2,2,256,256]{2,3,1,0:T(8,128)S(1)}, f32[2,2,256,256]{2,3,1,0:T(8,128)}, u32[]{:S(2)}) copy-start(f32[2,2,256,256]{2,3,1,0:T(8,128)} %get-tuple-element.75) | copy-start | bytes 3145732
  92.4 1.7 copy-start.1
  94.1 1.4 copy-start.7
  103.5 4.5 %copy-start.9 = (bf16[2,2,256,256]{2,3,1,0:T(8,128)(2,1)S(1)}, bf16[2,2,256,256]{2,3,1,0:T(8,128)(2,1)}, u32[]{:S(2)}) copy-start(bf16[2,2,256,256]{2,3,1,0:T(8,128)(2,1)} %get-tuple-element.49) | copy-start | bytes 1572868
  104.8 3.2 %copy-start.8 = (bf16[256,1,1,512]{0,3,2,1:T(8,128)(2,1)S(1)}, bf16[256,1,1,512]{0,3,2,1:T(8,128)(2,1)}, u32[]{:S(2)}) copy-start(bf16[256,1,1,512]{0,3,2,1:T(8,128)(2,1)} %copy-done.6) | copy-start | bytes 786436
  104.8 79.2 %collective-permute-start.4 = (bf16[2,256,256]{2,0,1:T(2,128)(2,1)}, bf16[2,256,256]{2,0,1:T(2,128)(2,1)}, u32[]{:S(2)}, u32[]{:S(2)}) collective-permute-start(bf16[2,256,256]{2,0,1:T(2,128)(2,1)} %pad_maximum_fusion.6), channel_id=1, source_target_pairs={{4,0},{8,4},{12,8},{16,12},{20,16},{24,20},{28,24},{32,28},{36,32}... | collective-permute-start | bytes 786440 | tf_op jit(solution)/shard_map/ppermute | solution.py:21
  111.3 72.7 %collective-permute-start.5 = (bf16[2,256,256]{2,0,1:T(2,128)(2,1)}, bf16[2,256,256]{2,0,1:T(2,128)(2,1)}, u32[]{:S(2)}, u32[]{:S(2)}) collective-permute-start(bf16[2,256,256]{2,0,1:T(2,128)(2,1)} %pad_maximum_fusion.7), channel_id=1, source_target_pairs={{8,0},{12,4},{16,8},{20,12},{24,16},{28,20},{32,24},{36,28},{40,32... | collective-permute-start | bytes 786440 | tf_op jit(solution)/shard_map/ppermute | solution.py:21
  117.9 1.8 copy-start.42
  122.3 71.2 %collective-permute-start.6 = (bf16[2,256,256]{2,0,1:T(2,128)(2,1)}, bf16[2,256,256]{2,0,1:T(2,128)(2,1)}, u32[]{:S(2)}, u32[]{:S(2)}) collective-permute-start(bf16[2,256,256]{2,0,1:T(2,128)(2,1)} %pad_maximum_fusion.8), channel_id=1, source_target_pairs={{4,0},{8,4},{12,8},{16,12},{20,16},{24,20},{28,24},{32,28},{36,32}... | collective-permute-start | bytes 786440 | tf_op jit(solution)/shard_map/ppermute | solution.py:21
  127.1 29.9 %copy-start.14 = (f32[2,128,2,256]{3,1,2,0:T(8,128)S(1)}, f32[2,128,2,256]{3,1,2,0:T(8,128)}, u32[]{:S(2)}) copy-start(f32[2,128,2,256]{3,1,2,0:T(8,128)} %fusion.89) | copy-start | bytes 1572868
  128.9 28.1 %copy-start.13 = (f32[2,128,2,256]{3,1,2,0:T(8,128)S(1)}, f32[2,128,2,256]{3,1,2,0:T(8,128)}, u32[]{:S(2)}) copy-start(f32[2,128,2,256]{3,1,2,0:T(8,128)} %fusion.88) | copy-start | bytes 1572868
  128.9 28.1 %copy-start.23 = (bf16[1,256,256]{1,2,0:T(8,128)(2,1)S(1)}, bf16[1,256,256]{1,2,0:T(8,128)(2,1)}, u32[]{:S(2)}) copy-start(bf16[1,256,256]{1,2,0:T(8,128)(2,1)} %copy.205) | copy-start | bytes 393220
  131.3 62.1 %collective-permute-start.7 = (bf16[2,256,256]{2,0,1:T(2,128)(2,1)}, bf16[2,256,256]{2,0,1:T(2,128)(2,1)}, u32[]{:S(2)}, u32[]{:S(2)}) collective-permute-start(bf16[2,256,256]{2,0,1:T(2,128)(2,1)} %pad_maximum_fusion.9), channel_id=1, source_target_pairs={{8,0},{12,4},{16,8},{20,12},{24,16},{28,20},{32,24},{36,28},{40,32... | collective-permute-start | bytes 786440 | tf_op jit(solution)/shard_map/ppermute | solution.py:21
  161.3 18.8 %all-to-all-start.2 = ((bf16[4,2,16384]{2,1,0:T(2,128)(2,1)}), bf16[4,2,16384]{2,1,0:T(2,128)(2,1)S(1)}, u32[]{:S(2)}, u32[]{:S(2)}) async-start(bf16[4,2,16384]{2,1,0:T(2,128)(2,1)} %reshape.273), calls=%async_computation.2 | async-start | bytes 524288 | tf_op jit(solution)/shard_map/all_to_all | solution.py:122
  168.1 15.4 %copy-start.5 = (bf16[256,1,1,512]{0,3,2,1:T(8,128)(2,1)S(1)}, bf16[256,1,1,512]{0,3,2,1:T(8,128)(2,1)}, u32[]{:S(2)}) copy-start(bf16[256,1,1,512]{0,3,2,1:T(8,128)(2,1)} %copy.246) | copy-start | bytes 786436
  180.1 9.4 %all-to-all-start.5 = ((bf16[4,2,16384]{2,1,0:T(2,128)(2,1)}), bf16[4,2,16384]{2,1,0:T(2,128)(2,1)S(1)}, u32[]{:S(2)}, u32[]{:S(2)}) async-start(bf16[4,2,16384]{2,1,0:T(2,128)(2,1)} %reshape.271), calls=%async_computation.5 | async-start | bytes 524288 | tf_op jit(solution)/shard_map/all_to_all | solution.py:122
  189.5 9.4 %all-to-all-start.6 = ((bf16[256,1,2,256]{3,2,1,0:T(2,128)(2,1)}), bf16[256,1,2,256]{3,2,1,0:T(2,128)(2,1)S(1)}, u32[]{:S(2)}, u32[]{:S(2)}) async-start(bf16[256,1,2,256]{3,2,1,0:T(2,128)(2,1)} %fusion.67), calls=%async_computation.6 | async-start | bytes 524288 | tf_op jit(solution)/shard_map/all_to_all | solution.py:126
  198.9 9.4 %all-to-all-start.7 = ((bf16[256,1,2,256]{3,2,1,0:T(2,128)(2,1)}), bf16[256,1,2,256]{3,2,1,0:T(2,128)(2,1)S(1)}, u32[]{:S(2)}, u32[]{:S(2)}) async-start(bf16[256,1,2,256]{3,2,1,0:T(2,128)(2,1)} %fusion.66), calls=%async_computation.7 | async-start | bytes 524288 | tf_op jit(solution)/shard_map/all_to_all | solution.py:126
  (22 other events, 20.6 us)

commit v3 on v1

v3 whole, which is shorter than its diff:
```python
import jax
import jax.numpy as jnp
from jax import lax
from jax.experimental import pallas as pl
from jax.sharding import PartitionSpec as P

QUERY_HEADS = 32
KEY_VALUE_HEADS = 16
HEAD_SIZE = 128
WINDOW = 512
SPAN = 2
CHAIN = False

score_scale = 168.0 ** (-0.5)
NT = (((1,), (1,)), ((), ()))
TN = (((0,), (0,)), ((), ()))


def attn_kernel(rel_ref, q_ref, g_ref, kv0_ref, kv1_ref, kv2_ref, dq_ref, dkv0_ref, dkv1_ref, dkv2_ref):
    tok = q_ref.shape[0]
    kv_refs = (kv0_ref, kv1_ref, kv2_ref)
    dkv_refs = (dkv0_ref, dkv1_ref, dkv2_ref)
    share = q_ref.shape[1] // HEAD_SIZE
    row = lax.broadcasted_iota(jnp.int32, (tok, tok), 0)
    col = lax.broadcasted_iota(jnp.int32, (tok, tok), 1)
    rel = rel_ref[...]
    masks = []
    for d in range(3):
        key_rel = col - tok * d
        masks.append((key_rel >= rel) & (key_rel <= row) & (row - key_rel < WINDOW))
    keys = [r[0] for r in kv_refs]
    vals = [r[1] for r in kv_refs]
    dk = [jnp.zeros((tok, HEAD_SIZE), jnp.float32) for _ in range(3)]
    dv = [jnp.zeros((tok, HEAD_SIZE), jnp.float32) for _ in range(3)]
    for j in range(share):
        qj = q_ref[:, j * HEAD_SIZE:(j + 1) * HEAD_SIZE]
        gj = g_ref[:, j * HEAD_SIZE:(j + 1) * HEAD_SIZE]
        scores = []
        for d in range(3):
            s = score_scale * lax.dot_general(qj, keys[d], NT, preferred_element_type=jnp.float32)
            scores.append(jnp.where(masks[d], s, -jnp.inf))
        m = jnp.max(scores[0], axis=1, keepdims=True)
        for d in range(1, 3):
            m = jnp.maximum(m, jnp.max(scores[d], axis=1, keepdims=True))
        tot = jnp.zeros_like(m)
        for d in range(3):
            tot = tot + jnp.sum(jnp.exp(scores[d] - m), axis=1, keepdims=True)
        lse = m + jnp.log(tot)
        probs, dprobs = [], []
        delta = jnp.zeros_like(m)
        for d in range(3):
            p = jnp.exp(scores[d] - lse)
            dp = lax.dot_general(gj, vals[d], NT, preferred_element_type=jnp.float32)
            delta = delta + jnp.sum(p * dp, axis=1, keepdims=True)
            probs.append(p)
            dprobs.append(dp)
        dq = jnp.zeros((tok, HEAD_SIZE), jnp.float32)
        for d in range(3):
            ds = (probs[d] * (dprobs[d] - delta)).astype(jnp.bfloat16)
            ph = probs[d].astype(jnp.bfloat16)
            dq = dq + jnp.dot(ds, keys[d], preferred_element_type=jnp.float32)
            dk[d] = dk[d] + lax.dot_general(ds, qj, TN, preferred_element_type=jnp.float32)
            dv[d] = dv[d] + lax.dot_general(ph, gj, TN, preferred_element_type=jnp.float32)
        dq_ref[:, j * HEAD_SIZE:(j + 1) * HEAD_SIZE] = score_scale * dq
    for d in range(3):
        dkv_refs[d][0] = score_scale * dk[d]
        dkv_refs[d][1] = dv[d]


def attend(rel, qh, gh, kv_blocks):
    tok, qcols = qh.shape
    kvcols = kv_blocks[0].shape[-1]
    groups = kvcols // HEAD_SIZE
    qblk = qcols // groups
    kv_spec = pl.BlockSpec((2, tok, HEAD_SIZE), lambda g: (0, 0, g))
    q_spec = pl.BlockSpec((tok, qblk), lambda g: (0, g))
    return pl.pallas_call(
        attn_kernel,
        grid=(groups,),
        in_specs=[pl.BlockSpec((tok, 1), lambda g: (0, 0)), q_spec, q_spec, kv_spec, kv_spec, kv_spec],
        out_specs=[q_spec, kv_spec, kv_spec, kv_spec],
        out_shape=[
            jax.ShapeDtypeStruct((tok, qcols), jnp.float32),
            jax.ShapeDtypeStruct((2, tok, kvcols), jnp.float32),
            jax.ShapeDtypeStruct((2, tok, kvcols), jnp.float32),
            jax.ShapeDtypeStruct((2, tok, kvcols), jnp.float32),
        ],
    )(rel, qh, gh, *kv_blocks)


def passed_along(block, axis, distance):
    devices = range(lax.axis_size(axis))
    route = [(i - distance, i) for i in devices if i - distance in devices]
    return lax.ppermute(block, axis, route)


def local(queries, normed_key_state, value_state_rows, output_gradient, doc_start):
    heads_ax = lax.axis_size("head")
    rows_in = queries.shape[0]
    kv_cols = normed_key_state.shape[1] // heads_ax
    q_cols = queries.shape[1] // heads_ax
    kv_in = jnp.stack(
        [
            normed_key_state.reshape(rows_in, heads_ax, kv_cols),
            value_state_rows.reshape(rows_in, heads_ax, kv_cols),
        ],
        axis=2,
    )
    kv_all = lax.all_to_all(kv_in, "head", split_axis=1, concat_axis=0, tiled=True)
    tok_rows = kv_all.shape[0]
    kv_local = jnp.moveaxis(kv_all[:, 0], 1, 0)
    kv_blocks = [kv_local]
    for distance in range(1, SPAN + 1):
        if CHAIN:
            kv_blocks.append(passed_along(kv_blocks[-1], "ctx", 1))
        else:
            kv_blocks.append(passed_along(kv_local, "ctx", distance))
    qg_in = jnp.stack(
        [
            queries.reshape(rows_in, heads_ax, q_cols),
            output_gradient.reshape(rows_in, heads_ax, q_cols),
        ],
        axis=2,
    )
    qg_all = lax.all_to_all(qg_in, "head", split_axis=1, concat_axis=0, tiled=True)
    shard_index = lax.axis_index("ctx")
    rel = (doc_start - shard_index * tok_rows).reshape(tok_rows, 1)
    dq, dkv0, dkv1, dkv2 = attend(rel, qg_all[:, 0, 0], qg_all[:, 0, 1], kv_blocks)
    if CHAIN:
        carried = passed_along(dkv2.astype(jnp.bfloat16), "ctx", -1)
        carried = passed_along((dkv1 + carried).astype(jnp.bfloat16), "ctx", -1)
        kv_total = dkv0 + carried
    else:
        kv_total = dkv0
        for distance, part in ((1, dkv1), (2, dkv2)):
            kv_total = kv_total + passed_along(part.astype(jnp.bfloat16), "ctx", -distance)
    grad_q = lax.all_to_all(
        dq.astype(jnp.bfloat16)[:, None], "head", split_axis=0, concat_axis=1, tiled=True
    ).reshape(rows_in, heads_ax * q_cols)
    kv_out = jnp.moveaxis(kv_total.astype(jnp.bfloat16), 0, 1)[:, None]
    kv_back = lax.all_to_all(kv_out, "head", split_axis=0, concat_axis=1, tiled=True)
    grad_k = kv_back[:, :, 0].reshape(rows_in, heads_ax * kv_cols)
    grad_v = kv_back[:, :, 1].reshape(rows_in, heads_ax * kv_cols)
    return grad_q, grad_k, grad_v


def solution(mesh):
    placed = (
        P(("ctx", "head"), None),
        P(("ctx", "head"), None),
        P(("ctx", "head"), None),
        P(("ctx", "head"), None),
        P("ctx"),
    )
    return jax.shard_map(
        local,
        mesh=mesh,
        in_specs=placed,
        out_specs=(P(("ctx", "head"), None), P(("ctx", "head"), None), P(("ctx", "head"), None)),
        check_vma=False,
    )
```

time: 193 us -> 184 us (0.953)
  the two profiles are of different devices: /device:TPU:190 before, /device:TPU:182 now
where the time goes in v3:
time: 184 us; the launch traced here: 183 us
  waiting for transfers between devices  121 us (66%)
  starting transfers between devices  28 us (15%)
  local copies, waits for them, and re-layouts  16.4 us (9%)
  Pallas kernels  10.4 us (6%)
  other arithmetic  6.52 us (4%)
    ppermute x4, waiting for transfers between devices, passed_along(): return lax.ppermute(block, axis, route)  106 us
    ppermute x4, starting transfers between devices, passed_along(): return lax.ppermute(block, axis, route)  13.8 us
    pallas_call x1, Pallas kernels, attend(): pl.pallas_call(attn_kernel, grid=(groups,), in_specs=[pl.BlockSpec((tok,...  10.4 us
    all_to_all x1, waiting for transfers between devices, local(): lax.all_to_all(kv_out, 'head', split_axis=0, concat_axis=1, tiled=True)  6.69 us
    unnamed x26, local copies, waits for them, and re-layouts  6.51 us
    all_to_all x1, waiting for transfers between devices, local(): lax.all_to_all(kv_in, 'head', split_axis=1, concat_axis=0, tiled=True)  5.33 us
    all_to_all x1, starting transfers between devices, local(): lax.all_to_all(kv_in, 'head', split_axis=1, concat_axis=0, tiled=True)  3.77 us
  transfers between devices with their start and end apart: 8, of which 7 were waited for; matrix products, arithmetic and copies ran while one was open for 7% of the time, Pallas kernels for 0%

profile of v3, /device:TPU:182, one launch (start us, length us, event | category | flops | bytes accessed | tf_op | source)
XLA Modules:
  0.0 183.1 jit_solution(4273564077674461746)
XLA Ops:
  0.6 1.2 stack_reshape.14
  1.8 0.2 stack_reshape.15
  2.0 0.4 pad_maximum_fusion.1
  2.4 0.9 copy.42
  3.3 3.8 %all-to-all-start.1 = ((bf16[64,4,2,512]{3,0,2,1:T(8,128)(2,1)}), bf16[64,4,2,512]{3,0,2,1:T(8,128)(2,1)S(1)}, u32[]{:S(2)}, u32[]{:S(2)}) async-start(bf16[64,4,2,512]{3,0,2,1:T(8,128)(2,1)} %copy.42), calls=%async_computation.1 | async-start | bytes 1048576 | tf_op jit(solution)/shard_map/all_to_all | solution.py:109
  7.1 0.4 stack_reshape.12
  7.4 0.7 copy-done.5
  8.1 0.4 stack_reshape.13
  8.5 0.7 pad_maximum_fusion
  9.2 1.3 copy.40
  10.5 5.3 %all-to-all-done.1 = bf16[64,4,2,512]{3,0,2,1:T(8,128)(2,1)S(1)} async-done(((bf16[64,4,2,512]{3,0,2,1:T(8,128)(2,1)}), bf16[64,4,2,512]{3,0,2,1:T(8,128)(2,1)S(1)}, u32[]{:S(2)}, u32[]{:S(2)}) %all-to-all-start.1) | async-done | bytes 524320 | tf_op jit(solution)/shard_map/all_to_all | solution.py:109
  15.9 3.5 %all-to-all-start = ((bf16[64,4,2,1024]{3,0,2,1:T(8,128)(2,1)}), bf16[64,4,2,1024]{3,0,2,1:T(8,128)(2,1)S(1)}, u32[]{:S(2)}, u32[]{:S(2)}) async-start(bf16[64,4,2,1024]{3,0,2,1:T(8,128)(2,1)} %copy.40), calls=%async_computation | async-start | bytes 2097152 | tf_op jit(solution)/shard_map/all_to_all | solution.py:125
  19.4 2.6 %collective-permute-start = (bf16[2,256,512]{2,1,0:T(8,128)(2,1)S(1)}, bf16[2,256,512]{2,1,0:T(8,128)(2,1)S(1)}, u32[]{:S(2)}, u32[]{:S(2)}) collective-permute-start(bf16[2,256,512]{2,1,0:T(8,128)(2,1)S(1)} %bitcast.47), channel_id=1, source_target_pairs={{0,4},{4,8},{8,12},{12,16},{16,20},{20,24},{24,28},{28,32},{32,36}... | collective-permute-start | bytes 1572872 | tf_op jit(solution)/shard_map/ppermute | solution.py:94
  22.0 7.2 %collective-permute-start.1 = (bf16[2,256,512]{2,1,0:T(8,128)(2,1)S(1)}, bf16[2,256,512]{2,1,0:T(8,128)(2,1)S(1)}, u32[]{:S(2)}, u32[]{:S(2)}) collective-permute-start(bf16[2,256,512]{2,1,0:T(8,128)(2,1)S(1)} %bitcast.48), channel_id=1, source_target_pairs={{0,8},{4,12},{8,16},{12,20},{16,24},{20,28},{24,32},{28,36},{32,40... | collective-permute-start | bytes 1572872 | tf_op jit(solution)/shard_map/ppermute | solution.py:94
  29.3 0.0 copy-start.9
  29.3 0.7 copy-done.9
  30.0 0.8 copy.44.rel_ref
  30.8 3.0 %all-to-all-done = bf16[64,4,2,1024]{3,0,2,1:T(8,128)(2,1)S(1)} async-done(((bf16[64,4,2,1024]{3,0,2,1:T(8,128)(2,1)}), bf16[64,4,2,1024]{3,0,2,1:T(8,128)(2,1)S(1)}, u32[]{:S(2)}, u32[]{:S(2)}) %all-to-all-start) | async-done | bytes 1048608 | tf_op jit(solution)/shard_map/all_to_all | solution.py:125
  33.8 0.1 copy.41
  33.9 1.0 slice_bitcast_fusion
  34.9 1.4 collective-permute-done.kv1_ref
  36.4 28.5 %collective-permute-done.1.kv2_ref = bf16[2,256,512]{2,1,0:T(8,128)(2,1)S(1)} collective-permute-done((bf16[2,256,512]{2,1,0:T(8,128)(2,1)S(1)}, bf16[2,256,512]{2,1,0:T(8,128)(2,1)S(1)}, u32[]{:S(2)}, u32[]{:S(2)}) %collective-permute-start.1) | collective-permute-done | bytes 524320 | tf_op jit(solution)/shard_map/ppermute | solution.py:94
  64.9 0.8 copy-done.7
  65.7 10.4 %shard_map.76 = (f32[256,1024]{1,0:T(8,128)}, f32[2,256,512]{2,1,0:T(8,128)}, f32[2,256,512]{2,1,0:T(8,128)}, f32[2,256,512]{2,1,0:T(8,128)}) custom-call(s32[256,1]{1,0:T(8,128)} %copy.44.rel_ref, bf16[256,1024]{1,0:T(8,128)(2,1)} %get-tuple-element.12.q_ref, bf16[256,1024]{1,0:T(8,128)(2,1)} %get-tuple-element.11.g_ref, bf16[2,256,512]{2,1,0:T(8,128)(2,1)} %bitcast.49, ...), custom_call_target="tpu_custom_call" | custom-call | tf_op jit(solution)/shard_map/pallas_call | solution.py:77
  76.1 2.2 %convert_element_type.19 = bf16[2,256,512]{2,1,0:T(8,128)(2,1)} convert(f32[2,256,512]{2,1,0:T(8,128)} %get-tuple-element.9) | non-fusion elementwise | flops 262144 | bytes 1572864 | tf_op jit(solution)/shard_map/convert_element_type | solution.py:136
  78.3 2.0 %collective-permute-start.2 = (bf16[2,256,512]{2,1,0:T(8,128)(2,1)}, bf16[2,256,512]{2,1,0:T(8,128)(2,1)S(1)}, u32[]{:S(2)}, u32[]{:S(2)}) collective-permute-start(bf16[2,256,512]{2,1,0:T(8,128)(2,1)} %convert_element_type.19), channel_id=1, source_target_pairs={{4,0},{8,4},{12,8},{16,12},{20,16},{24,20},{28,24},{32,28},{36,32}... | collective-permute-start | bytes 1572872 | tf_op jit(solution)/shard_map/ppermute | solution.py:94
  80.3 0.9 convert_element_type.21
  81.2 1.9 %collective-permute-start.3 = (bf16[2,256,512]{2,1,0:T(8,128)(2,1)}, bf16[2,256,512]{2,1,0:T(8,128)(2,1)}, u32[]{:S(2)}, u32[]{:S(2)}) collective-permute-start(bf16[2,256,512]{2,1,0:T(8,128)(2,1)} %convert_element_type.21), channel_id=1, source_target_pairs={{8,0},{12,4},{16,8},{20,12},{24,16},{28,20},{32,24},{36,28},{40,32... | collective-permute-start | bytes 1572872 | tf_op jit(solution)/shard_map/ppermute | solution.py:94
  83.1 0.1 convert_bitcast_fusion
  83.2 0.5 broadcast
  83.7 1.0 reduce
  84.7 1.2 reshape.16
  85.9 3.5 %all-to-all-start.2 = ((bf16[4,2,32768]{2,1,0:T(2,128)(2,1)}), bf16[4,2,32768]{2,1,0:T(2,128)(2,1)S(1)}, u32[]{:S(2)}, u32[]{:S(2)}) async-start(bf16[4,2,32768]{2,1,0:T(2,128)(2,1)} %reshape.16), calls=%async_computation.2 | async-start | bytes 1048576 | tf_op jit(solution)/shard_map/all_to_all | solution.py:137
  89.4 37.4 %collective-permute-done.2 = bf16[2,256,512]{2,1,0:T(8,128)(2,1)S(1)} collective-permute-done((bf16[2,256,512]{2,1,0:T(8,128)(2,1)}, bf16[2,256,512]{2,1,0:T(8,128)(2,1)S(1)}, u32[]{:S(2)}, u32[]{:S(2)}) %collective-permute-start.2) | collective-permute-done | bytes 524320 | tf_op jit(solution)/shard_map/ppermute | solution.py:94
  126.8 38.5 %collective-permute-done.3 = bf16[2,256,512]{2,1,0:T(8,128)(2,1)} collective-permute-done((bf16[2,256,512]{2,1,0:T(8,128)(2,1)}, bf16[2,256,512]{2,1,0:T(8,128)(2,1)}, u32[]{:S(2)}, u32[]{:S(2)}) %collective-permute-start.3) | collective-permute-done | bytes 524320 | tf_op jit(solution)/shard_map/ppermute | solution.py:94
  165.3 1.3 fusion
  166.6 1.3 copy.47
  167.9 3.5 %all-to-all-start.3 = ((bf16[256,1,2,512]{3,2,1,0:T(2,128)(2,1)}), bf16[256,1,2,512]{3,2,1,0:T(2,128)(2,1)S(1)}, u32[]{:S(2)}, u32[]{:S(2)}) async-start(bf16[256,1,2,512]{3,2,1,0:T(2,128)(2,1)} %copy.47), calls=%async_computation.3 | async-start | bytes 1048576 | tf_op jit(solution)/shard_map/all_to_all | solution.py:141
  171.4 0.5 reshape.17
  171.9 0.2 copy.50
  172.1 0.4 copy.46
  172.5 1.0 copy.51
  173.5 6.7 %all-to-all-done.3 = bf16[256,1,2,512]{3,2,1,0:T(2,128)(2,1)S(1)} async-done(((bf16[256,1,2,512]{3,2,1,0:T(2,128)(2,1)}), bf16[256,1,2,512]{3,2,1,0:T(2,128)(2,1)S(1)}, u32[]{:S(2)}, u32[]{:S(2)}) %all-to-all-start.3) | async-done | bytes 524320 | tf_op jit(solution)/shard_map/all_to_all | solution.py:141
  180.2 0.7 fusion.1
  180.9 0.3 copy.48
  181.3 0.8 copy.52
  182.0 0.3 copy.49
  182.3 0.8 copy.53
  (19 shorter events, 0.1 us)
Async XLA Ops:
  0.6 1.2 copy-start.8
  3.3 3.8 %copy-start.4 = (bf16[64,4096]{1,0:T(8,128)(2,1)S(1)}, bf16[64,4096]{1,0:T(8,128)(2,1)}, u32[]{:S(2)}) copy-start(bf16[64,4096]{1,0:T(8,128)(2,1)} %param.5) | copy-start | bytes 1572868
  3.3 12.6 %all-to-all-start.1 = ((bf16[64,4,2,512]{3,0,2,1:T(8,128)(2,1)}), bf16[64,4,2,512]{3,0,2,1:T(8,128)(2,1)S(1)}, u32[]{:S(2)}, u32[]{:S(2)}) async-start(bf16[64,4,2,512]{3,0,2,1:T(8,128)(2,1)} %copy.42), calls=%async_computation.1 | async-start | bytes 1048576 | tf_op jit(solution)/shard_map/all_to_all | solution.py:109
  7.1 1.0 copy-start.5
  15.9 17.9 %all-to-all-start = ((bf16[64,4,2,1024]{3,0,2,1:T(8,128)(2,1)}), bf16[64,4,2,1024]{3,0,2,1:T(8,128)(2,1)S(1)}, u32[]{:S(2)}, u32[]{:S(2)}) async-start(bf16[64,4,2,1024]{3,0,2,1:T(8,128)(2,1)} %copy.40), calls=%async_computation | async-start | bytes 2097152 | tf_op jit(solution)/shard_map/all_to_all | solution.py:125
  19.4 14.4 %copy-start = (bf16[4,64,1,2,512]{4,1,0,3,2:T(8,128)(2,1)}, bf16[4,64,1,2,512]{4,1,0,3,2:T(8,128)(2,1)S(1)}, u32[]{:S(2)}) copy-start(bf16[4,64,1,2,512]{4,1,0,3,2:T(8,128)(2,1)S(1)} %copy.43) | copy-start | bytes 1572868
  19.4 16.9 %collective-permute-start = (bf16[2,256,512]{2,1,0:T(8,128)(2,1)S(1)}, bf16[2,256,512]{2,1,0:T(8,128)(2,1)S(1)}, u32[]{:S(2)}, u32[]{:S(2)}) collective-permute-start(bf16[2,256,512]{2,1,0:T(8,128)(2,1)S(1)} %bitcast.47), channel_id=1, source_target_pairs={{0,4},{4,8},{8,12},{12,16},{16,20},{20,24},{24,28},{28,32},{32,36}... | collective-permute-start | bytes 1572872 | tf_op jit(solution)/shard_map/ppermute | solution.py:94
  22.0 42.8 %collective-permute-start.1 = (bf16[2,256,512]{2,1,0:T(8,128)(2,1)S(1)}, bf16[2,256,512]{2,1,0:T(8,128)(2,1)S(1)}, u32[]{:S(2)}, u32[]{:S(2)}) collective-permute-start(bf16[2,256,512]{2,1,0:T(8,128)(2,1)S(1)} %bitcast.48), channel_id=1, source_target_pairs={{0,8},{4,12},{8,16},{12,20},{16,24},{20,28},{24,32},{28,36},{32,40... | collective-permute-start | bytes 1572872 | tf_op jit(solution)/shard_map/ppermute | solution.py:94
  29.3 0.7 copy-start.9
  36.4 28.5 %copy-start.6 = (bf16[2,256,512]{2,1,0:T(8,128)(2,1)}, bf16[2,256,512]{2,1,0:T(8,128)(2,1)S(1)}, u32[]{:S(2)}) copy-start(bf16[2,256,512]{2,1,0:T(8,128)(2,1)S(1)} %collective-permute-done.kv1_ref) | copy-start | bytes 1572868
  64.9 0.8 copy-start.7
  76.1 4.2 %copy-start.2 = (f32[2,256,512]{2,1,0:T(8,128)S(1)}, f32[2,256,512]{2,1,0:T(8,128)}, u32[]{:S(2)}) copy-start(f32[2,256,512]{2,1,0:T(8,128)} %get-tuple-element.10) | copy-start | bytes 3145732
  78.3 4.8 %copy-start.1 = (f32[256,1024]{1,0:T(8,128)S(1)}, f32[256,1024]{1,0:T(8,128)}, u32[]{:S(2)}) copy-start(f32[256,1024]{1,0:T(8,128)} %get-tuple-element.7) | copy-start | bytes 3145732
  78.3 48.5 %collective-permute-start.2 = (bf16[2,256,512]{2,1,0:T(8,128)(2,1)}, bf16[2,256,512]{2,1,0:T(8,128)(2,1)S(1)}, u32[]{:S(2)}, u32[]{:S(2)}) collective-permute-start(bf16[2,256,512]{2,1,0:T(8,128)(2,1)} %convert_element_type.19), channel_id=1, source_target_pairs={{4,0},{8,4},{12,8},{16,12},{20,16},{24,20},{28,24},{32,28},{36,32}... | collective-permute-start | bytes 1572872 | tf_op jit(solution)/shard_map/ppermute | solution.py:94
  81.2 84.1 %collective-permute-start.3 = (bf16[2,256,512]{2,1,0:T(8,128)(2,1)}, bf16[2,256,512]{2,1,0:T(8,128)(2,1)}, u32[]{:S(2)}, u32[]{:S(2)}) collective-permute-start(bf16[2,256,512]{2,1,0:T(8,128)(2,1)} %convert_element_type.21), channel_id=1, source_target_pairs={{8,0},{12,4},{16,8},{20,12},{24,16},{28,20},{32,24},{36,28},{40,32... | collective-permute-start | bytes 1572872 | tf_op jit(solution)/shard_map/ppermute | solution.py:94
  84.7 80.6 %copy-start.3 = (f32[2,256,512]{2,1,0:T(8,128)S(1)}, f32[2,256,512]{2,1,0:T(8,128)}, u32[]{:S(2)}) copy-start(f32[2,256,512]{2,1,0:T(8,128)} %get-tuple-element.8) | copy-start | bytes 3145732
  85.9 82.0 %all-to-all-start.2 = ((bf16[4,2,32768]{2,1,0:T(2,128)(2,1)}), bf16[4,2,32768]{2,1,0:T(2,128)(2,1)S(1)}, u32[]{:S(2)}, u32[]{:S(2)}) async-start(bf16[4,2,32768]{2,1,0:T(2,128)(2,1)} %reshape.16), calls=%async_computation.2 | async-start | bytes 1048576 | tf_op jit(solution)/shard_map/all_to_all | solution.py:137
  167.9 12.3 %all-to-all-start.3 = ((bf16[256,1,2,512]{3,2,1,0:T(2,128)(2,1)}), bf16[256,1,2,512]{3,2,1,0:T(2,128)(2,1)S(1)}, u32[]{:S(2)}, u32[]{:S(2)}) async-start(bf16[256,1,2,512]{3,2,1,0:T(2,128)(2,1)} %copy.47), calls=%async_computation.3 | async-start | bytes 1048576 | tf_op jit(solution)/shard_map/all_to_all | solution.py:141

commit v4 on v3

--- a/solution.py
+++ b/solution.py
@@ -10,6 +10,7 @@
 WINDOW = 512
 SPAN = 2
 CHAIN = False
+CHUNKS = 2
 
 score_scale = 168.0 ** (-0.5)
 NT = (((1,), (1,)), ((), ()))
@@ -94,20 +95,8 @@
     return lax.ppermute(block, axis, route)
 
 
-def local(queries, normed_key_state, value_state_rows, output_gradient, doc_start):
-    heads_ax = lax.axis_size("head")
-    rows_in = queries.shape[0]
-    kv_cols = normed_key_state.shape[1] // heads_ax
-    q_cols = queries.shape[1] // heads_ax
-    kv_in = jnp.stack(
-        [
-            normed_key_state.reshape(rows_in, heads_ax, kv_cols),
-            value_state_rows.reshape(rows_in, heads_ax, kv_cols),
-        ],
-        axis=2,
-    )
+def chunk_pass(kv_in, qg_in, rel):
     kv_all = lax.all_to_all(kv_in, "head", split_axis=1, concat_axis=0, tiled=True)
-    tok_rows = kv_all.shape[0]
     kv_local = jnp.moveaxis(kv_all[:, 0], 1, 0)
     kv_blocks = [kv_local]
     for distance in range(1, SPAN + 1):
@@ -115,16 +104,7 @@
             kv_blocks.append(passed_along(kv_blocks[-1], "ctx", 1))
         else:
             kv_blocks.append(passed_along(kv_local, "ctx", distance))
-    qg_in = jnp.stack(
-        [
-            queries.reshape(rows_in, heads_ax, q_cols),
-            output_gradient.reshape(rows_in, heads_ax, q_cols),
-        ],
-        axis=2,
-    )
     qg_all = lax.all_to_all(qg_in, "head", split_axis=1, concat_axis=0, tiled=True)
-    shard_index = lax.axis_index("ctx")
-    rel = (doc_start - shard_index * tok_rows).reshape(tok_rows, 1)
     dq, dkv0, dkv1, dkv2 = attend(rel, qg_all[:, 0, 0], qg_all[:, 0, 1], kv_blocks)
     if CHAIN:
         carried = passed_along(dkv2.astype(jnp.bfloat16), "ctx", -1)
@@ -136,11 +116,35 @@
             kv_total = kv_total + passed_along(part.astype(jnp.bfloat16), "ctx", -distance)
     grad_q = lax.all_to_all(
         dq.astype(jnp.bfloat16)[:, None], "head", split_axis=0, concat_axis=1, tiled=True
-    ).reshape(rows_in, heads_ax * q_cols)
+    )
     kv_out = jnp.moveaxis(kv_total.astype(jnp.bfloat16), 0, 1)[:, None]
     kv_back = lax.all_to_all(kv_out, "head", split_axis=0, concat_axis=1, tiled=True)
-    grad_k = kv_back[:, :, 0].reshape(rows_in, heads_ax * kv_cols)
-    grad_v = kv_back[:, :, 1].reshape(rows_in, heads_ax * kv_cols)
+    return grad_q, kv_back
+
+
+def local(queries, normed_key_state, value_state_rows, output_gradient, doc_start):
+    heads_ax = lax.axis_size("head")
+    rows_in = queries.shape[0]
+    tok_rows = doc_start.shape[0]
+    kv_cols = normed_key_state.shape[1] // (heads_ax * CHUNKS)
+    q_cols = queries.shape[1] // (heads_ax * CHUNKS)
+    keys = normed_key_state.reshape(rows_in, heads_ax, CHUNKS, kv_cols)
+    values = value_state_rows.reshape(rows_in, heads_ax, CHUNKS, kv_cols)
+    qs = queries.reshape(rows_in, heads_ax, CHUNKS, q_cols)
+    gs = output_gradient.reshape(rows_in, heads_ax, CHUNKS, q_cols)
+    shard_index = lax.axis_index("ctx")
+    rel = (doc_start - shard_index * tok_rows).reshape(tok_rows, 1)
+    dq_parts, dkv_parts = [], []
+    for chunk in range(CHUNKS):
+        kv_in = jnp.stack([keys[:, :, chunk], values[:, :, chunk]], axis=2)
+        qg_in = jnp.stack([qs[:, :, chunk], gs[:, :, chunk]], axis=2)
+        dq, dkv = chunk_pass(kv_in, qg_in, rel)
+        dq_parts.append(dq)
+        dkv_parts.append(dkv)
+    grad_q = jnp.stack(dq_parts, axis=2).reshape(rows_in, heads_ax * CHUNKS * q_cols)
+    dkv = jnp.stack(dkv_parts, axis=3)
+    grad_k = dkv[:, :, 0].reshape(rows_in, heads_ax * CHUNKS * kv_cols)
+    grad_v = dkv[:, :, 1].reshape(rows_in, heads_ax * CHUNKS * kv_cols)
     return grad_q, grad_k, grad_v
 
 

time: 184 us -> 172 us (0.935)
  the two profiles are of different devices: /device:TPU:182 before, /device:TPU:312 now
where the time goes in v4:
time: 172 us; the launch traced here: 171 us
  waiting for transfers between devices  67.3 us (39%)
  starting transfers between devices  57.3 us (33%)
  local copies, waits for them, and re-layouts  23.7 us (14%)
  Pallas kernels  12.4 us (7%)
  other arithmetic  9.26 us (5%)
    all_to_all x2, waiting for transfers between devices, chunk_pass(): lax.all_to_all(dq.astype(jnp.bfloat16)[:, None], 'head', split_axis=0, co...  41.3 us
    ppermute x8, starting transfers between devices, passed_along(): return lax.ppermute(block, axis, route)  29.7 us
    pallas_call x2, Pallas kernels, attend(): pl.pallas_call(attn_kernel, grid=(groups,), in_specs=[pl.BlockSpec((tok,...  12.4 us
    all_to_all x2, waiting for transfers between devices, chunk_pass(): lax.all_to_all(kv_out, 'head', split_axis=0, concat_axis=1, tiled=True)  8.38 us
    all_to_all x2, starting transfers between devices, chunk_pass(): lax.all_to_all(dq.astype(jnp.bfloat16)[:, None], 'head', split_axis=0, co...  6.99 us
    all_to_all x2, starting transfers between devices, chunk_pass(): lax.all_to_all(qg_in, 'head', split_axis=1, concat_axis=0, tiled=True)  6.94 us
    all_to_all x2, starting transfers between devices, chunk_pass(): lax.all_to_all(kv_out, 'head', split_axis=0, concat_axis=1, tiled=True)  6.81 us
    all_to_all x2, starting transfers between devices, chunk_pass(): lax.all_to_all(kv_in, 'head', split_axis=1, concat_axis=0, tiled=True)  6.81 us
  transfers between devices with their start and end apart: 16, of which 8 were waited for; matrix products, arithmetic and copies ran while one was open for 13% of the time, Pallas kernels for 7%

profile of v4, /device:TPU:312, one launch (start us, length us, event | category | flops | bytes accessed | tf_op | source)
XLA Modules:
  0.0 171.2 jit_solution(6851727173595462358)
XLA Ops:
  0.6 1.2 reshape.33
  4.1 3.4 %all-to-all-start.1 = ((bf16[64,4,2,256]{3,0,2,1:T(8,128)(2,1)}), bf16[64,4,2,256]{3,0,2,1:T(8,128)(2,1)S(1)}, u32[]{:S(2)}, u32[]{:S(2)}) async-start(bf16[64,4,2,256]{3,0,2,1:T(8,128)(2,1)} %copy.63), calls=%async_computation.1 | async-start | bytes 524288 | tf_op jit(solution)/shard_map/all_to_all | solution.py:99
  10.3 3.2 %all-to-all-done.1 = bf16[64,4,2,256]{3,0,2,1:T(8,128)(2,1)S(1)} async-done(((bf16[64,4,2,256]{3,0,2,1:T(8,128)(2,1)}), bf16[64,4,2,256]{3,0,2,1:T(8,128)(2,1)S(1)}, u32[]{:S(2)}, u32[]{:S(2)}) %all-to-all-start.1) | async-done | bytes 262176 | tf_op jit(solution)/shard_map/all_to_all | solution.py:99
  13.5 3.4 %all-to-all-start.4 = ((bf16[64,4,2,256]{3,0,2,1:T(8,128)(2,1)}), bf16[64,4,2,256]{3,0,2,1:T(8,128)(2,1)S(1)}, u32[]{:S(2)}, u32[]{:S(2)}) async-start(bf16[64,4,2,256]{3,0,2,1:T(8,128)(2,1)} %copy.69), calls=%async_computation.4 | async-start | bytes 524288 | tf_op jit(solution)/shard_map/all_to_all | solution.py:99
  16.9 1.5 fusion.2
  18.5 1.2 pad_maximum_fusion.2
  19.7 0.9 copy.67
  20.6 2.3 %all-to-all-done.4 = bf16[64,4,2,256]{3,0,2,1:T(8,128)(2,1)S(1)} async-done(((bf16[64,4,2,256]{3,0,2,1:T(8,128)(2,1)}), bf16[64,4,2,256]{3,0,2,1:T(8,128)(2,1)S(1)}, u32[]{:S(2)}, u32[]{:S(2)}) %all-to-all-start.4) | async-done | bytes 262176 | tf_op jit(solution)/shard_map/all_to_all | solution.py:99
  22.9 3.5 %all-to-all-start.3 = ((bf16[64,4,2,512]{3,0,2,1:T(8,128)(2,1)}), bf16[64,4,2,512]{3,0,2,1:T(8,128)(2,1)S(1)}, u32[]{:S(2)}, u32[]{:S(2)}) async-start(bf16[64,4,2,512]{3,0,2,1:T(8,128)(2,1)} %copy.67), calls=%async_computation.3 | async-start | bytes 1048576 | tf_op jit(solution)/shard_map/all_to_all | solution.py:107
  26.4 1.2 pad_maximum_fusion.1
  27.6 1.0 copy.61
  28.6 6.6 %all-to-all-done.3 = bf16[64,4,2,512]{3,0,2,1:T(8,128)(2,1)S(1)} async-done(((bf16[64,4,2,512]{3,0,2,1:T(8,128)(2,1)}), bf16[64,4,2,512]{3,0,2,1:T(8,128)(2,1)S(1)}, u32[]{:S(2)}, u32[]{:S(2)}) %all-to-all-start.3) | async-done | bytes 524320 | tf_op jit(solution)/shard_map/all_to_all | solution.py:107
  35.2 3.5 %all-to-all-start = ((bf16[64,4,2,512]{3,0,2,1:T(8,128)(2,1)}), bf16[64,4,2,512]{3,0,2,1:T(8,128)(2,1)S(1)}, u32[]{:S(2)}, u32[]{:S(2)}) async-start(bf16[64,4,2,512]{3,0,2,1:T(8,128)(2,1)} %copy.61), calls=%async_computation | async-start | bytes 1048576 | tf_op jit(solution)/shard_map/all_to_all | solution.py:107
  38.7 3.7 %collective-permute-start.3 = (bf16[2,256,256]{2,1,0:T(8,128)(2,1)S(1)}, bf16[2,256,256]{2,1,0:T(8,128)(2,1)S(1)}, u32[]{:S(2)}, u32[]{:S(2)}) collective-permute-start(bf16[2,256,256]{2,1,0:T(8,128)(2,1)S(1)} %bitcast.73), channel_id=1, source_target_pairs={{0,8},{4,12},{8,16},{12,20},{16,24},{20,28},{24,32},{28,36},{32,40... | collective-permute-start | bytes 786440 | tf_op jit(solution)/shard_map/ppermute | solution.py:95
  42.5 3.5 %collective-permute-start.2 = (bf16[2,256,256]{2,1,0:T(8,128)(2,1)S(1)}, bf16[2,256,256]{2,1,0:T(8,128)(2,1)S(1)}, u32[]{:S(2)}, u32[]{:S(2)}) collective-permute-start(bf16[2,256,256]{2,1,0:T(8,128)(2,1)S(1)} %bitcast.74), channel_id=1, source_target_pairs={{0,4},{4,8},{8,12},{12,16},{16,20},{20,24},{24,28},{28,32},{32,36}... | collective-permute-start | bytes 786440 | tf_op jit(solution)/shard_map/ppermute | solution.py:95
  46.0 0.8 copy.65.rel_ref
  46.8 5.7 %collective-permute-start.1 = (bf16[2,256,256]{2,1,0:T(8,128)(2,1)S(1)}, bf16[2,256,256]{2,1,0:T(8,128)(2,1)S(1)}, u32[]{:S(2)}, u32[]{:S(2)}) collective-permute-start(bf16[2,256,256]{2,1,0:T(8,128)(2,1)S(1)} %bitcast.69), channel_id=1, source_target_pairs={{0,8},{4,12},{8,16},{12,20},{16,24},{20,28},{24,32},{28,36},{32,40... | collective-permute-start | bytes 786440 | tf_op jit(solution)/shard_map/ppermute | solution.py:95
  52.5 2.6 %collective-permute-start = (bf16[2,256,256]{2,1,0:T(8,128)(2,1)S(1)}, bf16[2,256,256]{2,1,0:T(8,128)(2,1)S(1)}, u32[]{:S(2)}, u32[]{:S(2)}) collective-permute-start(bf16[2,256,256]{2,1,0:T(8,128)(2,1)S(1)} %bitcast.70), channel_id=1, source_target_pairs={{0,4},{4,8},{8,12},{12,16},{16,20},{20,24},{24,28},{28,32},{32,36}... | collective-permute-start | bytes 786440 | tf_op jit(solution)/shard_map/ppermute | solution.py:95
  55.2 0.8 slice_bitcast_fusion
  56.4 5.1 %collective-permute-done.2.kv1_ref = bf16[2,256,256]{2,1,0:T(8,128)(2,1)S(1)} collective-permute-done((bf16[2,256,256]{2,1,0:T(8,128)(2,1)S(1)}, bf16[2,256,256]{2,1,0:T(8,128)(2,1)S(1)}, u32[]{:S(2)}, u32[]{:S(2)}) %collective-permute-start.2) | collective-permute-done | bytes 262176 | tf_op jit(solution)/shard_map/ppermute | solution.py:95
  62.2 6.2 %shard_map.77 = (f32[256,512]{1,0:T(8,128)}, f32[2,256,256]{2,1,0:T(8,128)}, f32[2,256,256]{2,1,0:T(8,128)}, f32[2,256,256]{2,1,0:T(8,128)}) custom-call(s32[256,1]{1,0:T(8,128)} %copy.65.rel_ref, bf16[256,512]{1,0:T(8,128)(2,1)} %get-tuple-element.28.q_ref, bf16[256,512]{1,0:T(8,128)(2,1)} %get-tuple-element.27.g_ref, bf16[2,256,256]{2,1,0:T(8,128)(2,1)} %bitcast.75, ...), custom_call_target="tpu_custom_call" | custom-call | tf_op jit(solution)/shard_map/pallas_call | solution.py:78
  68.5 1.1 convert_bitcast_fusion
  70.1 0.8 reduce
  70.9 0.9 reshape.36
  71.8 3.6 %all-to-all-start.5 = ((bf16[4,2,16384]{2,1,0:T(2,128)(2,1)}), bf16[4,2,16384]{2,1,0:T(2,128)(2,1)S(1)}, u32[]{:S(2)}, u32[]{:S(2)}) async-start(bf16[4,2,16384]{2,1,0:T(2,128)(2,1)} %reshape.36), calls=%async_computation.5 | async-start | bytes 524288 | tf_op jit(solution)/shard_map/all_to_all | solution.py:117
  75.4 1.0 copy-done.2
  76.4 3.7 %collective-permute-start.7 = (bf16[2,256,256]{2,1,0:T(8,128)(2,1)S(1)}, bf16[2,256,256]{2,1,0:T(8,128)(2,1)S(1)}, u32[]{:S(2)}, u32[]{:S(2)}) collective-permute-start(bf16[2,256,256]{2,1,0:T(8,128)(2,1)S(1)} %convert_element_type.45), channel_id=1, source_target_pairs={{8,0},{12,4},{16,8},{20,12},{24,16},{28,20},{32,24},{36,28},{40,32... | collective-permute-start | bytes 786440 | tf_op jit(solution)/shard_map/ppermute | solution.py:95
  80.2 5.1 %collective-permute-start.6 = (bf16[2,256,256]{2,1,0:T(8,128)(2,1)S(1)}, bf16[2,256,256]{2,1,0:T(8,128)(2,1)S(1)}, u32[]{:S(2)}, u32[]{:S(2)}) collective-permute-start(bf16[2,256,256]{2,1,0:T(8,128)(2,1)S(1)} %convert_element_type.43), channel_id=1, source_target_pairs={{4,0},{8,4},{12,8},{16,12},{20,16},{24,20},{28,24},{32,28},{36,32}... | collective-permute-start | bytes 786440 | tf_op jit(solution)/shard_map/ppermute | solution.py:95
  85.3 0.8 slice_bitcast_fusion.2
  86.9 6.2 %shard_map.76 = (f32[256,512]{1,0:T(8,128)}, f32[2,256,256]{2,1,0:T(8,128)}, f32[2,256,256]{2,1,0:T(8,128)}, f32[2,256,256]{2,1,0:T(8,128)}) custom-call(s32[256,1]{1,0:T(8,128)} %copy.65.rel_ref, bf16[256,512]{1,0:T(8,128)(2,1)} %get-tuple-element.22.q_ref, bf16[256,512]{1,0:T(8,128)(2,1)} %get-tuple-element.21.g_ref, bf16[2,256,256]{2,1,0:T(8,128)(2,1)} %bitcast.71, ...), custom_call_target="tpu_custom_call" | custom-call | tf_op jit(solution)/shard_map/pallas_call | solution.py:78
  93.1 1.1 convert_bitcast_fusion.1
  94.2 0.8 reduce.1
  95.0 0.9 reshape.38
  95.9 3.4 %all-to-all-start.2 = ((bf16[4,2,16384]{2,1,0:T(2,128)(2,1)}), bf16[4,2,16384]{2,1,0:T(2,128)(2,1)S(1)}, u32[]{:S(2)}, u32[]{:S(2)}) async-start(bf16[4,2,16384]{2,1,0:T(2,128)(2,1)} %reshape.38), calls=%async_computation.2 | async-start | bytes 524288 | tf_op jit(solution)/shard_map/all_to_all | solution.py:117
  99.4 1.0 copy-done.4
  101.1 2.2 %collective-permute-start.5 = (bf16[2,256,256]{2,1,0:T(8,128)(2,1)}, bf16[2,256,256]{2,1,0:T(8,128)(2,1)S(1)}, u32[]{:S(2)}, u32[]{:S(2)}) collective-permute-start(bf16[2,256,256]{2,1,0:T(8,128)(2,1)} %convert_element_type.40), channel_id=1, source_target_pairs={{8,0},{12,4},{16,8},{20,12},{24,16},{28,20},{32,24},{36,28},{40,32... | collective-permute-start | bytes 786440 | tf_op jit(solution)/shard_map/ppermute | solution.py:95
  103.3 3.1 %collective-permute-start.4 = (bf16[2,256,256]{2,1,0:T(8,128)(2,1)S(1)}, bf16[2,256,256]{2,1,0:T(8,128)(2,1)S(1)}, u32[]{:S(2)}, u32[]{:S(2)}) collective-permute-start(bf16[2,256,256]{2,1,0:T(8,128)(2,1)S(1)} %convert_element_type.38), channel_id=1, source_target_pairs={{4,0},{8,4},{12,8},{16,12},{20,16},{24,20},{28,24},{32,28},{36,32}... | collective-permute-start | bytes 786440 | tf_op jit(solution)/shard_map/ppermute | solution.py:95
  106.6 1.0 copy.75
  107.6 41.3 %all-to-all-done.2 = bf16[4,2,16384]{2,1,0:T(2,128)(2,1)S(1)} async-done(((bf16[4,2,16384]{2,1,0:T(2,128)(2,1)}), bf16[4,2,16384]{2,1,0:T(2,128)(2,1)S(1)}, u32[]{:S(2)}, u32[]{:S(2)}) %all-to-all-start.2) | async-done | bytes 262176 | tf_op jit(solution)/shard_map/all_to_all | solution.py:117
  148.9 3.4 %all-to-all-start.7 = ((bf16[256,1,2,256]{3,2,1,0:T(2,128)(2,1)}), bf16[256,1,2,256]{3,2,1,0:T(2,128)(2,1)S(1)}, u32[]{:S(2)}, u32[]{:S(2)}) async-start(bf16[256,1,2,256]{3,2,1,0:T(2,128)(2,1)} %copy.75), calls=%async_computation.7 | async-start | bytes 524288 | tf_op jit(solution)/shard_map/all_to_all | solution.py:121
  152.4 1.0 copy.74
  153.4 4.9 %all-to-all-done.7 = bf16[256,1,2,256]{3,2,1,0:T(2,128)(2,1)S(1)} async-done(((bf16[256,1,2,256]{3,2,1,0:T(2,128)(2,1)}), bf16[256,1,2,256]{3,2,1,0:T(2,128)(2,1)S(1)}, u32[]{:S(2)}, u32[]{:S(2)}) %all-to-all-start.7) | async-done | bytes 262176 | tf_op jit(solution)/shard_map/all_to_all | solution.py:121
  158.3 3.4 %all-to-all-start.6 = ((bf16[256,1,2,256]{3,2,1,0:T(2,128)(2,1)}), bf16[256,1,2,256]{3,2,1,0:T(2,128)(2,1)S(1)}, u32[]{:S(2)}, u32[]{:S(2)}) async-start(bf16[256,1,2,256]{3,2,1,0:T(2,128)(2,1)} %copy.74), calls=%async_computation.6 | async-start | bytes 524288 | tf_op jit(solution)/shard_map/all_to_all | solution.py:121
  163.0 1.2 reshape.35
  164.1 3.5 %all-to-all-done.6 = bf16[256,1,2,256]{3,2,1,0:T(2,128)(2,1)S(1)} async-done(((bf16[256,1,2,256]{3,2,1,0:T(2,128)(2,1)}), bf16[256,1,2,256]{3,2,1,0:T(2,128)(2,1)S(1)}, u32[]{:S(2)}, u32[]{:S(2)}) %all-to-all-start.6) | async-done | bytes 262176 | tf_op jit(solution)/shard_map/all_to_all | solution.py:121
  167.6 0.9 pad_maximum_fusion
  169.0 0.9 reshape_squeeze.7
  170.3 0.9 reshape_squeeze.6
  (67 shorter events, 10.7 us)
Async XLA Ops:
  0.6 1.2 copy-start.10
  3.4 4.2 %copy-start.6 = (bf16[64,4096]{1,0:T(8,128)(2,1)S(1)}, bf16[64,4096]{1,0:T(8,128)(2,1)}, u32[]{:S(2)}) copy-start(bf16[64,4096]{1,0:T(8,128)(2,1)} %param.5) | copy-start | bytes 1572868
  4.1 9.4 %all-to-all-start.1 = ((bf16[64,4,2,256]{3,0,2,1:T(8,128)(2,1)}), bf16[64,4,2,256]{3,0,2,1:T(8,128)(2,1)S(1)}, u32[]{:S(2)}, u32[]{:S(2)}) async-start(bf16[64,4,2,256]{3,0,2,1:T(8,128)(2,1)} %copy.63), calls=%async_computation.1 | async-start | bytes 524288 | tf_op jit(solution)/shard_map/all_to_all | solution.py:99
  7.6 1.0 copy-start.7
  13.5 9.4 %all-to-all-start.4 = ((bf16[64,4,2,256]{3,0,2,1:T(8,128)(2,1)}), bf16[64,4,2,256]{3,0,2,1:T(8,128)(2,1)S(1)}, u32[]{:S(2)}, u32[]{:S(2)}) async-start(bf16[64,4,2,256]{3,0,2,1:T(8,128)(2,1)} %copy.69), calls=%async_computation.4 | async-start | bytes 524288 | tf_op jit(solution)/shard_map/all_to_all | solution.py:99
  22.9 12.3 %all-to-all-start.3 = ((bf16[64,4,2,512]{3,0,2,1:T(8,128)(2,1)}), bf16[64,4,2,512]{3,0,2,1:T(8,128)(2,1)S(1)}, u32[]{:S(2)}, u32[]{:S(2)}) async-start(bf16[64,4,2,512]{3,0,2,1:T(8,128)(2,1)} %copy.67), calls=%async_computation.3 | async-start | bytes 1048576 | tf_op jit(solution)/shard_map/all_to_all | solution.py:107
  35.2 34.4 %all-to-all-start = ((bf16[64,4,2,512]{3,0,2,1:T(8,128)(2,1)}), bf16[64,4,2,512]{3,0,2,1:T(8,128)(2,1)S(1)}, u32[]{:S(2)}, u32[]{:S(2)}) async-start(bf16[64,4,2,512]{3,0,2,1:T(8,128)(2,1)} %copy.61), calls=%async_computation | async-start | bytes 1048576 | tf_op jit(solution)/shard_map/all_to_all | solution.py:107
  38.7 8.1 %copy-start.1 = (bf16[4,64,1,2,256]{4,1,0,3,2:T(8,128)(2,1)}, bf16[4,64,1,2,256]{4,1,0,3,2:T(8,128)(2,1)S(1)}, u32[]{:S(2)}) copy-start(bf16[4,64,1,2,256]{4,1,0,3,2:T(8,128)(2,1)S(1)} %copy.70) | copy-start | bytes 786436
  38.7 7.3 %copy-start.15 = (s32[256]{0:T(256)S(1)}, s32[256]{0:T(256)}, u32[]{:S(2)}) copy-start(s32[256]{0:T(256)} %param.9) | copy-start | bytes 3076
  38.7 17.7 %collective-permute-start.3 = (bf16[2,256,256]{2,1,0:T(8,128)(2,1)S(1)}, bf16[2,256,256]{2,1,0:T(8,128)(2,1)S(1)}, u32[]{:S(2)}, u32[]{:S(2)}) collective-permute-start(bf16[2,256,256]{2,1,0:T(8,128)(2,1)S(1)} %bitcast.73), channel_id=1, source_target_pairs={{0,8},{4,12},{8,16},{12,20},{16,24},{20,28},{24,32},{28,36},{32,40... | collective-permute-start | bytes 786440 | tf_op jit(solution)/shard_map/ppermute | solution.py:95
  42.5 19.1 %collective-permute-start.2 = (bf16[2,256,256]{2,1,0:T(8,128)(2,1)S(1)}, bf16[2,256,256]{2,1,0:T(8,128)(2,1)S(1)}, u32[]{:S(2)}, u32[]{:S(2)}) collective-permute-start(bf16[2,256,256]{2,1,0:T(8,128)(2,1)S(1)} %bitcast.74), channel_id=1, source_target_pairs={{0,4},{4,8},{8,12},{12,16},{16,20},{20,24},{24,28},{28,32},{32,36}... | collective-permute-start | bytes 786440 | tf_op jit(solution)/shard_map/ppermute | solution.py:95
  46.8 8.4 %copy-start = (bf16[4,64,1,2,256]{4,1,0,3,2:T(8,128)(2,1)}, bf16[4,64,1,2,256]{4,1,0,3,2:T(8,128)(2,1)S(1)}, u32[]{:S(2)}) copy-start(bf16[4,64,1,2,256]{4,1,0,3,2:T(8,128)(2,1)S(1)} %copy.64) | copy-start | bytes 786436
  46.8 39.3 %collective-permute-start.1 = (bf16[2,256,256]{2,1,0:T(8,128)(2,1)S(1)}, bf16[2,256,256]{2,1,0:T(8,128)(2,1)S(1)}, u32[]{:S(2)}, u32[]{:S(2)}) collective-permute-start(bf16[2,256,256]{2,1,0:T(8,128)(2,1)S(1)} %bitcast.69), channel_id=1, source_target_pairs={{0,8},{4,12},{8,16},{12,20},{16,24},{20,28},{24,32},{28,36},{32,40... | collective-permute-start | bytes 786440 | tf_op jit(solution)/shard_map/ppermute | solution.py:95
  52.5 33.6 %collective-permute-start = (bf16[2,256,256]{2,1,0:T(8,128)(2,1)S(1)}, bf16[2,256,256]{2,1,0:T(8,128)(2,1)S(1)}, u32[]{:S(2)}, u32[]{:S(2)}) collective-permute-start(bf16[2,256,256]{2,1,0:T(8,128)(2,1)S(1)} %bitcast.70), channel_id=1, source_target_pairs={{0,4},{4,8},{8,12},{12,16},{16,20},{20,24},{24,28},{28,32},{32,36}... | collective-permute-start | bytes 786440 | tf_op jit(solution)/shard_map/ppermute | solution.py:95
  56.4 5.1 %copy-start.13 = (bf16[2,256,256]{2,1,0:T(8,128)(2,1)}, bf16[2,256,256]{2,1,0:T(8,128)(2,1)S(1)}, u32[]{:S(2)}) copy-start(bf16[2,256,256]{2,1,0:T(8,128)(2,1)S(1)} %collective-permute-done.3.kv2_ref) | copy-start | bytes 786436
  61.5 0.7 copy-start.14
  70.9 4.5 %copy-start.3 = (f32[2,256,256]{2,1,0:T(8,128)S(1)}, f32[2,256,256]{2,1,0:T(8,128)}, u32[]{:S(2)}) copy-start(f32[2,256,256]{2,1,0:T(8,128)} %get-tuple-element.17) | copy-start | bytes 1572868
  71.8 24.1 %all-to-all-start.5 = ((bf16[4,2,16384]{2,1,0:T(2,128)(2,1)}), bf16[4,2,16384]{2,1,0:T(2,128)(2,1)S(1)}, u32[]{:S(2)}, u32[]{:S(2)}) async-start(bf16[4,2,16384]{2,1,0:T(2,128)(2,1)} %reshape.36), calls=%async_computation.5 | async-start | bytes 524288 | tf_op jit(solution)/shard_map/all_to_all | solution.py:117
  75.4 1.0 copy-start.2
  76.4 30.0 %collective-permute-start.7 = (bf16[2,256,256]{2,1,0:T(8,128)(2,1)S(1)}, bf16[2,256,256]{2,1,0:T(8,128)(2,1)S(1)}, u32[]{:S(2)}, u32[]{:S(2)}) collective-permute-start(bf16[2,256,256]{2,1,0:T(8,128)(2,1)S(1)} %convert_element_type.45), channel_id=1, source_target_pairs={{8,0},{12,4},{16,8},{20,12},{24,16},{28,20},{32,24},{36,28},{40,32... | collective-permute-start | bytes 786440 | tf_op jit(solution)/shard_map/ppermute | solution.py:95
  80.2 26.3 %collective-permute-start.6 = (bf16[2,256,256]{2,1,0:T(8,128)(2,1)S(1)}, bf16[2,256,256]{2,1,0:T(8,128)(2,1)S(1)}, u32[]{:S(2)}, u32[]{:S(2)}) collective-permute-start(bf16[2,256,256]{2,1,0:T(8,128)(2,1)S(1)} %convert_element_type.43), channel_id=1, source_target_pairs={{4,0},{8,4},{12,8},{16,12},{20,16},{24,20},{28,24},{32,28},{36,32}... | collective-permute-start | bytes 786440 | tf_op jit(solution)/shard_map/ppermute | solution.py:95
  86.1 0.7 copy-start.11
  86.2 0.8 copy-start.12
  95.0 4.3 %copy-start.5 = (f32[2,256,256]{2,1,0:T(8,128)S(1)}, f32[2,256,256]{2,1,0:T(8,128)}, u32[]{:S(2)}) copy-start(f32[2,256,256]{2,1,0:T(8,128)} %get-tuple-element.14) | copy-start | bytes 1572868
  95.9 53.0 %all-to-all-start.2 = ((bf16[4,2,16384]{2,1,0:T(2,128)(2,1)}), bf16[4,2,16384]{2,1,0:T(2,128)(2,1)S(1)}, u32[]{:S(2)}, u32[]{:S(2)}) async-start(bf16[4,2,16384]{2,1,0:T(2,128)(2,1)} %reshape.38), calls=%async_computation.2 | async-start | bytes 524288 | tf_op jit(solution)/shard_map/all_to_all | solution.py:117
  99.3 1.0 copy-start.4
  99.4 7.1 %copy-start.8 = (f32[2,256,256]{2,1,0:T(8,128)S(1)}, f32[2,256,256]{2,1,0:T(8,128)}, u32[]{:S(2)}) copy-start(f32[2,256,256]{2,1,0:T(8,128)} %get-tuple-element.16) | copy-start | bytes 1572868
  101.1 51.2 %collective-permute-start.5 = (bf16[2,256,256]{2,1,0:T(8,128)(2,1)}, bf16[2,256,256]{2,1,0:T(8,128)(2,1)S(1)}, u32[]{:S(2)}, u32[]{:S(2)}) collective-permute-start(bf16[2,256,256]{2,1,0:T(8,128)(2,1)} %convert_element_type.40), channel_id=1, source_target_pairs={{8,0},{12,4},{16,8},{20,12},{24,16},{28,20},{32,24},{36,28},{40,32... | collective-permute-start | bytes 786440 | tf_op jit(solution)/shard_map/ppermute | solution.py:95
  103.3 49.0 %collective-permute-start.4 = (bf16[2,256,256]{2,1,0:T(8,128)(2,1)S(1)}, bf16[2,256,256]{2,1,0:T(8,128)(2,1)S(1)}, u32[]{:S(2)}, u32[]{:S(2)}) collective-permute-start(bf16[2,256,256]{2,1,0:T(8,128)(2,1)S(1)} %convert_element_type.38), channel_id=1, source_target_pairs={{4,0},{8,4},{12,8},{16,12},{20,16},{24,20},{28,24},{32,28},{36,32}... | collective-permute-start | bytes 786440 | tf_op jit(solution)/shard_map/ppermute | solution.py:95
  106.6 45.7 %copy-start.9 = (f32[2,256,256]{2,1,0:T(8,128)S(1)}, f32[2,256,256]{2,1,0:T(8,128)}, u32[]{:S(2)}) copy-start(f32[2,256,256]{2,1,0:T(8,128)} %get-tuple-element.13) | copy-start | bytes 1572868
  148.9 9.4 %all-to-all-start.7 = ((bf16[256,1,2,256]{3,2,1,0:T(2,128)(2,1)}), bf16[256,1,2,256]{3,2,1,0:T(2,128)(2,1)S(1)}, u32[]{:S(2)}, u32[]{:S(2)}) async-start(bf16[256,1,2,256]{3,2,1,0:T(2,128)(2,1)} %copy.75), calls=%async_computation.7 | async-start | bytes 524288 | tf_op jit(solution)/shard_map/all_to_all | solution.py:121
  158.3 9.4 %all-to-all-start.6 = ((bf16[256,1,2,256]{3,2,1,0:T(2,128)(2,1)}), bf16[256,1,2,256]{3,2,1,0:T(2,128)(2,1)S(1)}, u32[]{:S(2)}, u32[]{:S(2)}) async-start(bf16[256,1,2,256]{3,2,1,0:T(2,128)(2,1)} %copy.74), calls=%async_computation.6 | async-start | bytes 524288 | tf_op jit(solution)/shard_map/all_to_all | solution.py:121

commit v5 on v3

--- a/solution.py
+++ b/solution.py
@@ -16,9 +16,8 @@
 TN = (((0,), (0,)), ((), ()))
 
 
-def attn_kernel(rel_ref, q_ref, g_ref, kv0_ref, kv1_ref, kv2_ref, dq_ref, dkv0_ref, dkv1_ref, dkv2_ref):
+def attn_kernel(rel_ref, q_ref, g_ref, k0_ref, v0_ref, k1_ref, v1_ref, k2_ref, v2_ref, dq_ref, dkv0_ref, dkv1_ref, dkv2_ref):
     tok = q_ref.shape[0]
-    kv_refs = (kv0_ref, kv1_ref, kv2_ref)
     dkv_refs = (dkv0_ref, dkv1_ref, dkv2_ref)
     share = q_ref.shape[1] // HEAD_SIZE
     row = lax.broadcasted_iota(jnp.int32, (tok, tok), 0)
@@ -28,8 +27,8 @@
     for d in range(3):
         key_rel = col - tok * d
         masks.append((key_rel >= rel) & (key_rel <= row) & (row - key_rel < WINDOW))
-    keys = [r[0] for r in kv_refs]
-    vals = [r[1] for r in kv_refs]
+    keys = [k0_ref[...], k1_ref[...], k2_ref[...]]
+    vals = [v0_ref[...], v1_ref[...], v2_ref[...]]
     dk = [jnp.zeros((tok, HEAD_SIZE), jnp.float32) for _ in range(3)]
     dv = [jnp.zeros((tok, HEAD_SIZE), jnp.float32) for _ in range(3)]
     for j in range(share):
@@ -67,25 +66,36 @@
         dkv_refs[d][1] = dv[d]
 
 
-def attend(rel, qh, gh, kv_blocks):
-    tok, qcols = qh.shape
-    kvcols = kv_blocks[0].shape[-1]
+def attend(rel, x_all, kv_blocks):
+    tok = x_all.shape[0]
+    kvcols = kv_blocks[0].shape[1] // 2
     groups = kvcols // HEAD_SIZE
-    qblk = qcols // groups
+    qblk = 2 * kvcols // groups
+    col = lambda off: pl.BlockSpec((tok, HEAD_SIZE), lambda g: (0, off + g))
+    qcol = lambda off: pl.BlockSpec((tok, qblk), lambda g: (0, off + g))
     kv_spec = pl.BlockSpec((2, tok, HEAD_SIZE), lambda g: (0, 0, g))
-    q_spec = pl.BlockSpec((tok, qblk), lambda g: (0, g))
     return pl.pallas_call(
         attn_kernel,
         grid=(groups,),
-        in_specs=[pl.BlockSpec((tok, 1), lambda g: (0, 0)), q_spec, q_spec, kv_spec, kv_spec, kv_spec],
-        out_specs=[q_spec, kv_spec, kv_spec, kv_spec],
+        in_specs=[
+            pl.BlockSpec((tok, 1), lambda g: (0, 0)),
+            qcol(2 * kvcols // qblk),
+            qcol(4 * kvcols // qblk),
+            col(0),
+            col(groups),
+            col(0),
+            col(groups),
+            col(0),
+            col(groups),
+        ],
+        out_specs=[pl.BlockSpec((tok, qblk), lambda g: (0, g)), kv_spec, kv_spec, kv_spec],
         out_shape=[
-            jax.ShapeDtypeStruct((tok, qcols), jnp.float32),
+            jax.ShapeDtypeStruct((tok, 2 * kvcols), jnp.float32),
             jax.ShapeDtypeStruct((2, tok, kvcols), jnp.float32),
             jax.ShapeDtypeStruct((2, tok, kvcols), jnp.float32),
             jax.ShapeDtypeStruct((2, tok, kvcols), jnp.float32),
         ],
-    )(rel, qh, gh, *kv_blocks)
+    )(rel, x_all, x_all, x_all, x_all, kv_blocks[0], kv_blocks[0], kv_blocks[1], kv_blocks[1])
 
 
 def passed_along(block, axis, distance):
@@ -97,35 +107,30 @@
 def local(queries, normed_key_state, value_state_rows, output_gradient, doc_start):
     heads_ax = lax.axis_size("head")
     rows_in = queries.shape[0]
+    tok_rows = doc_start.shape[0]
     kv_cols = normed_key_state.shape[1] // heads_ax
     q_cols = queries.shape[1] // heads_ax
-    kv_in = jnp.stack(
+    x_in = jnp.concatenate(
         [
             normed_key_state.reshape(rows_in, heads_ax, kv_cols),
             value_state_rows.reshape(rows_in, heads_ax, kv_cols),
-        ],
-        axis=2,
-    )
-    kv_all = lax.all_to_all(kv_in, "head", split_axis=1, concat_axis=0, tiled=True)
-    tok_rows = kv_all.shape[0]
-    kv_local = jnp.moveaxis(kv_all[:, 0], 1, 0)
-    kv_blocks = [kv_local]
-    for distance in range(1, SPAN + 1):
-        if CHAIN:
-            kv_blocks.append(passed_along(kv_blocks[-1], "ctx", 1))
-        else:
-            kv_blocks.append(passed_along(kv_local, "ctx", distance))
-    qg_in = jnp.stack(
-        [
             queries.reshape(rows_in, heads_ax, q_cols),
             output_gradient.reshape(rows_in, heads_ax, q_cols),
         ],
         axis=2,
     )
-    qg_all = lax.all_to_all(qg_in, "head", split_axis=1, concat_axis=0, tiled=True)
+    x_all = lax.all_to_all(x_in, "head", split_axis=1, concat_axis=0, tiled=True)
+    x_all = x_all.reshape(tok_rows, 2 * kv_cols + 2 * q_cols)
+    kv_local = x_all[:, : 2 * kv_cols]
+    if CHAIN:
+        kv1 = passed_along(kv_local, "ctx", 1)
+        kv2 = passed_along(kv1, "ctx", 1)
+    else:
+        kv1 = passed_along(kv_local, "ctx", 1)
+        kv2 = passed_along(kv_local, "ctx", 2)
     shard_index = lax.axis_index("ctx")
     rel = (doc_start - shard_index * tok_rows).reshape(tok_rows, 1)
-    dq, dkv0, dkv1, dkv2 = attend(rel, qg_all[:, 0, 0], qg_all[:, 0, 1], kv_blocks)
+    dq, dkv0, dkv1, dkv2 = attend(rel, x_all, (kv1, kv2))
     if CHAIN:
         carried = passed_along(dkv2.astype(jnp.bfloat16), "ctx", -1)
         carried = passed_along((dkv1 + carried).astype(jnp.bfloat16), "ctx", -1)
@@ -134,13 +139,14 @@
         kv_total = dkv0
         for distance, part in ((1, dkv1), (2, dkv2)):
             kv_total = kv_total + passed_along(part.astype(jnp.bfloat16), "ctx", -distance)
-    grad_q = lax.all_to_all(
-        dq.astype(jnp.bfloat16)[:, None], "head", split_axis=0, concat_axis=1, tiled=True
-    ).reshape(rows_in, heads_ax * q_cols)
-    kv_out = jnp.moveaxis(kv_total.astype(jnp.bfloat16), 0, 1)[:, None]
-    kv_back = lax.all_to_all(kv_out, "head", split_axis=0, concat_axis=1, tiled=True)
-    grad_k = kv_back[:, :, 0].reshape(rows_in, heads_ax * kv_cols)
-    grad_v = kv_back[:, :, 1].reshape(rows_in, heads_ax * kv_cols)
+    out_loc = jnp.concatenate(
+        [dq.astype(jnp.bfloat16), kv_total[0].astype(jnp.bfloat16), kv_total[1].astype(jnp.bfloat16)],
+        axis=1,
+    )[:, None]
+    out = lax.all_to_all(out_loc, "head", split_axis=0, concat_axis=1, tiled=True)
+    grad_q = out[:, :, :q_cols].reshape(rows_in, heads_ax * q_cols)
+    grad_k = out[:, :, q_cols : q_cols + kv_cols].reshape(rows_in, heads_ax * kv_cols)
+    grad_v = out[:, :, q_cols + kv_cols :].reshape(rows_in, heads_ax * kv_cols)
     return grad_q, grad_k, grad_v
 
 

time: 184 us -> 188 us (1.022)
  blocking collectives: 0 us -> 40.3 us
  starting transfers between devices: 28 us -> 13 us
  waiting for transfers between devices: 121 us -> 110 us
  local copies, waits for them, and re-layouts: 16.4 us -> 8.34 us
    all_to_all x0 -> x2, blocking collectives: none -> 40.3 us  [the longest x1 23.5 us: local(): lax.all_to_all(x_in, 'head', split_axis=1, concat_axis=0, tiled=True)]
    all_to_all x4 -> x0, waiting for transfers between devices: 15 us -> none  [the longest x1 6.69 us: local(): lax.all_to_all(kv_out, 'head', split_axis=0, concat_axis=1, tiled=True)]
    all_to_all x4 -> x0, starting transfers between devices: 14.2 us -> none  [the longest x1 3.77 us: local(): lax.all_to_all(kv_in, 'head', split_axis=1, concat_axis=0, tiled=True)]
    another operation x6 -> x0, local copies, waits for them, and re-layouts: 4.31 us -> none  [the longest x3 2.25 us: local(): jnp.stack([normed_key_state.reshape(rows_in, heads_ax, kv_cols), value_st...]
    ppermute x4, waiting for transfers between devices: 106 us -> 110 us  [passed_along(): return lax.ppermute(block, axis, route)]
    reshape x0 -> x5, local copies, waits for them, and re-layouts: none -> 3.67 us  [the longest x1 1.34 us: local(): output_gradient.reshape(rows_in, heads_ax, q_cols)]
    unnamed x26 -> x21, local copies, waits for them, and re-layouts: 6.51 us -> 3.28 us
  transfers between devices with their start and end apart: 8 -> 4, of which waited for: 7 -> 4; matrix products, arithmetic and copies ran while one was open for 7% -> 1% of each run, Pallas kernels for 0% -> 0%
where the time goes in v5:
time: 188 us
  waiting for transfers between devices  110 us (59%)
  blocking collectives  40.3 us (21%)
  starting transfers between devices  13 us (7%)
  Pallas kernels  10.5 us (6%)
  local copies, waits for them, and re-layouts  8.34 us (4%)
  other arithmetic  4.68 us (2%)
    ppermute x4, waiting for transfers between devices, passed_along(): return lax.ppermute(block, axis, route)  110 us
    all_to_all x1, blocking collectives, local(): lax.all_to_all(x_in, 'head', split_axis=1, concat_axis=0, tiled=True)  23.5 us
    all_to_all x1, blocking collectives, local(): lax.all_to_all(out_loc, 'head', split_axis=0, concat_axis=1, tiled=True)  16.9 us
    ppermute x4, starting transfers between devices, passed_along(): return lax.ppermute(block, axis, route)  13 us
    pallas_call x1, Pallas kernels, attend(): pl.pallas_call(attn_kernel, grid=(groups,), in_specs=[pl.BlockSpec((tok,...  10.5 us
  transfers between devices with their start and end apart: 4, of which 4 were waited for; matrix products, arithmetic and copies ran while one was open for 1% of the time, Pallas kernels for 0%

profile of v5, /device:TPU:182, one launch (start us, length us, event | category | flops | bytes accessed | tf_op | source)
XLA Modules:
  0.0 187.7 jit_solution(10203587876845571797)
XLA Ops:
  0.6 0.0 copy-start.6
  0.6 0.0 copy-start.5
  0.7 1.3 copy_bitcast_fusion
  2.0 0.0 copy-done.6
  2.0 0.0 copy-done.5
  2.1 0.2 pad_maximum_fusion
  2.2 0.0 copy-start.7
  2.2 23.5 %all_to_all.33 = bf16[64,4,3072]{2,0,1:T(8,128)(2,1)S(1)} all-to-all(bf16[64,4,3072]{2,0,1:T(8,128)(2,1)S(1)} %pad_maximum_fusion), channel_id=1, replica_groups=mesh['ctx'=128,'head'=4] {'head'}, dimensions={1} | all-to-all | bytes 3145728 | tf_op jit(solution)/shard_map/all_to_all | solution.py:122
  25.7 0.0 copy-start
  25.8 2.6 %collective-permute-start = (bf16[256,1024]{1,0:T(8,128)(2,1)S(1)}, bf16[256,1024]{1,0:T(8,128)(2,1)S(1)}, u32[]{:S(2)}, u32[]{:S(2)}) collective-permute-start(bf16[256,1024]{1,0:T(8,128)(2,1)S(1)} %slice.26), channel_id=1, source_target_pairs={{0,4},{4,8},{8,12},{12,16},{16,20},{20,24},{24,28},{28,32},{32,36}... | collective-permute-start | bytes 1572872 | tf_op jit(solution)/shard_map/ppermute | solution.py:104
  28.4 6.5 %collective-permute-start.1 = (bf16[256,1024]{1,0:T(8,128)(2,1)S(1)}, bf16[256,1024]{1,0:T(8,128)(2,1)S(1)}, u32[]{:S(2)}, u32[]{:S(2)}) collective-permute-start(bf16[256,1024]{1,0:T(8,128)(2,1)S(1)} %slice.26), channel_id=1, source_target_pairs={{0,8},{4,12},{8,16},{12,20},{16,24},{20,28},{24,32},{28,36},{32,40... | collective-permute-start | bytes 1572872 | tf_op jit(solution)/shard_map/ppermute | solution.py:104
  34.9 0.0 copy-done.7
  34.9 0.8 copy.42.rel_ref
  35.7 18.0 %collective-permute-done.k1_ref.v1_ref = bf16[256,1024]{1,0:T(8,128)(2,1)S(1)} collective-permute-done((bf16[256,1024]{1,0:T(8,128)(2,1)S(1)}, bf16[256,1024]{1,0:T(8,128)(2,1)S(1)}, u32[]{:S(2)}, u32[]{:S(2)}) %collective-permute-start) | collective-permute-done | bytes 524320 | tf_op jit(solution)/shard_map/ppermute | solution.py:104
  53.7 0.0 copy-start.1
  53.7 15.7 %collective-permute-done.1.k2_ref.v2_ref = bf16[256,1024]{1,0:T(8,128)(2,1)S(1)} collective-permute-done((bf16[256,1024]{1,0:T(8,128)(2,1)S(1)}, bf16[256,1024]{1,0:T(8,128)(2,1)S(1)}, u32[]{:S(2)}, u32[]{:S(2)}) %collective-permute-start.1) | collective-permute-done | bytes 524320 | tf_op jit(solution)/shard_map/ppermute | solution.py:104
  69.4 0.0 copy-done
  69.4 0.0 copy-done.1
  69.4 0.0 copy-start.2
  69.4 0.8 copy-done.2
  70.2 10.5 %shard_map.76 = (f32[256,1024]{1,0:T(8,128)}, f32[2,256,512]{2,1,0:T(8,128)}, f32[2,256,512]{2,1,0:T(8,128)}, f32[2,256,512]{2,1,0:T(8,128)}) custom-call(s32[256,1]{1,0:T(8,128)} %copy.42.rel_ref, bf16[256,3072]{1,0:T(8,128)(2,1)} %bitcast.39, bf16[256,3072]{1,0:T(8,128)(2,1)} %bitcast.40, bf16[256,3072]{1,0:T(8,128)(2,1)} %bitcast.41, ...), custom_call_target="tpu_custom_call" | custom-call | tf_op jit(solution)/shard_map/pallas_call | solution.py:77
  80.7 0.0 copy-start.3
  80.8 0.0 copy-start.4
  80.8 1.4 convert_element_type.24
  82.2 1.9 %collective-permute-start.2 = (bf16[2,256,512]{2,1,0:T(8,128)(2,1)S(1)}, bf16[2,256,512]{2,1,0:T(8,128)(2,1)S(1)}, u32[]{:S(2)}, u32[]{:S(2)}) collective-permute-start(bf16[2,256,512]{2,1,0:T(8,128)(2,1)S(1)} %convert_element_type.24), channel_id=1, source_target_pairs={{4,0},{8,4},{12,8},{16,12},{20,16},{24,20},{28,24},{32,28},{36,32}... | collective-permute-start | bytes 1572872 | tf_op jit(solution)/shard_map/ppermute | solution.py:104
  84.1 1.3 convert_element_type.26
  85.4 1.9 %collective-permute-start.3 = (bf16[2,256,512]{2,1,0:T(8,128)(2,1)S(1)}, bf16[2,256,512]{2,1,0:T(8,128)(2,1)S(1)}, u32[]{:S(2)}, u32[]{:S(2)}) collective-permute-start(bf16[2,256,512]{2,1,0:T(8,128)(2,1)S(1)} %convert_element_type.26), channel_id=1, source_target_pairs={{8,0},{12,4},{16,8},{20,12},{24,16},{28,20},{32,24},{36,28},{40,32... | collective-permute-start | bytes 1572872 | tf_op jit(solution)/shard_map/ppermute | solution.py:104
  87.4 0.0 copy-done.3
  87.4 0.1 convert_element_type.23
  87.4 34.1 %collective-permute-done.2 = bf16[2,256,512]{2,1,0:T(8,128)(2,1)S(1)} collective-permute-done((bf16[2,256,512]{2,1,0:T(8,128)(2,1)S(1)}, bf16[2,256,512]{2,1,0:T(8,128)(2,1)S(1)}, u32[]{:S(2)}, u32[]{:S(2)}) %collective-permute-start.2) | collective-permute-done | bytes 524320 | tf_op jit(solution)/shard_map/ppermute | solution.py:104
  121.5 42.2 %collective-permute-done.3 = bf16[2,256,512]{2,1,0:T(8,128)(2,1)S(1)} collective-permute-done((bf16[2,256,512]{2,1,0:T(8,128)(2,1)S(1)}, bf16[2,256,512]{2,1,0:T(8,128)(2,1)S(1)}, u32[]{:S(2)}, u32[]{:S(2)}) %collective-permute-start.3) | collective-permute-done | bytes 524320 | tf_op jit(solution)/shard_map/ppermute | solution.py:104
  163.7 0.0 copy-done.4
  163.7 0.2 add_convert_fusion
  164.0 0.1 maximum_bitcast_fusion
  164.1 0.5 broadcast
  164.6 1.4 reduce
  166.1 0.8 reshape.45
  166.9 16.9 %all_to_all.34 = bf16[4,2,65536]{2,1,0:T(2,128)(2,1)S(1)} all-to-all(bf16[4,2,65536]{2,1,0:T(2,128)(2,1)S(1)} %reshape.45), channel_id=1, replica_groups=mesh['ctx'=128,'head'=4] {'head'}, dimensions={0} | all-to-all | bytes 2097152 | tf_op jit(solution)/shard_map/all_to_all | solution.py:146
  183.7 0.9 reshape.46
  184.7 0.6 copy.47
  185.4 0.8 copy.52
  186.2 0.7 copy.53
  186.9 0.7 copy.54
  (6 shorter events, 0.2 us)
Async XLA Ops:
  0.6 1.4 copy-start.6
  0.6 1.4 copy-start.5
  2.2 32.7 %copy-start.7 = (s32[256]{0:T(256)S(1)}, s32[256]{0:T(256)}, u32[]{:S(2)}) copy-start(s32[256]{0:T(256)} %param.9) | copy-start | bytes 3076
  25.7 43.7 %copy-start = (bf16[64,4,3072]{2,0,1:T(8,128)(2,1)}, bf16[64,4,3072]{2,0,1:T(8,128)(2,1)S(1)}, u32[]{:S(2)}) copy-start(bf16[64,4,3072]{2,0,1:T(8,128)(2,1)S(1)} %all_to_all.33) | copy-start | bytes 4718596
  25.8 27.9 %collective-permute-start = (bf16[256,1024]{1,0:T(8,128)(2,1)S(1)}, bf16[256,1024]{1,0:T(8,128)(2,1)S(1)}, u32[]{:S(2)}, u32[]{:S(2)}) collective-permute-start(bf16[256,1024]{1,0:T(8,128)(2,1)S(1)} %slice.26), channel_id=1, source_target_pairs={{0,4},{4,8},{8,12},{12,16},{16,20},{20,24},{24,28},{28,32},{32,36}... | collective-permute-start | bytes 1572872 | tf_op jit(solution)/shard_map/ppermute | solution.py:104
  28.4 41.0 %collective-permute-start.1 = (bf16[256,1024]{1,0:T(8,128)(2,1)S(1)}, bf16[256,1024]{1,0:T(8,128)(2,1)S(1)}, u32[]{:S(2)}, u32[]{:S(2)}) collective-permute-start(bf16[256,1024]{1,0:T(8,128)(2,1)S(1)} %slice.26), channel_id=1, source_target_pairs={{0,8},{4,12},{8,16},{12,20},{16,24},{20,28},{24,32},{28,36},{32,40... | collective-permute-start | bytes 1572872 | tf_op jit(solution)/shard_map/ppermute | solution.py:104
  53.7 15.7 %copy-start.1 = (bf16[256,1024]{1,0:T(8,128)(2,1)}, bf16[256,1024]{1,0:T(8,128)(2,1)S(1)}, u32[]{:S(2)}) copy-start(bf16[256,1024]{1,0:T(8,128)(2,1)S(1)} %collective-permute-done.k1_ref.v1_ref) | copy-start | bytes 1572868
  69.4 0.8 copy-start.2
  80.7 6.6 %copy-start.3 = (f32[256,1024]{1,0:T(8,128)S(1)}, f32[256,1024]{1,0:T(8,128)}, u32[]{:S(2)}) copy-start(f32[256,1024]{1,0:T(8,128)} %get-tuple-element.7) | copy-start | bytes 3145732
  80.8 83.0 %copy-start.4 = (f32[2,256,512]{2,1,0:T(8,128)S(1)}, f32[2,256,512]{2,1,0:T(8,128)}, u32[]{:S(2)}) copy-start(f32[2,256,512]{2,1,0:T(8,128)} %get-tuple-element.8) | copy-start | bytes 3145732
  82.2 39.3 %collective-permute-start.2 = (bf16[2,256,512]{2,1,0:T(8,128)(2,1)S(1)}, bf16[2,256,512]{2,1,0:T(8,128)(2,1)S(1)}, u32[]{:S(2)}, u32[]{:S(2)}) collective-permute-start(bf16[2,256,512]{2,1,0:T(8,128)(2,1)S(1)} %convert_element_type.24), channel_id=1, source_target_pairs={{4,0},{8,4},{12,8},{16,12},{20,16},{24,20},{28,24},{32,28},{36,32}... | collective-permute-start | bytes 1572872 | tf_op jit(solution)/shard_map/ppermute | solution.py:104
  85.4 78.3 %collective-permute-start.3 = (bf16[2,256,512]{2,1,0:T(8,128)(2,1)S(1)}, bf16[2,256,512]{2,1,0:T(8,128)(2,1)S(1)}, u32[]{:S(2)}, u32[]{:S(2)}) collective-permute-start(bf16[2,256,512]{2,1,0:T(8,128)(2,1)S(1)} %convert_element_type.26), channel_id=1, source_target_pairs={{8,0},{12,4},{16,8},{20,12},{24,16},{28,20},{32,24},{36,28},{40,32... | collective-permute-start | bytes 1572872 | tf_op jit(solution)/shard_map/ppermute | solution.py:104

commit v6 on v5

--- a/solution.py
+++ b/solution.py
@@ -10,6 +10,7 @@
 WINDOW = 512
 SPAN = 2
 CHAIN = False
+CHUNKS = 2
 
 score_scale = 168.0 ** (-0.5)
 NT = (((1,), (1,)), ((), ()))
@@ -104,21 +105,8 @@
     return lax.ppermute(block, axis, route)
 
 
-def local(queries, normed_key_state, value_state_rows, output_gradient, doc_start):
-    heads_ax = lax.axis_size("head")
-    rows_in = queries.shape[0]
-    tok_rows = doc_start.shape[0]
-    kv_cols = normed_key_state.shape[1] // heads_ax
-    q_cols = queries.shape[1] // heads_ax
-    x_in = jnp.concatenate(
-        [
-            normed_key_state.reshape(rows_in, heads_ax, kv_cols),
-            value_state_rows.reshape(rows_in, heads_ax, kv_cols),
-            queries.reshape(rows_in, heads_ax, q_cols),
-            output_gradient.reshape(rows_in, heads_ax, q_cols),
-        ],
-        axis=2,
-    )
+def chunk_pass(x_in, rel, kv_cols, q_cols):
+    tok_rows = rel.shape[0]
     x_all = lax.all_to_all(x_in, "head", split_axis=1, concat_axis=0, tiled=True)
     x_all = x_all.reshape(tok_rows, 2 * kv_cols + 2 * q_cols)
     kv_local = x_all[:, : 2 * kv_cols]
@@ -128,8 +116,6 @@
     else:
         kv1 = passed_along(kv_local, "ctx", 1)
         kv2 = passed_along(kv_local, "ctx", 2)
-    shard_index = lax.axis_index("ctx")
-    rel = (doc_start - shard_index * tok_rows).reshape(tok_rows, 1)
     dq, dkv0, dkv1, dkv2 = attend(rel, x_all, (kv1, kv2))
     if CHAIN:
         carried = passed_along(dkv2.astype(jnp.bfloat16), "ctx", -1)
@@ -143,10 +129,31 @@
         [dq.astype(jnp.bfloat16), kv_total[0].astype(jnp.bfloat16), kv_total[1].astype(jnp.bfloat16)],
         axis=1,
     )[:, None]
-    out = lax.all_to_all(out_loc, "head", split_axis=0, concat_axis=1, tiled=True)
-    grad_q = out[:, :, :q_cols].reshape(rows_in, heads_ax * q_cols)
-    grad_k = out[:, :, q_cols : q_cols + kv_cols].reshape(rows_in, heads_ax * kv_cols)
-    grad_v = out[:, :, q_cols + kv_cols :].reshape(rows_in, heads_ax * kv_cols)
+    return lax.all_to_all(out_loc, "head", split_axis=0, concat_axis=1, tiled=True)
+
+
+def local(queries, normed_key_state, value_state_rows, output_gradient, doc_start):
+    heads_ax = lax.axis_size("head")
+    rows_in = queries.shape[0]
+    tok_rows = doc_start.shape[0]
+    kv_cols = normed_key_state.shape[1] // (heads_ax * CHUNKS)
+    q_cols = queries.shape[1] // (heads_ax * CHUNKS)
+    shard_index = lax.axis_index("ctx")
+    rel = (doc_start - shard_index * tok_rows).reshape(tok_rows, 1)
+    parts = [
+        normed_key_state.reshape(rows_in, heads_ax, CHUNKS, kv_cols),
+        value_state_rows.reshape(rows_in, heads_ax, CHUNKS, kv_cols),
+        queries.reshape(rows_in, heads_ax, CHUNKS, q_cols),
+        output_gradient.reshape(rows_in, heads_ax, CHUNKS, q_cols),
+    ]
+    outs = []
+    for chunk in range(CHUNKS):
+        x_in = jnp.concatenate([p[:, :, chunk] for p in parts], axis=2)
+        outs.append(chunk_pass(x_in, rel, kv_cols, q_cols))
+    out = jnp.stack(outs, axis=2)
+    grad_q = out[..., :q_cols].reshape(rows_in, heads_ax * CHUNKS * q_cols)
+    grad_k = out[..., q_cols : q_cols + kv_cols].reshape(rows_in, heads_ax * CHUNKS * kv_cols)
+    grad_v = out[..., q_cols + kv_cols :].reshape(rows_in, heads_ax * CHUNKS * kv_cols)
     return grad_q, grad_k, grad_v
 
 

time: 188 us -> 153 us (0.81)
  the two profiles are of different devices: /device:TPU:182 before, /device:TPU:62 now
where the time goes in v6:
time: 153 us; the launch traced here: 152 us
  waiting for transfers between devices  68 us (44%)
  starting transfers between devices  45.2 us (30%)
  local copies, waits for them, and re-layouts  17.6 us (12%)
  Pallas kernels  12.6 us (8%)
  other arithmetic  7.82 us (5%)
    ppermute x8, waiting for transfers between devices, passed_along(): return lax.ppermute(block, axis, route)  43.4 us
    ppermute x8, starting transfers between devices, passed_along(): return lax.ppermute(block, axis, route)  27.1 us
    all_to_all x2, waiting for transfers between devices, chunk_pass(): lax.all_to_all(out_loc, 'head', split_axis=0, concat_axis=1, tiled=True)  13.3 us
    pallas_call x2, Pallas kernels, attend(): pl.pallas_call(attn_kernel, grid=(groups,), in_specs=[pl.BlockSpec((tok,...  12.6 us
    all_to_all x2, waiting for transfers between devices, chunk_pass(): lax.all_to_all(x_in, 'head', split_axis=1, concat_axis=0, tiled=True)  11.3 us
    all_to_all x2, starting transfers between devices, chunk_pass(): lax.all_to_all(out_loc, 'head', split_axis=0, concat_axis=1, tiled=True)  11 us
    all_to_all x2, starting transfers between devices, chunk_pass(): lax.all_to_all(x_in, 'head', split_axis=1, concat_axis=0, tiled=True)  7.13 us
    unnamed x34, local copies, waits for them, and re-layouts  6.2 us
  transfers between devices with their start and end apart: 12, of which 8 were waited for; matrix products, arithmetic and copies ran while one was open for 8% of the time, Pallas kernels for 8%

profile of v6, /device:TPU:62, one launch (start us, length us, event | category | flops | bytes accessed | tf_op | source)
XLA Modules:
  0.0 152.3 jit_solution(2393857147050756001)
XLA Ops:
  0.6 1.1 reshape.45
  1.8 1.1 reshape.46
  4.0 0.4 reshape.47
  4.4 0.4 reshape.48
  4.8 0.7 fusion.3
  5.5 0.7 fusion.2
  6.6 1.0 pad_maximum_fusion.1
  7.6 3.6 %all-to-all-start.2 = ((bf16[64,4,1536]{2,0,1:T(8,128)(2,1)}), bf16[64,4,1536]{2,0,1:T(8,128)(2,1)S(1)}, u32[]{:S(2)}, u32[]{:S(2)}) async-start(bf16[64,4,1536]{2,0,1:T(8,128)(2,1)} %pad_maximum_fusion.1), calls=%async_computation.2 | async-start | bytes 1572864 | tf_op jit(solution)/shard_map/all_to_all | solution.py:110
  11.6 0.9 pad_maximum_fusion
  12.6 10.3 %all-to-all-done.2 = bf16[64,4,1536]{2,0,1:T(8,128)(2,1)S(1)} async-done(((bf16[64,4,1536]{2,0,1:T(8,128)(2,1)}), bf16[64,4,1536]{2,0,1:T(8,128)(2,1)S(1)}, u32[]{:S(2)}, u32[]{:S(2)}) %all-to-all-start.2) | async-done | bytes 786464 | tf_op jit(solution)/shard_map/all_to_all | solution.py:110
  22.9 3.5 %all-to-all-start = ((bf16[64,4,1536]{2,0,1:T(8,128)(2,1)}), bf16[64,4,1536]{2,0,1:T(8,128)(2,1)S(1)}, u32[]{:S(2)}, u32[]{:S(2)}) async-start(bf16[64,4,1536]{2,0,1:T(8,128)(2,1)} %pad_maximum_fusion), calls=%async_computation | async-start | bytes 1572864 | tf_op jit(solution)/shard_map/all_to_all | solution.py:110
  26.4 6.2 %collective-permute-start.5 = (bf16[256,512]{1,0:T(8,128)(2,1)S(1)}, bf16[256,512]{1,0:T(8,128)(2,1)S(1)}, u32[]{:S(2)}, u32[]{:S(2)}) collective-permute-start(bf16[256,512]{1,0:T(8,128)(2,1)S(1)} %slice.83), channel_id=1, source_target_pairs={{0,8},{4,12},{8,16},{12,20},{16,24},{20,28},{24,32},{28,36},{32,40... | collective-permute-start | bytes 786440 | tf_op jit(solution)/shard_map/ppermute | solution.py:105
  32.6 3.5 %collective-permute-start.4 = (bf16[256,512]{1,0:T(8,128)(2,1)S(1)}, bf16[256,512]{1,0:T(8,128)(2,1)S(1)}, u32[]{:S(2)}, u32[]{:S(2)}) collective-permute-start(bf16[256,512]{1,0:T(8,128)(2,1)S(1)} %slice.83), channel_id=1, source_target_pairs={{0,4},{4,8},{8,12},{12,16},{16,20},{20,24},{24,28},{28,32},{32,36}... | collective-permute-start | bytes 786440 | tf_op jit(solution)/shard_map/ppermute | solution.py:105
  36.2 0.8 copy.63.rel_ref
  37.0 1.0 all-to-all-done
  38.0 6.2 %collective-permute-start.1 = (bf16[256,512]{1,0:T(8,128)(2,1)S(1)}, bf16[256,512]{1,0:T(8,128)(2,1)S(1)}, u32[]{:S(2)}, u32[]{:S(2)}) collective-permute-start(bf16[256,512]{1,0:T(8,128)(2,1)S(1)} %slice.76), channel_id=1, source_target_pairs={{0,8},{4,12},{8,16},{12,20},{16,24},{20,28},{24,32},{28,36},{32,40... | collective-permute-start | bytes 786440 | tf_op jit(solution)/shard_map/ppermute | solution.py:105
  44.2 3.5 %collective-permute-start = (bf16[256,512]{1,0:T(8,128)(2,1)S(1)}, bf16[256,512]{1,0:T(8,128)(2,1)S(1)}, u32[]{:S(2)}, u32[]{:S(2)}) collective-permute-start(bf16[256,512]{1,0:T(8,128)(2,1)S(1)} %slice.76), channel_id=1, source_target_pairs={{0,4},{4,8},{8,12},{12,16},{16,20},{20,24},{24,28},{28,32},{32,36}... | collective-permute-start | bytes 786440 | tf_op jit(solution)/shard_map/ppermute | solution.py:105
  47.7 15.8 %collective-permute-done.4.k1_ref.v1_ref = bf16[256,512]{1,0:T(8,128)(2,1)S(1)} collective-permute-done((bf16[256,512]{1,0:T(8,128)(2,1)S(1)}, bf16[256,512]{1,0:T(8,128)(2,1)S(1)}, u32[]{:S(2)}, u32[]{:S(2)}) %collective-permute-start.4) | collective-permute-done | bytes 262176 | tf_op jit(solution)/shard_map/ppermute | solution.py:105
  63.5 0.7 copy-done.4
  64.2 6.3 %shard_map.77 = (f32[256,512]{1,0:T(8,128)}, f32[2,256,256]{2,1,0:T(8,128)}, f32[2,256,256]{2,1,0:T(8,128)}, f32[2,256,256]{2,1,0:T(8,128)}) custom-call(s32[256,1]{1,0:T(8,128)} %copy.63.rel_ref, bf16[256,1536]{1,0:T(8,128)(2,1)} %bitcast.46, bf16[256,1536]{1,0:T(8,128)(2,1)} %bitcast.47, bf16[256,1536]{1,0:T(8,128)(2,1)} %bitcast.48, ...), custom_call_target="tpu_custom_call" | custom-call | tf_op jit(solution)/shard_map/pallas_call | solution.py:78
  70.5 1.1 convert_element_type.54
  71.7 1.1 convert_element_type.56
  72.7 1.9 %collective-permute-start.7 = (bf16[2,256,256]{2,1,0:T(8,128)(2,1)S(1)}, bf16[2,256,256]{2,1,0:T(8,128)(2,1)S(1)}, u32[]{:S(2)}, u32[]{:S(2)}) collective-permute-start(bf16[2,256,256]{2,1,0:T(8,128)(2,1)S(1)} %convert_element_type.56), channel_id=1, source_target_pairs={{8,0},{12,4},{16,8},{20,12},{24,16},{28,20},{32,24},{36,28},{40,32... | collective-permute-start | bytes 786440 | tf_op jit(solution)/shard_map/ppermute | solution.py:105
  74.7 1.9 %collective-permute-start.6 = (bf16[2,256,256]{2,1,0:T(8,128)(2,1)S(1)}, bf16[2,256,256]{2,1,0:T(8,128)(2,1)S(1)}, u32[]{:S(2)}, u32[]{:S(2)}) collective-permute-start(bf16[2,256,256]{2,1,0:T(8,128)(2,1)S(1)} %convert_element_type.54), channel_id=1, source_target_pairs={{4,0},{8,4},{12,8},{16,12},{20,16},{24,20},{28,24},{32,28},{36,32}... | collective-permute-start | bytes 786440 | tf_op jit(solution)/shard_map/ppermute | solution.py:105
  76.7 0.7 copy-done.3
  77.4 0.7 copy-done.5
  78.1 6.3 %shard_map.76 = (f32[256,512]{1,0:T(8,128)}, f32[2,256,256]{2,1,0:T(8,128)}, f32[2,256,256]{2,1,0:T(8,128)}, f32[2,256,256]{2,1,0:T(8,128)}) custom-call(s32[256,1]{1,0:T(8,128)} %copy.63.rel_ref, bf16[256,1536]{1,0:T(8,128)(2,1)} %bitcast.51, bf16[256,1536]{1,0:T(8,128)(2,1)} %bitcast.52, bf16[256,1536]{1,0:T(8,128)(2,1)} %bitcast.53, ...), custom_call_target="tpu_custom_call" | custom-call | tf_op jit(solution)/shard_map/pallas_call | solution.py:78
  84.4 1.2 convert_element_type.47
  85.6 1.9 %collective-permute-start.3 = (bf16[2,256,256]{2,1,0:T(8,128)(2,1)S(1)}, bf16[2,256,256]{2,1,0:T(8,128)(2,1)S(1)}, u32[]{:S(2)}, u32[]{:S(2)}) collective-permute-start(bf16[2,256,256]{2,1,0:T(8,128)(2,1)S(1)} %convert_element_type.49), channel_id=1, source_target_pairs={{8,0},{12,4},{16,8},{20,12},{24,16},{28,20},{32,24},{36,28},{40,32... | collective-permute-start | bytes 786440 | tf_op jit(solution)/shard_map/ppermute | solution.py:105
  87.5 1.9 %collective-permute-start.2 = (bf16[2,256,256]{2,1,0:T(8,128)(2,1)S(1)}, bf16[2,256,256]{2,1,0:T(8,128)(2,1)S(1)}, u32[]{:S(2)}, u32[]{:S(2)}) collective-permute-start(bf16[2,256,256]{2,1,0:T(8,128)(2,1)S(1)} %convert_element_type.47), channel_id=1, source_target_pairs={{4,0},{8,4},{12,8},{16,12},{20,16},{24,20},{28,24},{32,28},{36,32}... | collective-permute-start | bytes 786440 | tf_op jit(solution)/shard_map/ppermute | solution.py:105
  89.4 4.5 %collective-permute-done.7 = bf16[2,256,256]{2,1,0:T(8,128)(2,1)S(1)} collective-permute-done((bf16[2,256,256]{2,1,0:T(8,128)(2,1)S(1)}, bf16[2,256,256]{2,1,0:T(8,128)(2,1)S(1)}, u32[]{:S(2)}, u32[]{:S(2)}) %collective-permute-start.7) | collective-permute-done | bytes 262176 | tf_op jit(solution)/shard_map/ppermute | solution.py:105
  93.9 22.0 %collective-permute-done.6 = bf16[2,256,256]{2,1,0:T(8,128)(2,1)S(1)} collective-permute-done((bf16[2,256,256]{2,1,0:T(8,128)(2,1)S(1)}, bf16[2,256,256]{2,1,0:T(8,128)(2,1)S(1)}, u32[]{:S(2)}, u32[]{:S(2)}) %collective-permute-start.6) | collective-permute-done | bytes 262176 | tf_op jit(solution)/shard_map/ppermute | solution.py:105
  116.1 0.5 broadcast
  116.6 1.0 reduce.1
  117.6 1.2 reshape.56
  118.8 6.3 %all-to-all-start.3 = ((bf16[4,2,32768]{2,1,0:T(2,128)(2,1)}), bf16[4,2,32768]{2,1,0:T(2,128)(2,1)S(1)}, u32[]{:S(2)}, u32[]{:S(2)}) async-start(bf16[4,2,32768]{2,1,0:T(2,128)(2,1)} %reshape.56), calls=%async_computation.3 | async-start | bytes 1048576 | tf_op jit(solution)/shard_map/all_to_all | solution.py:132
  125.1 1.2 collective-permute-done.2
  126.5 1.0 reduce
  127.6 1.2 reshape.54
  128.7 5.2 %all-to-all-done.3 = bf16[4,2,32768]{2,1,0:T(2,128)(2,1)S(1)} async-done(((bf16[4,2,32768]{2,1,0:T(2,128)(2,1)}), bf16[4,2,32768]{2,1,0:T(2,128)(2,1)S(1)}, u32[]{:S(2)}, u32[]{:S(2)}) %all-to-all-start.3) | async-done | bytes 524320 | tf_op jit(solution)/shard_map/all_to_all | solution.py:132
  133.9 4.7 %all-to-all-start.1 = ((bf16[4,2,32768]{2,1,0:T(2,128)(2,1)}), bf16[4,2,32768]{2,1,0:T(2,128)(2,1)S(1)}, u32[]{:S(2)}, u32[]{:S(2)}) async-start(bf16[4,2,32768]{2,1,0:T(2,128)(2,1)} %reshape.54), calls=%async_computation.1 | async-start | bytes 1048576 | tf_op jit(solution)/shard_map/all_to_all | solution.py:132
  138.6 0.5 reshape.57
  139.3 8.1 %all-to-all-done.1 = bf16[4,2,32768]{2,1,0:T(2,128)(2,1)S(1)} async-done(((bf16[4,2,32768]{2,1,0:T(2,128)(2,1)}), bf16[4,2,32768]{2,1,0:T(2,128)(2,1)S(1)}, u32[]{:S(2)}, u32[]{:S(2)}) %all-to-all-start.1) | async-done | bytes 524320 | tf_op jit(solution)/shard_map/all_to_all | solution.py:132
  147.4 0.5 reshape.55
  148.5 0.9 reshape.53
  149.4 0.5 copy.71
  149.9 1.2 reshape.51
  151.4 0.9 reshape.52
  (53 shorter events, 3.3 us)
Async XLA Ops:
  2.9 1.0 copy-start.9
  3.3 1.1 copy-start.10
  7.6 15.3 %all-to-all-start.2 = ((bf16[64,4,1536]{2,0,1:T(8,128)(2,1)}), bf16[64,4,1536]{2,0,1:T(8,128)(2,1)S(1)}, u32[]{:S(2)}, u32[]{:S(2)}) async-start(bf16[64,4,1536]{2,0,1:T(8,128)(2,1)} %pad_maximum_fusion.1), calls=%async_computation.2 | async-start | bytes 1572864 | tf_op jit(solution)/shard_map/all_to_all | solution.py:110
  12.6 23.6 %copy-start.13 = (s32[256]{0:T(256)S(1)}, s32[256]{0:T(256)}, u32[]{:S(2)}) copy-start(s32[256]{0:T(256)} %param.9) | copy-start | bytes 3076
  22.9 3.5 %copy-start = (bf16[64,4,1536]{2,0,1:T(8,128)(2,1)}, bf16[64,4,1536]{2,0,1:T(8,128)(2,1)S(1)}, u32[]{:S(2)}) copy-start(bf16[64,4,1536]{2,0,1:T(8,128)(2,1)S(1)} %all-to-all-done.2) | copy-start | bytes 2359300
  22.9 15.1 %all-to-all-start = ((bf16[64,4,1536]{2,0,1:T(8,128)(2,1)}), bf16[64,4,1536]{2,0,1:T(8,128)(2,1)S(1)}, u32[]{:S(2)}, u32[]{:S(2)}) async-start(bf16[64,4,1536]{2,0,1:T(8,128)(2,1)} %pad_maximum_fusion), calls=%async_computation | async-start | bytes 1572864 | tf_op jit(solution)/shard_map/all_to_all | solution.py:110
  26.4 21.3 %collective-permute-start.5 = (bf16[256,512]{1,0:T(8,128)(2,1)S(1)}, bf16[256,512]{1,0:T(8,128)(2,1)S(1)}, u32[]{:S(2)}, u32[]{:S(2)}) collective-permute-start(bf16[256,512]{1,0:T(8,128)(2,1)S(1)} %slice.83), channel_id=1, source_target_pairs={{0,8},{4,12},{8,16},{12,20},{16,24},{20,28},{24,32},{28,36},{32,40... | collective-permute-start | bytes 786440 | tf_op jit(solution)/shard_map/ppermute | solution.py:105
  32.6 30.9 %collective-permute-start.4 = (bf16[256,512]{1,0:T(8,128)(2,1)S(1)}, bf16[256,512]{1,0:T(8,128)(2,1)S(1)}, u32[]{:S(2)}, u32[]{:S(2)}) collective-permute-start(bf16[256,512]{1,0:T(8,128)(2,1)S(1)} %slice.83), channel_id=1, source_target_pairs={{0,4},{4,8},{8,12},{12,16},{16,20},{20,24},{24,28},{28,32},{32,36}... | collective-permute-start | bytes 786440 | tf_op jit(solution)/shard_map/ppermute | solution.py:105
  38.0 32.5 %copy-start.1 = (bf16[64,4,1536]{2,0,1:T(8,128)(2,1)}, bf16[64,4,1536]{2,0,1:T(8,128)(2,1)S(1)}, u32[]{:S(2)}) copy-start(bf16[64,4,1536]{2,0,1:T(8,128)(2,1)S(1)} %all-to-all-done) | copy-start | bytes 2359300
  38.0 38.7 %collective-permute-start.1 = (bf16[256,512]{1,0:T(8,128)(2,1)S(1)}, bf16[256,512]{1,0:T(8,128)(2,1)S(1)}, u32[]{:S(2)}, u32[]{:S(2)}) collective-permute-start(bf16[256,512]{1,0:T(8,128)(2,1)S(1)} %slice.76), channel_id=1, source_target_pairs={{0,8},{4,12},{8,16},{12,20},{16,24},{20,28},{24,32},{28,36},{32,40... | collective-permute-start | bytes 786440 | tf_op jit(solution)/shard_map/ppermute | solution.py:105
  44.2 32.4 %collective-permute-start = (bf16[256,512]{1,0:T(8,128)(2,1)S(1)}, bf16[256,512]{1,0:T(8,128)(2,1)S(1)}, u32[]{:S(2)}, u32[]{:S(2)}) collective-permute-start(bf16[256,512]{1,0:T(8,128)(2,1)S(1)} %slice.76), channel_id=1, source_target_pairs={{0,4},{4,8},{8,12},{12,16},{16,20},{20,24},{24,28},{28,32},{32,36}... | collective-permute-start | bytes 786440 | tf_op jit(solution)/shard_map/ppermute | solution.py:105
  47.7 15.8 %copy-start.2 = (bf16[256,512]{1,0:T(8,128)(2,1)}, bf16[256,512]{1,0:T(8,128)(2,1)S(1)}, u32[]{:S(2)}) copy-start(bf16[256,512]{1,0:T(8,128)(2,1)S(1)} %collective-permute-done.5.k2_ref.v2_ref) | copy-start | bytes 786436
  63.5 0.7 copy-start.4
  70.5 6.1 %copy-start.7 = (f32[256,512]{1,0:T(8,128)S(1)}, f32[256,512]{1,0:T(8,128)}, u32[]{:S(2)}) copy-start(f32[256,512]{1,0:T(8,128)} %get-tuple-element.15) | copy-start | bytes 1572868
  72.7 21.2 %collective-permute-start.7 = (bf16[2,256,256]{2,1,0:T(8,128)(2,1)S(1)}, bf16[2,256,256]{2,1,0:T(8,128)(2,1)S(1)}, u32[]{:S(2)}, u32[]{:S(2)}) collective-permute-start(bf16[2,256,256]{2,1,0:T(8,128)(2,1)S(1)} %convert_element_type.56), channel_id=1, source_target_pairs={{8,0},{12,4},{16,8},{20,12},{24,16},{28,20},{32,24},{36,28},{40,32... | collective-permute-start | bytes 786440 | tf_op jit(solution)/shard_map/ppermute | solution.py:105
  74.7 41.2 %collective-permute-start.6 = (bf16[2,256,256]{2,1,0:T(8,128)(2,1)S(1)}, bf16[2,256,256]{2,1,0:T(8,128)(2,1)S(1)}, u32[]{:S(2)}, u32[]{:S(2)}) collective-permute-start(bf16[2,256,256]{2,1,0:T(8,128)(2,1)S(1)} %convert_element_type.54), channel_id=1, source_target_pairs={{4,0},{8,4},{12,8},{16,12},{20,16},{24,20},{28,24},{32,28},{36,32}... | collective-permute-start | bytes 786440 | tf_op jit(solution)/shard_map/ppermute | solution.py:105
  76.6 0.7 copy-start.3
  77.4 0.7 copy-start.5
  84.3 1.2 copy-start.8
  84.4 31.5 %copy-start.12 = (f32[2,256,256]{2,1,0:T(8,128)S(1)}, f32[2,256,256]{2,1,0:T(8,128)}, u32[]{:S(2)}) copy-start(f32[2,256,256]{2,1,0:T(8,128)} %get-tuple-element.16) | copy-start | bytes 1572868
  85.6 39.5 %collective-permute-start.3 = (bf16[2,256,256]{2,1,0:T(8,128)(2,1)S(1)}, bf16[2,256,256]{2,1,0:T(8,128)(2,1)S(1)}, u32[]{:S(2)}, u32[]{:S(2)}) collective-permute-start(bf16[2,256,256]{2,1,0:T(8,128)(2,1)S(1)} %convert_element_type.49), channel_id=1, source_target_pairs={{8,0},{12,4},{16,8},{20,12},{24,16},{28,20},{32,24},{36,28},{40,32... | collective-permute-start | bytes 786440 | tf_op jit(solution)/shard_map/ppermute | solution.py:105
  87.5 38.8 %collective-permute-start.2 = (bf16[2,256,256]{2,1,0:T(8,128)(2,1)S(1)}, bf16[2,256,256]{2,1,0:T(8,128)(2,1)S(1)}, u32[]{:S(2)}, u32[]{:S(2)}) collective-permute-start(bf16[2,256,256]{2,1,0:T(8,128)(2,1)S(1)} %convert_element_type.47), channel_id=1, source_target_pairs={{4,0},{8,4},{12,8},{16,12},{20,16},{24,20},{28,24},{32,28},{36,32}... | collective-permute-start | bytes 786440 | tf_op jit(solution)/shard_map/ppermute | solution.py:105
  117.6 7.5 %copy-start.6 = (f32[256,512]{1,0:T(8,128)S(1)}, f32[256,512]{1,0:T(8,128)}, u32[]{:S(2)}) copy-start(f32[256,512]{1,0:T(8,128)} %get-tuple-element.11) | copy-start | bytes 1572868
  118.8 7.5 %copy-start.11 = (f32[2,256,256]{2,1,0:T(8,128)S(1)}, f32[2,256,256]{2,1,0:T(8,128)}, u32[]{:S(2)}) copy-start(f32[2,256,256]{2,1,0:T(8,128)} %get-tuple-element.12) | copy-start | bytes 1572868
  118.8 15.1 %all-to-all-start.3 = ((bf16[4,2,32768]{2,1,0:T(2,128)(2,1)}), bf16[4,2,32768]{2,1,0:T(2,128)(2,1)S(1)}, u32[]{:S(2)}, u32[]{:S(2)}) async-start(bf16[4,2,32768]{2,1,0:T(2,128)(2,1)} %reshape.56), calls=%async_computation.3 | async-start | bytes 1048576 | tf_op jit(solution)/shard_map/all_to_all | solution.py:132
  133.9 13.5 %all-to-all-start.1 = ((bf16[4,2,32768]{2,1,0:T(2,128)(2,1)}), bf16[4,2,32768]{2,1,0:T(2,128)(2,1)S(1)}, u32[]{:S(2)}, u32[]{:S(2)}) async-start(bf16[4,2,32768]{2,1,0:T(2,128)(2,1)} %reshape.54), calls=%async_computation.1 | async-start | bytes 1048576 | tf_op jit(solution)/shard_map/all_to_all | solution.py:132

commit v7 on v6

--- a/solution.py
+++ b/solution.py
@@ -9,7 +9,7 @@
 HEAD_SIZE = 128
 WINDOW = 512
 SPAN = 2
-CHAIN = False
+CHAIN = True
 CHUNKS = 2
 
 score_scale = 168.0 ** (-0.5)

time: 153 us -> 168 us (1.098)
  the two profiles are of different devices: /device:TPU:62 before, /device:TPU:262 now
where the time goes in v7:
time: 168 us; the launch traced here: 167 us
  waiting for transfers between devices  94.6 us (56%)
  starting transfers between devices  35.1 us (21%)
  local copies, waits for them, and re-layouts  17 us (10%)
  Pallas kernels  12.6 us (8%)
  other arithmetic  6.71 us (4%)
    all_to_all x2, waiting for transfers between devices, chunk_pass(): lax.all_to_all(x_in, 'head', split_axis=1, concat_axis=0, tiled=True)  61.3 us
    ppermute x8, starting transfers between devices, passed_along(): return lax.ppermute(block, axis, route)  20.7 us
    ppermute x8, waiting for transfers between devices, passed_along(): return lax.ppermute(block, axis, route)  19 us
    all_to_all x2, waiting for transfers between devices, chunk_pass(): lax.all_to_all(out_loc, 'head', split_axis=0, concat_axis=1, tiled=True)  14.3 us
    pallas_call x2, Pallas kernels, attend(): pl.pallas_call(attn_kernel, grid=(groups,), in_specs=[pl.BlockSpec((tok,...  12.6 us
    all_to_all x2, starting transfers between devices, chunk_pass(): lax.all_to_all(out_loc, 'head', split_axis=0, concat_axis=1, tiled=True)  7.43 us
    all_to_all x2, starting transfers between devices, chunk_pass(): lax.all_to_all(x_in, 'head', split_axis=1, concat_axis=0, tiled=True)  6.99 us
    unnamed x36, local copies, waits for them, and re-layouts  5.55 us
  transfers between devices with their start and end apart: 12, of which 8 were waited for; matrix products, arithmetic and copies ran while one was open for 6% of the time, Pallas kernels for 8%

profile of v7, /device:TPU:262, one launch (start us, length us, event | category | flops | bytes accessed | tf_op | source)
XLA Modules:
  0.0 167.1 jit_solution(8589892085393167164)
XLA Ops:
  0.6 1.1 reshape.45
  1.8 1.1 reshape.46
  2.9 0.4 fusion.5
  3.3 0.4 fusion.4
  4.0 0.4 reshape.47
  4.4 0.4 reshape.48
  4.8 0.7 fusion.3
  5.5 0.7 fusion.2
  6.6 1.0 pad_maximum_fusion.1
  7.6 3.5 %all-to-all-start.2 = ((bf16[64,4,1536]{2,0,1:T(8,128)(2,1)}), bf16[64,4,1536]{2,0,1:T(8,128)(2,1)S(1)}, u32[]{:S(2)}, u32[]{:S(2)}) async-start(bf16[64,4,1536]{2,0,1:T(8,128)(2,1)} %pad_maximum_fusion.1), calls=%async_computation.2 | async-start | bytes 1572864 | tf_op jit(solution)/shard_map/all_to_all | solution.py:110
  11.5 0.9 pad_maximum_fusion
  12.4 10.3 %all-to-all-done.2 = bf16[64,4,1536]{2,0,1:T(8,128)(2,1)S(1)} async-done(((bf16[64,4,1536]{2,0,1:T(8,128)(2,1)}), bf16[64,4,1536]{2,0,1:T(8,128)(2,1)S(1)}, u32[]{:S(2)}, u32[]{:S(2)}) %all-to-all-start.2) | async-done | bytes 786464 | tf_op jit(solution)/shard_map/all_to_all | solution.py:110
  22.7 3.5 %all-to-all-start = ((bf16[64,4,1536]{2,0,1:T(8,128)(2,1)}), bf16[64,4,1536]{2,0,1:T(8,128)(2,1)S(1)}, u32[]{:S(2)}, u32[]{:S(2)}) async-start(bf16[64,4,1536]{2,0,1:T(8,128)(2,1)} %pad_maximum_fusion), calls=%async_computation | async-start | bytes 1572864 | tf_op jit(solution)/shard_map/all_to_all | solution.py:110
  26.2 3.5 %collective-permute-start.4 = (bf16[256,512]{1,0:T(8,128)(2,1)S(1)}, bf16[256,512]{1,0:T(8,128)(2,1)S(1)}, u32[]{:S(2)}, u32[]{:S(2)}) collective-permute-start(bf16[256,512]{1,0:T(8,128)(2,1)S(1)} %slice.83), channel_id=1, source_target_pairs={{0,4},{4,8},{8,12},{12,16},{16,20},{20,24},{24,28},{28,32},{32,36}... | collective-permute-start | bytes 786440 | tf_op jit(solution)/shard_map/ppermute | solution.py:105
  29.7 51.0 %all-to-all-done = bf16[64,4,1536]{2,0,1:T(8,128)(2,1)S(1)} async-done(((bf16[64,4,1536]{2,0,1:T(8,128)(2,1)}), bf16[64,4,1536]{2,0,1:T(8,128)(2,1)S(1)}, u32[]{:S(2)}, u32[]{:S(2)}) %all-to-all-start) | async-done | bytes 786464 | tf_op jit(solution)/shard_map/all_to_all | solution.py:110
  80.8 1.9 %collective-permute-start = (bf16[256,512]{1,0:T(8,128)(2,1)S(1)}, bf16[256,512]{1,0:T(8,128)(2,1)S(1)}, u32[]{:S(2)}, u32[]{:S(2)}) collective-permute-start(bf16[256,512]{1,0:T(8,128)(2,1)S(1)} %slice.76), channel_id=1, source_target_pairs={{0,4},{4,8},{8,12},{12,16},{16,20},{20,24},{24,28},{28,32},{32,36}... | collective-permute-start | bytes 786440 | tf_op jit(solution)/shard_map/ppermute | solution.py:105
  82.7 1.9 %collective-permute-start.5 = (bf16[256,512]{1,0:T(8,128)(2,1)S(1)}, bf16[256,512]{1,0:T(8,128)(2,1)S(1)}, u32[]{:S(2)}, u32[]{:S(2)}) collective-permute-start(bf16[256,512]{1,0:T(8,128)(2,1)S(1)} %collective-permute-done.4.k1_ref.v1_ref), channel_id=1, source_target_pairs={{0,4},{4,8},{8,12},{12,16},{16,20},{20,24},{24,28},{28,32},{32,36}... | collective-permute-start | bytes 786440 | tf_op jit(solution)/shard_map/ppermute | solution.py:105
  84.7 0.8 copy.63.rel_ref
  85.5 8.5 %collective-permute-done.k1_ref.v1_ref = bf16[256,512]{1,0:T(8,128)(2,1)S(1)} collective-permute-done((bf16[256,512]{1,0:T(8,128)(2,1)S(1)}, bf16[256,512]{1,0:T(8,128)(2,1)S(1)}, u32[]{:S(2)}, u32[]{:S(2)}) %collective-permute-start) | collective-permute-done | bytes 262176 | tf_op jit(solution)/shard_map/ppermute | solution.py:105
  94.0 1.9 %collective-permute-start.1 = (bf16[256,512]{1,0:T(8,128)(2,1)S(1)}, bf16[256,512]{1,0:T(8,128)(2,1)S(1)}, u32[]{:S(2)}, u32[]{:S(2)}) collective-permute-start(bf16[256,512]{1,0:T(8,128)(2,1)S(1)} %collective-permute-done.k1_ref.v1_ref), channel_id=1, source_target_pairs={{0,4},{4,8},{8,12},{12,16},{16,20},{20,24},{24,28},{28,32},{32,36}... | collective-permute-start | bytes 786440 | tf_op jit(solution)/shard_map/ppermute | solution.py:105
  95.9 2.6 %collective-permute-done.5.k2_ref.v2_ref = bf16[256,512]{1,0:T(8,128)(2,1)S(1)} collective-permute-done((bf16[256,512]{1,0:T(8,128)(2,1)S(1)}, bf16[256,512]{1,0:T(8,128)(2,1)S(1)}, u32[]{:S(2)}, u32[]{:S(2)}) %collective-permute-start.5) | collective-permute-done | bytes 262176 | tf_op jit(solution)/shard_map/ppermute | solution.py:105
  98.5 0.7 copy-done.4
  99.2 6.3 %shard_map.77 = (f32[256,512]{1,0:T(8,128)}, f32[2,256,256]{2,1,0:T(8,128)}, f32[2,256,256]{2,1,0:T(8,128)}, f32[2,256,256]{2,1,0:T(8,128)}) custom-call(s32[256,1]{1,0:T(8,128)} %copy.63.rel_ref, bf16[256,1536]{1,0:T(8,128)(2,1)} %bitcast.46, bf16[256,1536]{1,0:T(8,128)(2,1)} %bitcast.47, bf16[256,1536]{1,0:T(8,128)(2,1)} %bitcast.48, ...), custom_call_target="tpu_custom_call" | custom-call | tf_op jit(solution)/shard_map/pallas_call | solution.py:78
  105.6 1.1 convert_element_type.54
  106.6 3.4 %collective-permute-start.6 = (bf16[2,256,256]{2,1,0:T(8,128)(2,1)S(1)}, bf16[2,256,256]{2,1,0:T(8,128)(2,1)S(1)}, u32[]{:S(2)}, u32[]{:S(2)}) collective-permute-start(bf16[2,256,256]{2,1,0:T(8,128)(2,1)S(1)} %convert_element_type.54), channel_id=1, source_target_pairs={{4,0},{8,4},{12,8},{16,12},{20,16},{24,20},{28,24},{32,28},{36,32}... | collective-permute-start | bytes 786440 | tf_op jit(solution)/shard_map/ppermute | solution.py:105
  110.0 0.7 copy-done.5
  110.7 6.3 %shard_map.76 = (f32[256,512]{1,0:T(8,128)}, f32[2,256,256]{2,1,0:T(8,128)}, f32[2,256,256]{2,1,0:T(8,128)}, f32[2,256,256]{2,1,0:T(8,128)}) custom-call(s32[256,1]{1,0:T(8,128)} %copy.63.rel_ref, bf16[256,1536]{1,0:T(8,128)(2,1)} %bitcast.51, bf16[256,1536]{1,0:T(8,128)(2,1)} %bitcast.52, bf16[256,1536]{1,0:T(8,128)(2,1)} %bitcast.53, ...), custom_call_target="tpu_custom_call" | custom-call | tf_op jit(solution)/shard_map/pallas_call | solution.py:78
  117.1 1.1 convert_element_type.47
  118.2 2.1 %collective-permute-start.2 = (bf16[2,256,256]{2,1,0:T(8,128)(2,1)S(1)}, bf16[2,256,256]{2,1,0:T(8,128)(2,1)S(1)}, u32[]{:S(2)}, u32[]{:S(2)}) collective-permute-start(bf16[2,256,256]{2,1,0:T(8,128)(2,1)S(1)} %convert_element_type.47), channel_id=1, source_target_pairs={{4,0},{8,4},{12,8},{16,12},{20,16},{24,20},{28,24},{32,28},{36,32}... | collective-permute-start | bytes 786440 | tf_op jit(solution)/shard_map/ppermute | solution.py:105
  120.4 2.1 %collective-permute-start.7 = (bf16[2,256,256]{2,1,0:T(8,128)(2,1)S(1)}, bf16[2,256,256]{2,1,0:T(8,128)(2,1)S(1)}, u32[]{:S(2)}, u32[]{:S(2)}) collective-permute-start(bf16[2,256,256]{2,1,0:T(8,128)(2,1)S(1)} %add_convert_fusion.1), channel_id=1, source_target_pairs={{4,0},{8,4},{12,8},{16,12},{20,16},{24,20},{28,24},{32,28},{36,32}... | collective-permute-start | bytes 786440 | tf_op jit(solution)/shard_map/ppermute | solution.py:105
  122.5 6.7 %collective-permute-done.2 = bf16[2,256,256]{2,1,0:T(8,128)(2,1)S(1)} collective-permute-done((bf16[2,256,256]{2,1,0:T(8,128)(2,1)S(1)}, bf16[2,256,256]{2,1,0:T(8,128)(2,1)S(1)}, u32[]{:S(2)}, u32[]{:S(2)}) %collective-permute-start.2) | collective-permute-done | bytes 262176 | tf_op jit(solution)/shard_map/ppermute | solution.py:105
  129.2 4.0 %collective-permute-start.3 = (bf16[2,256,256]{2,1,0:T(8,128)(2,1)S(1)}, bf16[2,256,256]{2,1,0:T(8,128)(2,1)S(1)}, u32[]{:S(2)}, u32[]{:S(2)}) collective-permute-start(bf16[2,256,256]{2,1,0:T(8,128)(2,1)S(1)} %add_convert_fusion.3), channel_id=1, source_target_pairs={{4,0},{8,4},{12,8},{16,12},{20,16},{24,20},{28,24},{32,28},{36,32}... | collective-permute-start | bytes 786440 | tf_op jit(solution)/shard_map/ppermute | solution.py:105
  133.2 1.2 collective-permute-done.7
  134.6 0.5 broadcast
  135.1 1.0 reduce.1
  136.2 1.2 reshape.56
  137.4 3.8 %all-to-all-start.3 = ((bf16[4,2,32768]{2,1,0:T(2,128)(2,1)}), bf16[4,2,32768]{2,1,0:T(2,128)(2,1)S(1)}, u32[]{:S(2)}, u32[]{:S(2)}) async-start(bf16[4,2,32768]{2,1,0:T(2,128)(2,1)} %reshape.56), calls=%async_computation.3 | async-start | bytes 1048576 | tf_op jit(solution)/shard_map/all_to_all | solution.py:132
  141.4 1.0 reduce
  142.4 1.2 reshape.54
  143.6 6.4 %all-to-all-done.3 = bf16[4,2,32768]{2,1,0:T(2,128)(2,1)S(1)} async-done(((bf16[4,2,32768]{2,1,0:T(2,128)(2,1)}), bf16[4,2,32768]{2,1,0:T(2,128)(2,1)S(1)}, u32[]{:S(2)}, u32[]{:S(2)}) %all-to-all-start.3) | async-done | bytes 524320 | tf_op jit(solution)/shard_map/all_to_all | solution.py:132
  149.9 3.7 %all-to-all-start.1 = ((bf16[4,2,32768]{2,1,0:T(2,128)(2,1)}), bf16[4,2,32768]{2,1,0:T(2,128)(2,1)S(1)}, u32[]{:S(2)}, u32[]{:S(2)}) async-start(bf16[4,2,32768]{2,1,0:T(2,128)(2,1)} %reshape.54), calls=%async_computation.1 | async-start | bytes 1048576 | tf_op jit(solution)/shard_map/all_to_all | solution.py:132
  153.6 0.5 reshape.57
  154.3 7.9 %all-to-all-done.1 = bf16[4,2,32768]{2,1,0:T(2,128)(2,1)S(1)} async-done(((bf16[4,2,32768]{2,1,0:T(2,128)(2,1)}), bf16[4,2,32768]{2,1,0:T(2,128)(2,1)S(1)}, u32[]{:S(2)}, u32[]{:S(2)}) %all-to-all-start.1) | async-done | bytes 524320 | tf_op jit(solution)/shard_map/all_to_all | solution.py:132
  162.2 0.5 reshape.55
  163.3 0.9 reshape.53
  164.2 0.5 copy.71
  164.7 1.2 reshape.51
  166.2 0.9 reshape.52
  (55 shorter events, 2.6 us)
Async XLA Ops:
  2.9 1.0 copy-start.8
  3.3 1.1 copy-start.9
  7.6 15.1 %all-to-all-start.2 = ((bf16[64,4,1536]{2,0,1:T(8,128)(2,1)}), bf16[64,4,1536]{2,0,1:T(8,128)(2,1)S(1)}, u32[]{:S(2)}, u32[]{:S(2)}) async-start(bf16[64,4,1536]{2,0,1:T(8,128)(2,1)} %pad_maximum_fusion.1), calls=%async_computation.2 | async-start | bytes 1572864 | tf_op jit(solution)/shard_map/all_to_all | solution.py:110
  12.4 72.2 %copy-start.14 = (s32[256]{0:T(256)S(1)}, s32[256]{0:T(256)}, u32[]{:S(2)}) copy-start(s32[256]{0:T(256)} %param.9) | copy-start | bytes 3076
  22.7 3.5 %copy-start = (bf16[64,4,1536]{2,0,1:T(8,128)(2,1)}, bf16[64,4,1536]{2,0,1:T(8,128)(2,1)S(1)}, u32[]{:S(2)}) copy-start(bf16[64,4,1536]{2,0,1:T(8,128)(2,1)S(1)} %all-to-all-done.2) | copy-start | bytes 2359300
  22.7 58.0 %all-to-all-start = ((bf16[64,4,1536]{2,0,1:T(8,128)(2,1)}), bf16[64,4,1536]{2,0,1:T(8,128)(2,1)S(1)}, u32[]{:S(2)}, u32[]{:S(2)}) async-start(bf16[64,4,1536]{2,0,1:T(8,128)(2,1)} %pad_maximum_fusion), calls=%async_computation | async-start | bytes 1572864 | tf_op jit(solution)/shard_map/all_to_all | solution.py:110
  26.2 56.5 %collective-permute-start.4 = (bf16[256,512]{1,0:T(8,128)(2,1)S(1)}, bf16[256,512]{1,0:T(8,128)(2,1)S(1)}, u32[]{:S(2)}, u32[]{:S(2)}) collective-permute-start(bf16[256,512]{1,0:T(8,128)(2,1)S(1)} %slice.83), channel_id=1, source_target_pairs={{0,4},{4,8},{8,12},{12,16},{16,20},{20,24},{24,28},{28,32},{32,36}... | collective-permute-start | bytes 786440 | tf_op jit(solution)/shard_map/ppermute | solution.py:105
  80.7 24.8 %copy-start.1 = (bf16[64,4,1536]{2,0,1:T(8,128)(2,1)}, bf16[64,4,1536]{2,0,1:T(8,128)(2,1)S(1)}, u32[]{:S(2)}) copy-start(bf16[64,4,1536]{2,0,1:T(8,128)(2,1)S(1)} %all-to-all-done) | copy-start | bytes 2359300
  80.8 13.2 %collective-permute-start = (bf16[256,512]{1,0:T(8,128)(2,1)S(1)}, bf16[256,512]{1,0:T(8,128)(2,1)S(1)}, u32[]{:S(2)}, u32[]{:S(2)}) collective-permute-start(bf16[256,512]{1,0:T(8,128)(2,1)S(1)} %slice.76), channel_id=1, source_target_pairs={{0,4},{4,8},{8,12},{12,16},{16,20},{20,24},{24,28},{28,32},{32,36}... | collective-permute-start | bytes 786440 | tf_op jit(solution)/shard_map/ppermute | solution.py:105
  82.7 15.8 %copy-start.3 = (bf16[256,512]{1,0:T(8,128)(2,1)}, bf16[256,512]{1,0:T(8,128)(2,1)S(1)}, u32[]{:S(2)}) copy-start(bf16[256,512]{1,0:T(8,128)(2,1)S(1)} %collective-permute-done.4.k1_ref.v1_ref) | copy-start | bytes 786436
  82.7 15.8 %collective-permute-start.5 = (bf16[256,512]{1,0:T(8,128)(2,1)S(1)}, bf16[256,512]{1,0:T(8,128)(2,1)S(1)}, u32[]{:S(2)}, u32[]{:S(2)}) collective-permute-start(bf16[256,512]{1,0:T(8,128)(2,1)S(1)} %collective-permute-done.4.k1_ref.v1_ref), channel_id=1, source_target_pairs={{0,4},{4,8},{8,12},{12,16},{16,20},{20,24},{24,28},{28,32},{32,36}... | collective-permute-start | bytes 786440 | tf_op jit(solution)/shard_map/ppermute | solution.py:105
  93.9 11.6 %copy-start.2 = (bf16[256,512]{1,0:T(8,128)(2,1)}, bf16[256,512]{1,0:T(8,128)(2,1)S(1)}, u32[]{:S(2)}) copy-start(bf16[256,512]{1,0:T(8,128)(2,1)S(1)} %collective-permute-done.k1_ref.v1_ref) | copy-start | bytes 786436
  94.0 16.1 %collective-permute-start.1 = (bf16[256,512]{1,0:T(8,128)(2,1)S(1)}, bf16[256,512]{1,0:T(8,128)(2,1)S(1)}, u32[]{:S(2)}, u32[]{:S(2)}) collective-permute-start(bf16[256,512]{1,0:T(8,128)(2,1)S(1)} %collective-permute-done.k1_ref.v1_ref), channel_id=1, source_target_pairs={{0,4},{4,8},{8,12},{12,16},{16,20},{20,24},{24,28},{28,32},{32,36}... | collective-permute-start | bytes 786440 | tf_op jit(solution)/shard_map/ppermute | solution.py:105
  98.5 0.7 copy-start.4
  106.6 13.7 %collective-permute-start.6 = (bf16[2,256,256]{2,1,0:T(8,128)(2,1)S(1)}, bf16[2,256,256]{2,1,0:T(8,128)(2,1)S(1)}, u32[]{:S(2)}, u32[]{:S(2)}) collective-permute-start(bf16[2,256,256]{2,1,0:T(8,128)(2,1)S(1)} %convert_element_type.54), channel_id=1, source_target_pairs={{4,0},{8,4},{12,8},{16,12},{20,16},{24,20},{28,24},{32,28},{36,32}... | collective-permute-start | bytes 786440 | tf_op jit(solution)/shard_map/ppermute | solution.py:105
  110.0 0.7 copy-start.5
  110.7 9.6 %copy-start.12 = (f32[2,256,256]{2,1,0:T(8,128)S(1)}, f32[2,256,256]{2,1,0:T(8,128)}, u32[]{:S(2)}) copy-start(f32[2,256,256]{2,1,0:T(8,128)} %get-tuple-element.17) | copy-start | bytes 1572868
  117.1 5.4 %copy-start.7 = (f32[256,512]{1,0:T(8,128)S(1)}, f32[256,512]{1,0:T(8,128)}, u32[]{:S(2)}) copy-start(f32[256,512]{1,0:T(8,128)} %get-tuple-element.15) | copy-start | bytes 1572868
  118.2 11.0 %copy-start.13 = (f32[2,256,256]{2,1,0:T(8,128)S(1)}, f32[2,256,256]{2,1,0:T(8,128)}, u32[]{:S(2)}) copy-start(f32[2,256,256]{2,1,0:T(8,128)} %get-tuple-element.13) | copy-start | bytes 1572868
  118.2 10.9 %collective-permute-start.2 = (bf16[2,256,256]{2,1,0:T(8,128)(2,1)S(1)}, bf16[2,256,256]{2,1,0:T(8,128)(2,1)S(1)}, u32[]{:S(2)}, u32[]{:S(2)}) collective-permute-start(bf16[2,256,256]{2,1,0:T(8,128)(2,1)S(1)} %convert_element_type.47), channel_id=1, source_target_pairs={{4,0},{8,4},{12,8},{16,12},{20,16},{24,20},{28,24},{32,28},{36,32}... | collective-permute-start | bytes 786440 | tf_op jit(solution)/shard_map/ppermute | solution.py:105
  120.4 14.1 %copy-start.11 = (f32[2,256,256]{2,1,0:T(8,128)S(1)}, f32[2,256,256]{2,1,0:T(8,128)}, u32[]{:S(2)}) copy-start(f32[2,256,256]{2,1,0:T(8,128)} %get-tuple-element.16) | copy-start | bytes 1572868
  120.4 14.1 %collective-permute-start.7 = (bf16[2,256,256]{2,1,0:T(8,128)(2,1)S(1)}, bf16[2,256,256]{2,1,0:T(8,128)(2,1)S(1)}, u32[]{:S(2)}, u32[]{:S(2)}) collective-permute-start(bf16[2,256,256]{2,1,0:T(8,128)(2,1)S(1)} %add_convert_fusion.1), channel_id=1, source_target_pairs={{4,0},{8,4},{12,8},{16,12},{20,16},{24,20},{28,24},{32,28},{36,32}... | collective-permute-start | bytes 786440 | tf_op jit(solution)/shard_map/ppermute | solution.py:105
  129.2 11.9 %collective-permute-start.3 = (bf16[2,256,256]{2,1,0:T(8,128)(2,1)S(1)}, bf16[2,256,256]{2,1,0:T(8,128)(2,1)S(1)}, u32[]{:S(2)}, u32[]{:S(2)}) collective-permute-start(bf16[2,256,256]{2,1,0:T(8,128)(2,1)S(1)} %add_convert_fusion.3), channel_id=1, source_target_pairs={{4,0},{8,4},{12,8},{16,12},{20,16},{24,20},{28,24},{32,28},{36,32}... | collective-permute-start | bytes 786440 | tf_op jit(solution)/shard_map/ppermute | solution.py:105
  136.2 5.0 %copy-start.6 = (f32[256,512]{1,0:T(8,128)S(1)}, f32[256,512]{1,0:T(8,128)}, u32[]{:S(2)}) copy-start(f32[256,512]{1,0:T(8,128)} %get-tuple-element.11) | copy-start | bytes 1572868
  137.4 3.8 %copy-start.10 = (f32[2,256,256]{2,1,0:T(8,128)S(1)}, f32[2,256,256]{2,1,0:T(8,128)}, u32[]{:S(2)}) copy-start(f32[2,256,256]{2,1,0:T(8,128)} %get-tuple-element.12) | copy-start | bytes 1572868
  137.4 12.6 %all-to-all-start.3 = ((bf16[4,2,32768]{2,1,0:T(2,128)(2,1)}), bf16[4,2,32768]{2,1,0:T(2,128)(2,1)S(1)}, u32[]{:S(2)}, u32[]{:S(2)}) async-start(bf16[4,2,32768]{2,1,0:T(2,128)(2,1)} %reshape.56), calls=%async_computation.3 | async-start | bytes 1048576 | tf_op jit(solution)/shard_map/all_to_all | solution.py:132
  149.9 12.3 %all-to-all-start.1 = ((bf16[4,2,32768]{2,1,0:T(2,128)(2,1)}), bf16[4,2,32768]{2,1,0:T(2,128)(2,1)S(1)}, u32[]{:S(2)}, u32[]{:S(2)}) async-start(bf16[4,2,32768]{2,1,0:T(2,128)(2,1)} %reshape.54), calls=%async_computation.1 | async-start | bytes 1048576 | tf_op jit(solution)/shard_map/all_to_all | solution.py:132

commit v8 on v6

--- a/solution.py
+++ b/solution.py
@@ -10,7 +10,7 @@
 WINDOW = 512
 SPAN = 2
 CHAIN = False
-CHUNKS = 2
+CHUNKS = 4
 
 score_scale = 168.0 ** (-0.5)
 NT = (((1,), (1,)), ((), ()))

time: 153 us -> 193 us (1.26)
  the two profiles are of different devices: /device:TPU:62 before, /device:TPU:184 now
where the time goes in v8:
time: 193 us; the launch traced here: 191 us
  starting transfers between devices  94.2 us (49%)
  waiting for transfers between devices  49.2 us (25%)
  local copies, waits for them, and re-layouts  19 us (10%)
  Pallas kernels  15.7 us (8%)
  other arithmetic  11.3 us (6%)
    ppermute x16, starting transfers between devices, passed_along(): return lax.ppermute(block, axis, route)  65.9 us
    all_to_all x4, waiting for transfers between devices, chunk_pass(): lax.all_to_all(out_loc, 'head', split_axis=0, concat_axis=1, tiled=True)  21.8 us
    all_to_all x4, waiting for transfers between devices, chunk_pass(): lax.all_to_all(x_in, 'head', split_axis=1, concat_axis=0, tiled=True)  19.4 us
    pallas_call x4, Pallas kernels, attend(): pl.pallas_call(attn_kernel, grid=(groups,), in_specs=[pl.BlockSpec((tok,...  15.7 us
    all_to_all x4, starting transfers between devices, chunk_pass(): lax.all_to_all(out_loc, 'head', split_axis=0, concat_axis=1, tiled=True)  14.3 us
    all_to_all x4, starting transfers between devices, chunk_pass(): lax.all_to_all(x_in, 'head', split_axis=1, concat_axis=0, tiled=True)  14 us
    unnamed x68, local copies, waits for them, and re-layouts  8.93 us
    ppermute x16, waiting for transfers between devices, passed_along(): return lax.ppermute(block, axis, route)  7.95 us
  transfers between devices with their start and end apart: 24, of which 8 were waited for; matrix products, arithmetic and copies ran while one was open for 9% of the time, Pallas kernels for 8%

profile of v8, /device:TPU:184, one launch (start us, length us, event | category | flops | bytes accessed | tf_op | source)
XLA Modules:
  0.0 191.0 jit_solution(14606666921434082893)
XLA Ops:
  0.6 1.2 reshape.59
  7.3 3.6 %all-to-all-start.2 = ((bf16[64,4,768]{2,0,1:T(8,128)(2,1)}), bf16[64,4,768]{2,0,1:T(8,128)(2,1)S(1)}, u32[]{:S(2)}, u32[]{:S(2)}) async-start(bf16[64,4,768]{2,0,1:T(8,128)(2,1)} %pad_maximum_fusion.2), calls=%async_computation.2 | async-start | bytes 786432 | tf_op jit(solution)/shard_map/all_to_all | solution.py:110
  11.8 6.5 %all-to-all-done.2 = bf16[64,4,768]{2,0,1:T(8,128)(2,1)S(1)} async-done(((bf16[64,4,768]{2,0,1:T(8,128)(2,1)}), bf16[64,4,768]{2,0,1:T(8,128)(2,1)S(1)}, u32[]{:S(2)}, u32[]{:S(2)}) %all-to-all-start.2) | async-done | bytes 393248 | tf_op jit(solution)/shard_map/all_to_all | solution.py:110
  18.3 3.5 %all-to-all-start.4 = ((bf16[64,4,768]{2,0,1:T(8,128)(2,1)}), bf16[64,4,768]{2,0,1:T(8,128)(2,1)S(1)}, u32[]{:S(2)}, u32[]{:S(2)}) async-start(bf16[64,4,768]{2,0,1:T(8,128)(2,1)} %pad_maximum_fusion.3), calls=%async_computation.4 | async-start | bytes 786432 | tf_op jit(solution)/shard_map/all_to_all | solution.py:110
  22.7 6.5 %all-to-all-done.4 = bf16[64,4,768]{2,0,1:T(8,128)(2,1)S(1)} async-done(((bf16[64,4,768]{2,0,1:T(8,128)(2,1)}), bf16[64,4,768]{2,0,1:T(8,128)(2,1)S(1)}, u32[]{:S(2)}, u32[]{:S(2)}) %all-to-all-start.4) | async-done | bytes 393248 | tf_op jit(solution)/shard_map/all_to_all | solution.py:110
  29.2 3.5 %all-to-all-start = ((bf16[64,4,768]{2,0,1:T(8,128)(2,1)}), bf16[64,4,768]{2,0,1:T(8,128)(2,1)S(1)}, u32[]{:S(2)}, u32[]{:S(2)}) async-start(bf16[64,4,768]{2,0,1:T(8,128)(2,1)} %pad_maximum_fusion.1), calls=%async_computation | async-start | bytes 786432 | tf_op jit(solution)/shard_map/all_to_all | solution.py:110
  33.6 6.5 %all-to-all-done = bf16[64,4,768]{2,0,1:T(8,128)(2,1)S(1)} async-done(((bf16[64,4,768]{2,0,1:T(8,128)(2,1)}), bf16[64,4,768]{2,0,1:T(8,128)(2,1)S(1)}, u32[]{:S(2)}, u32[]{:S(2)}) %all-to-all-start) | async-done | bytes 393248 | tf_op jit(solution)/shard_map/all_to_all | solution.py:110
  40.0 3.5 %all-to-all-start.6 = ((bf16[64,4,768]{2,0,1:T(8,128)(2,1)}), bf16[64,4,768]{2,0,1:T(8,128)(2,1)S(1)}, u32[]{:S(2)}, u32[]{:S(2)}) async-start(bf16[64,4,768]{2,0,1:T(8,128)(2,1)} %pad_maximum_fusion.4), calls=%async_computation.6 | async-start | bytes 786432 | tf_op jit(solution)/shard_map/all_to_all | solution.py:110
  43.5 3.6 %collective-permute-start.5 = (bf16[256,256]{1,0:T(8,128)(2,1)S(1)}, bf16[256,256]{1,0:T(8,128)(2,1)S(1)}, u32[]{:S(2)}, u32[]{:S(2)}) collective-permute-start(bf16[256,256]{1,0:T(8,128)(2,1)S(1)} %slice.143), channel_id=1, source_target_pairs={{0,8},{4,12},{8,16},{12,20},{16,24},{20,28},{24,32},{28,36},{32,40... | collective-permute-start | bytes 393224 | tf_op jit(solution)/shard_map/ppermute | solution.py:105
  47.2 3.5 %collective-permute-start.4 = (bf16[256,256]{1,0:T(8,128)(2,1)S(1)}, bf16[256,256]{1,0:T(8,128)(2,1)S(1)}, u32[]{:S(2)}, u32[]{:S(2)}) collective-permute-start(bf16[256,256]{1,0:T(8,128)(2,1)S(1)} %slice.143), channel_id=1, source_target_pairs={{0,4},{4,8},{8,12},{12,16},{16,20},{20,24},{24,28},{28,32},{32,36}... | collective-permute-start | bytes 393224 | tf_op jit(solution)/shard_map/ppermute | solution.py:105
  50.7 5.7 %collective-permute-start.9 = (bf16[256,256]{1,0:T(8,128)(2,1)S(1)}, bf16[256,256]{1,0:T(8,128)(2,1)S(1)}, u32[]{:S(2)}, u32[]{:S(2)}) collective-permute-start(bf16[256,256]{1,0:T(8,128)(2,1)S(1)} %slice.150), channel_id=1, source_target_pairs={{0,8},{4,12},{8,16},{12,20},{16,24},{20,28},{24,32},{28,36},{32,40... | collective-permute-start | bytes 393224 | tf_op jit(solution)/shard_map/ppermute | solution.py:105
  56.4 2.6 %collective-permute-start.8 = (bf16[256,256]{1,0:T(8,128)(2,1)S(1)}, bf16[256,256]{1,0:T(8,128)(2,1)S(1)}, u32[]{:S(2)}, u32[]{:S(2)}) collective-permute-start(bf16[256,256]{1,0:T(8,128)(2,1)S(1)} %slice.150), channel_id=1, source_target_pairs={{0,4},{4,8},{8,12},{12,16},{16,20},{20,24},{24,28},{28,32},{32,36}... | collective-permute-start | bytes 393224 | tf_op jit(solution)/shard_map/ppermute | solution.py:105
  59.0 2.7 %collective-permute-start.1 = (bf16[256,256]{1,0:T(8,128)(2,1)S(1)}, bf16[256,256]{1,0:T(8,128)(2,1)S(1)}, u32[]{:S(2)}, u32[]{:S(2)}) collective-permute-start(bf16[256,256]{1,0:T(8,128)(2,1)S(1)} %slice.136), channel_id=1, source_target_pairs={{0,8},{4,12},{8,16},{12,20},{16,24},{20,28},{24,32},{28,36},{32,40... | collective-permute-start | bytes 393224 | tf_op jit(solution)/shard_map/ppermute | solution.py:105
  61.8 2.6 %collective-permute-start = (bf16[256,256]{1,0:T(8,128)(2,1)S(1)}, bf16[256,256]{1,0:T(8,128)(2,1)S(1)}, u32[]{:S(2)}, u32[]{:S(2)}) collective-permute-start(bf16[256,256]{1,0:T(8,128)(2,1)S(1)} %slice.136), channel_id=1, source_target_pairs={{0,4},{4,8},{8,12},{12,16},{16,20},{20,24},{24,28},{28,32},{32,36}... | collective-permute-start | bytes 393224 | tf_op jit(solution)/shard_map/ppermute | solution.py:105
  64.4 7.9 %collective-permute-done.1.k2_ref.v2_ref = bf16[256,256]{1,0:T(8,128)(2,1)S(1)} collective-permute-done((bf16[256,256]{1,0:T(8,128)(2,1)S(1)}, bf16[256,256]{1,0:T(8,128)(2,1)S(1)}, u32[]{:S(2)}, u32[]{:S(2)}) %collective-permute-start.1) | collective-permute-done | bytes 131104 | tf_op jit(solution)/shard_map/ppermute | solution.py:105
  72.4 5.6 %collective-permute-start.13 = (bf16[256,256]{1,0:T(8,128)(2,1)S(1)}, bf16[256,256]{1,0:T(8,128)(2,1)S(1)}, u32[]{:S(2)}, u32[]{:S(2)}) collective-permute-start(bf16[256,256]{1,0:T(8,128)(2,1)S(1)} %slice.157), channel_id=1, source_target_pairs={{0,8},{4,12},{8,16},{12,20},{16,24},{20,28},{24,32},{28,36},{32,40... | collective-permute-start | bytes 393224 | tf_op jit(solution)/shard_map/ppermute | solution.py:105
  78.0 1.9 %collective-permute-start.12 = (bf16[256,256]{1,0:T(8,128)(2,1)S(1)}, bf16[256,256]{1,0:T(8,128)(2,1)S(1)}, u32[]{:S(2)}, u32[]{:S(2)}) collective-permute-start(bf16[256,256]{1,0:T(8,128)(2,1)S(1)} %slice.157), channel_id=1, source_target_pairs={{0,4},{4,8},{8,12},{12,16},{16,20},{20,24},{24,28},{28,32},{32,36}... | collective-permute-start | bytes 393224 | tf_op jit(solution)/shard_map/ppermute | solution.py:105
  80.7 3.9 %shard_map.76 = (f32[256,256]{1,0:T(8,128)}, f32[2,256,128]{2,1,0:T(8,128)}, f32[2,256,128]{2,1,0:T(8,128)}, f32[2,256,128]{2,1,0:T(8,128)}) custom-call(s32[256,1]{1,0:T(8,128)} %copy.105.rel_ref, bf16[256,768]{1,0:T(8,128)(2,1)} %bitcast.105, bf16[256,768]{1,0:T(8,128)(2,1)} %bitcast.106, bf16[256,768]{1,0:T(8,128)(2,1)} %bitcast.107, ...), custom_call_target="tpu_custom_call" | custom-call | tf_op jit(solution)/shard_map/pallas_call | solution.py:78
  84.6 1.0 convert_element_type.93
  85.7 3.1 %collective-permute-start.3 = (bf16[2,256,128]{2,1,0:T(8,128)(2,1)S(1)}, bf16[2,256,128]{2,1,0:T(8,128)(2,1)S(1)}, u32[]{:S(2)}, u32[]{:S(2)}) collective-permute-start(bf16[2,256,128]{2,1,0:T(8,128)(2,1)S(1)} %convert_element_type.95), channel_id=1, source_target_pairs={{8,0},{12,4},{16,8},{20,12},{24,16},{28,20},{32,24},{36,28},{40,32... | collective-permute-start | bytes 393224 | tf_op jit(solution)/shard_map/ppermute | solution.py:105
  88.8 2.7 %collective-permute-start.2 = (bf16[2,256,128]{2,1,0:T(8,128)(2,1)S(1)}, bf16[2,256,128]{2,1,0:T(8,128)(2,1)S(1)}, u32[]{:S(2)}, u32[]{:S(2)}) collective-permute-start(bf16[2,256,128]{2,1,0:T(8,128)(2,1)S(1)} %convert_element_type.93), channel_id=1, source_target_pairs={{4,0},{8,4},{12,8},{16,12},{20,16},{24,20},{28,24},{32,28},{36,32}... | collective-permute-start | bytes 393224 | tf_op jit(solution)/shard_map/ppermute | solution.py:105
  91.6 3.9 %shard_map.78 = (f32[256,256]{1,0:T(8,128)}, f32[2,256,128]{2,1,0:T(8,128)}, f32[2,256,128]{2,1,0:T(8,128)}, f32[2,256,128]{2,1,0:T(8,128)}) custom-call(s32[256,1]{1,0:T(8,128)} %copy.105.rel_ref, bf16[256,768]{1,0:T(8,128)(2,1)} %bitcast.95, bf16[256,768]{1,0:T(8,128)(2,1)} %bitcast.96, bf16[256,768]{1,0:T(8,128)(2,1)} %bitcast.97, ...), custom_call_target="tpu_custom_call" | custom-call | tf_op jit(solution)/shard_map/pallas_call | solution.py:78
  95.6 1.0 convert_element_type.106
  96.6 0.9 copy-done.16
  97.6 5.1 %collective-permute-start.11 = (bf16[2,256,128]{2,1,0:T(8,128)(2,1)S(1)}, bf16[2,256,128]{2,1,0:T(8,128)(2,1)S(1)}, u32[]{:S(2)}, u32[]{:S(2)}) collective-permute-start(bf16[2,256,128]{2,1,0:T(8,128)(2,1)S(1)} %convert_element_type.109), channel_id=1, source_target_pairs={{8,0},{12,4},{16,8},{20,12},{24,16},{28,20},{32,24},{36,28},{40,32... | collective-permute-start | bytes 393224 | tf_op jit(solution)/shard_map/ppermute | solution.py:105
  102.7 3.9 %shard_map.77 = (f32[256,256]{1,0:T(8,128)}, f32[2,256,128]{2,1,0:T(8,128)}, f32[2,256,128]{2,1,0:T(8,128)}, f32[2,256,128]{2,1,0:T(8,128)}) custom-call(s32[256,1]{1,0:T(8,128)} %copy.105.rel_ref, bf16[256,768]{1,0:T(8,128)(2,1)} %bitcast.90, bf16[256,768]{1,0:T(8,128)(2,1)} %bitcast.91, bf16[256,768]{1,0:T(8,128)(2,1)} %bitcast.92, ...), custom_call_target="tpu_custom_call" | custom-call | tf_op jit(solution)/shard_map/pallas_call | solution.py:78
  106.7 1.0 convert_element_type.99
  107.7 0.9 copy-done.17
  108.7 9.0 %collective-permute-start.10 = (bf16[2,256,128]{2,1,0:T(8,128)(2,1)S(1)}, bf16[2,256,128]{2,1,0:T(8,128)(2,1)S(1)}, u32[]{:S(2)}, u32[]{:S(2)}) collective-permute-start(bf16[2,256,128]{2,1,0:T(8,128)(2,1)S(1)} %convert_element_type.107), channel_id=1, source_target_pairs={{4,0},{8,4},{12,8},{16,12},{20,16},{24,20},{28,24},{32,28},{36,32}... | collective-permute-start | bytes 393224 | tf_op jit(solution)/shard_map/ppermute | solution.py:105
  117.7 10.7 %collective-permute-start.7 = (bf16[2,256,128]{2,1,0:T(8,128)(2,1)S(1)}, bf16[2,256,128]{2,1,0:T(8,128)(2,1)S(1)}, u32[]{:S(2)}, u32[]{:S(2)}) collective-permute-start(bf16[2,256,128]{2,1,0:T(8,128)(2,1)S(1)} %convert_element_type.102), channel_id=1, source_target_pairs={{8,0},{12,4},{16,8},{20,12},{24,16},{28,20},{32,24},{36,28},{40,32... | collective-permute-start | bytes 393224 | tf_op jit(solution)/shard_map/ppermute | solution.py:105
  128.4 3.9 %shard_map.79 = (f32[256,256]{1,0:T(8,128)}, f32[2,256,128]{2,1,0:T(8,128)}, f32[2,256,128]{2,1,0:T(8,128)}, f32[2,256,128]{2,1,0:T(8,128)}) custom-call(s32[256,1]{1,0:T(8,128)} %copy.105.rel_ref, bf16[256,768]{1,0:T(8,128)(2,1)} %bitcast.100, bf16[256,768]{1,0:T(8,128)(2,1)} %bitcast.101, bf16[256,768]{1,0:T(8,128)(2,1)} %bitcast.102, ...), custom_call_target="tpu_custom_call" | custom-call | tf_op jit(solution)/shard_map/pallas_call | solution.py:78
  132.3 1.0 convert_element_type.113
  133.4 0.9 copy-done.15
  134.3 3.2 %collective-permute-start.6 = (bf16[2,256,128]{2,1,0:T(8,128)(2,1)S(1)}, bf16[2,256,128]{2,1,0:T(8,128)(2,1)S(1)}, u32[]{:S(2)}, u32[]{:S(2)}) collective-permute-start(bf16[2,256,128]{2,1,0:T(8,128)(2,1)S(1)} %convert_element_type.100), channel_id=1, source_target_pairs={{4,0},{8,4},{12,8},{16,12},{20,16},{24,20},{28,24},{32,28},{36,32}... | collective-permute-start | bytes 393224 | tf_op jit(solution)/shard_map/ppermute | solution.py:105
  137.5 1.9 %collective-permute-start.15 = (bf16[2,256,128]{2,1,0:T(8,128)(2,1)S(1)}, bf16[2,256,128]{2,1,0:T(8,128)(2,1)S(1)}, u32[]{:S(2)}, u32[]{:S(2)}) collective-permute-start(bf16[2,256,128]{2,1,0:T(8,128)(2,1)S(1)} %convert_element_type.116), channel_id=1, source_target_pairs={{8,0},{12,4},{16,8},{20,12},{24,16},{28,20},{32,24},{36,28},{40,32... | collective-permute-start | bytes 393224 | tf_op jit(solution)/shard_map/ppermute | solution.py:105
  141.0 0.9 reshape.76
  141.9 4.1 %all-to-all-start.1 = ((bf16[4,2,16384]{2,1,0:T(2,128)(2,1)}), bf16[4,2,16384]{2,1,0:T(2,128)(2,1)S(1)}, u32[]{:S(2)}, u32[]{:S(2)}) async-start(bf16[4,2,16384]{2,1,0:T(2,128)(2,1)} %reshape.76), calls=%async_computation.1 | async-start | bytes 524288 | tf_op jit(solution)/shard_map/all_to_all | solution.py:132
  146.0 1.9 collective-permute-start.14
  149.8 8.7 %all-to-all-done.1 = bf16[4,2,16384]{2,1,0:T(2,128)(2,1)S(1)} async-done(((bf16[4,2,16384]{2,1,0:T(2,128)(2,1)}), bf16[4,2,16384]{2,1,0:T(2,128)(2,1)S(1)}, u32[]{:S(2)}, u32[]{:S(2)}) %all-to-all-start.1) | async-done | bytes 262176 | tf_op jit(solution)/shard_map/all_to_all | solution.py:132
  158.5 3.4 %all-to-all-start.5 = ((bf16[4,2,16384]{2,1,0:T(2,128)(2,1)}), bf16[4,2,16384]{2,1,0:T(2,128)(2,1)S(1)}, u32[]{:S(2)}, u32[]{:S(2)}) async-start(bf16[4,2,16384]{2,1,0:T(2,128)(2,1)} %reshape.72), calls=%async_computation.5 | async-start | bytes 524288 | tf_op jit(solution)/shard_map/all_to_all | solution.py:132
  162.9 0.9 reshape.74
  163.8 4.1 %all-to-all-done.5 = bf16[4,2,16384]{2,1,0:T(2,128)(2,1)S(1)} async-done(((bf16[4,2,16384]{2,1,0:T(2,128)(2,1)}), bf16[4,2,16384]{2,1,0:T(2,128)(2,1)S(1)}, u32[]{:S(2)}, u32[]{:S(2)}) %all-to-all-start.5) | async-done | bytes 262176 | tf_op jit(solution)/shard_map/all_to_all | solution.py:132
  167.9 3.4 %all-to-all-start.3 = ((bf16[4,2,16384]{2,1,0:T(2,128)(2,1)}), bf16[4,2,16384]{2,1,0:T(2,128)(2,1)S(1)}, u32[]{:S(2)}, u32[]{:S(2)}) async-start(bf16[4,2,16384]{2,1,0:T(2,128)(2,1)} %reshape.74), calls=%async_computation.3 | async-start | bytes 524288 | tf_op jit(solution)/shard_map/all_to_all | solution.py:132
  172.3 0.9 reshape.70
  173.1 4.1 %all-to-all-done.3 = bf16[4,2,16384]{2,1,0:T(2,128)(2,1)S(1)} async-done(((bf16[4,2,16384]{2,1,0:T(2,128)(2,1)}), bf16[4,2,16384]{2,1,0:T(2,128)(2,1)S(1)}, u32[]{:S(2)}, u32[]{:S(2)}) %all-to-all-start.3) | async-done | bytes 262176 | tf_op jit(solution)/shard_map/all_to_all | solution.py:132
  177.2 3.4 %all-to-all-start.7 = ((bf16[4,2,16384]{2,1,0:T(2,128)(2,1)}), bf16[4,2,16384]{2,1,0:T(2,128)(2,1)S(1)}, u32[]{:S(2)}, u32[]{:S(2)}) async-start(bf16[4,2,16384]{2,1,0:T(2,128)(2,1)} %reshape.70), calls=%async_computation.7 | async-start | bytes 524288 | tf_op jit(solution)/shard_map/all_to_all | solution.py:132
  181.7 5.0 %all-to-all-done.7 = bf16[4,2,16384]{2,1,0:T(2,128)(2,1)S(1)} async-done(((bf16[4,2,16384]{2,1,0:T(2,128)(2,1)}), bf16[4,2,16384]{2,1,0:T(2,128)(2,1)S(1)}, u32[]{:S(2)}, u32[]{:S(2)}) %all-to-all-start.7) | async-done | bytes 262176 | tf_op jit(solution)/shard_map/all_to_all | solution.py:132
  187.7 1.2 reshape.67
  (136 shorter events, 18.6 us)
Async XLA Ops:
  0.6 1.2 copy-start.22
  2.4 1.0 copy-start.12
  3.4 1.0 copy-start.13
  7.3 11.1 %all-to-all-start.2 = ((bf16[64,4,768]{2,0,1:T(8,128)(2,1)}), bf16[64,4,768]{2,0,1:T(8,128)(2,1)S(1)}, u32[]{:S(2)}, u32[]{:S(2)}) async-start(bf16[64,4,768]{2,0,1:T(8,128)(2,1)} %pad_maximum_fusion.2), calls=%async_computation.2 | async-start | bytes 786432 | tf_op jit(solution)/shard_map/all_to_all | solution.py:110
  18.3 25.2 %copy-start = (bf16[64,4,768]{2,0,1:T(8,128)(2,1)}, bf16[64,4,768]{2,0,1:T(8,128)(2,1)S(1)}, u32[]{:S(2)}) copy-start(bf16[64,4,768]{2,0,1:T(8,128)(2,1)S(1)} %all-to-all-done.2) | copy-start | bytes 1179652
  18.3 10.8 %all-to-all-start.4 = ((bf16[64,4,768]{2,0,1:T(8,128)(2,1)}), bf16[64,4,768]{2,0,1:T(8,128)(2,1)S(1)}, u32[]{:S(2)}, u32[]{:S(2)}) async-start(bf16[64,4,768]{2,0,1:T(8,128)(2,1)} %pad_maximum_fusion.3), calls=%async_computation.4 | async-start | bytes 786432 | tf_op jit(solution)/shard_map/all_to_all | solution.py:110
  29.2 21.5 %copy-start.1 = (bf16[64,4,768]{2,0,1:T(8,128)(2,1)}, bf16[64,4,768]{2,0,1:T(8,128)(2,1)S(1)}, u32[]{:S(2)}) copy-start(bf16[64,4,768]{2,0,1:T(8,128)(2,1)S(1)} %all-to-all-done.4) | copy-start | bytes 1179652
  29.2 10.8 %all-to-all-start = ((bf16[64,4,768]{2,0,1:T(8,128)(2,1)}), bf16[64,4,768]{2,0,1:T(8,128)(2,1)S(1)}, u32[]{:S(2)}, u32[]{:S(2)}) async-start(bf16[64,4,768]{2,0,1:T(8,128)(2,1)} %pad_maximum_fusion.1), calls=%async_computation | async-start | bytes 786432 | tf_op jit(solution)/shard_map/all_to_all | solution.py:110
  40.0 19.0 %copy-start.3 = (bf16[64,4,768]{2,0,1:T(8,128)(2,1)}, bf16[64,4,768]{2,0,1:T(8,128)(2,1)S(1)}, u32[]{:S(2)}) copy-start(bf16[64,4,768]{2,0,1:T(8,128)(2,1)S(1)} %all-to-all-done) | copy-start | bytes 1179652
  40.0 24.4 %all-to-all-start.6 = ((bf16[64,4,768]{2,0,1:T(8,128)(2,1)}), bf16[64,4,768]{2,0,1:T(8,128)(2,1)S(1)}, u32[]{:S(2)}, u32[]{:S(2)}) async-start(bf16[64,4,768]{2,0,1:T(8,128)(2,1)} %pad_maximum_fusion.4), calls=%async_computation.6 | async-start | bytes 786432 | tf_op jit(solution)/shard_map/all_to_all | solution.py:110
  43.5 18.2 %collective-permute-start.5 = (bf16[256,256]{1,0:T(8,128)(2,1)S(1)}, bf16[256,256]{1,0:T(8,128)(2,1)S(1)}, u32[]{:S(2)}, u32[]{:S(2)}) collective-permute-start(bf16[256,256]{1,0:T(8,128)(2,1)S(1)} %slice.143), channel_id=1, source_target_pairs={{0,8},{4,12},{8,16},{12,20},{16,24},{20,28},{24,32},{28,36},{32,40... | collective-permute-start | bytes 393224 | tf_op jit(solution)/shard_map/ppermute | solution.py:105
  47.2 50.4 %collective-permute-start.4 = (bf16[256,256]{1,0:T(8,128)(2,1)S(1)}, bf16[256,256]{1,0:T(8,128)(2,1)S(1)}, u32[]{:S(2)}, u32[]{:S(2)}) collective-permute-start(bf16[256,256]{1,0:T(8,128)(2,1)S(1)} %slice.143), channel_id=1, source_target_pairs={{0,4},{4,8},{8,12},{12,16},{16,20},{20,24},{24,28},{28,32},{32,36}... | collective-permute-start | bytes 393224 | tf_op jit(solution)/shard_map/ppermute | solution.py:105
  50.7 35.0 %collective-permute-start.9 = (bf16[256,256]{1,0:T(8,128)(2,1)S(1)}, bf16[256,256]{1,0:T(8,128)(2,1)S(1)}, u32[]{:S(2)}, u32[]{:S(2)}) collective-permute-start(bf16[256,256]{1,0:T(8,128)(2,1)S(1)} %slice.150), channel_id=1, source_target_pairs={{0,8},{4,12},{8,16},{12,20},{16,24},{20,28},{24,32},{28,36},{32,40... | collective-permute-start | bytes 393224 | tf_op jit(solution)/shard_map/ppermute | solution.py:105
  56.4 32.4 %collective-permute-start.8 = (bf16[256,256]{1,0:T(8,128)(2,1)S(1)}, bf16[256,256]{1,0:T(8,128)(2,1)S(1)}, u32[]{:S(2)}, u32[]{:S(2)}) collective-permute-start(bf16[256,256]{1,0:T(8,128)(2,1)S(1)} %slice.150), channel_id=1, source_target_pairs={{0,4},{4,8},{8,12},{12,16},{16,20},{20,24},{24,28},{28,32},{32,36}... | collective-permute-start | bytes 393224 | tf_op jit(solution)/shard_map/ppermute | solution.py:105
  59.0 5.4 %copy-start.27 = (s32[256]{0:T(256)S(1)}, s32[256]{0:T(256)}, u32[]{:S(2)}) copy-start(s32[256]{0:T(256)} %param.9) | copy-start | bytes 3076
  59.0 13.3 %collective-permute-start.1 = (bf16[256,256]{1,0:T(8,128)(2,1)S(1)}, bf16[256,256]{1,0:T(8,128)(2,1)S(1)}, u32[]{:S(2)}, u32[]{:S(2)}) collective-permute-start(bf16[256,256]{1,0:T(8,128)(2,1)S(1)} %slice.136), channel_id=1, source_target_pairs={{0,8},{4,12},{8,16},{12,20},{16,24},{20,28},{24,32},{28,36},{32,40... | collective-permute-start | bytes 393224 | tf_op jit(solution)/shard_map/ppermute | solution.py:105
  61.7 2.7 %copy-start.4 = (bf16[256,256]{1,0:T(8,128)(2,1)}, bf16[256,256]{1,0:T(8,128)(2,1)S(1)}, u32[]{:S(2)}) copy-start(bf16[256,256]{1,0:T(8,128)(2,1)S(1)} %collective-permute-done.5.k2_ref.v2_ref) | copy-start | bytes 393220
  61.8 16.2 %collective-permute-start = (bf16[256,256]{1,0:T(8,128)(2,1)S(1)}, bf16[256,256]{1,0:T(8,128)(2,1)S(1)}, u32[]{:S(2)}, u32[]{:S(2)}) collective-permute-start(bf16[256,256]{1,0:T(8,128)(2,1)S(1)} %slice.136), channel_id=1, source_target_pairs={{0,4},{4,8},{8,12},{12,16},{16,20},{20,24},{24,28},{28,32},{32,36}... | collective-permute-start | bytes 393224 | tf_op jit(solution)/shard_map/ppermute | solution.py:105
  64.4 20.2 %copy-start.2 = (bf16[64,4,768]{2,0,1:T(8,128)(2,1)}, bf16[64,4,768]{2,0,1:T(8,128)(2,1)S(1)}, u32[]{:S(2)}) copy-start(bf16[64,4,768]{2,0,1:T(8,128)(2,1)S(1)} %all-to-all-done.6) | copy-start | bytes 1179652
  72.4 8.3 %copy-start.10 = (bf16[256,256]{1,0:T(8,128)(2,1)}, bf16[256,256]{1,0:T(8,128)(2,1)S(1)}, u32[]{:S(2)}) copy-start(bf16[256,256]{1,0:T(8,128)(2,1)S(1)} %collective-permute-done.1.k2_ref.v2_ref) | copy-start | bytes 393220
  72.4 36.3 %collective-permute-start.13 = (bf16[256,256]{1,0:T(8,128)(2,1)S(1)}, bf16[256,256]{1,0:T(8,128)(2,1)S(1)}, u32[]{:S(2)}, u32[]{:S(2)}) collective-permute-start(bf16[256,256]{1,0:T(8,128)(2,1)S(1)} %slice.157), channel_id=1, source_target_pairs={{0,8},{4,12},{8,16},{12,20},{16,24},{20,28},{24,32},{28,36},{32,40... | collective-permute-start | bytes 393224 | tf_op jit(solution)/shard_map/ppermute | solution.py:105
  78.0 2.7 %copy-start.11 = (bf16[256,256]{1,0:T(8,128)(2,1)}, bf16[256,256]{1,0:T(8,128)(2,1)S(1)}, u32[]{:S(2)}) copy-start(bf16[256,256]{1,0:T(8,128)(2,1)S(1)} %collective-permute-done.k1_ref.v1_ref) | copy-start | bytes 393220
  78.0 39.7 %collective-permute-start.12 = (bf16[256,256]{1,0:T(8,128)(2,1)S(1)}, bf16[256,256]{1,0:T(8,128)(2,1)S(1)}, u32[]{:S(2)}, u32[]{:S(2)}) collective-permute-start(bf16[256,256]{1,0:T(8,128)(2,1)S(1)} %slice.157), channel_id=1, source_target_pairs={{0,4},{4,8},{8,12},{12,16},{16,20},{20,24},{24,28},{28,32},{32,36}... | collective-permute-start | bytes 393224 | tf_op jit(solution)/shard_map/ppermute | solution.py:105
  84.6 1.0 copy-start.19
  85.6 5.9 %copy-start.14 = (f32[256,256]{1,0:T(8,128)S(1)}, f32[256,256]{1,0:T(8,128)}, u32[]{:S(2)}) copy-start(f32[256,256]{1,0:T(8,128)} %get-tuple-element.19) | copy-start | bytes 786436
  85.7 5.9 %copy-start.8 = (bf16[256,256]{1,0:T(8,128)(2,1)}, bf16[256,256]{1,0:T(8,128)(2,1)S(1)}, u32[]{:S(2)}) copy-start(bf16[256,256]{1,0:T(8,128)(2,1)S(1)} %collective-permute-done.9.k2_ref.v2_ref) | copy-start | bytes 393220
  85.7 48.6 %collective-permute-start.3 = (bf16[2,256,128]{2,1,0:T(8,128)(2,1)S(1)}, bf16[2,256,128]{2,1,0:T(8,128)(2,1)S(1)}, u32[]{:S(2)}, u32[]{:S(2)}) collective-permute-start(bf16[2,256,128]{2,1,0:T(8,128)(2,1)S(1)} %convert_element_type.95), channel_id=1, source_target_pairs={{8,0},{12,4},{16,8},{20,12},{24,16},{28,20},{32,24},{36,28},{40,32... | collective-permute-start | bytes 393224 | tf_op jit(solution)/shard_map/ppermute | solution.py:105
  88.8 2.8 %copy-start.9 = (bf16[256,256]{1,0:T(8,128)(2,1)}, bf16[256,256]{1,0:T(8,128)(2,1)S(1)}, u32[]{:S(2)}) copy-start(bf16[256,256]{1,0:T(8,128)(2,1)S(1)} %collective-permute-done.8.k1_ref.v1_ref) | copy-start | bytes 393220
  88.8 48.7 %collective-permute-start.2 = (bf16[2,256,128]{2,1,0:T(8,128)(2,1)S(1)}, bf16[2,256,128]{2,1,0:T(8,128)(2,1)S(1)}, u32[]{:S(2)}, u32[]{:S(2)}) collective-permute-start(bf16[2,256,128]{2,1,0:T(8,128)(2,1)S(1)} %convert_element_type.93), channel_id=1, source_target_pairs={{4,0},{8,4},{12,8},{16,12},{20,16},{24,20},{28,24},{32,28},{36,32}... | collective-permute-start | bytes 393224 | tf_op jit(solution)/shard_map/ppermute | solution.py:105
  95.6 1.0 copy-start.20
  97.6 5.2 %copy-start.5 = (bf16[256,256]{1,0:T(8,128)(2,1)}, bf16[256,256]{1,0:T(8,128)(2,1)S(1)}, u32[]{:S(2)}) copy-start(bf16[256,256]{1,0:T(8,128)(2,1)S(1)} %collective-permute-done.4.k1_ref.v1_ref) | copy-start | bytes 393220
  97.6 48.4 %collective-permute-start.11 = (bf16[2,256,128]{2,1,0:T(8,128)(2,1)S(1)}, bf16[2,256,128]{2,1,0:T(8,128)(2,1)S(1)}, u32[]{:S(2)}, u32[]{:S(2)}) collective-permute-start(bf16[2,256,128]{2,1,0:T(8,128)(2,1)S(1)} %convert_element_type.109), channel_id=1, source_target_pairs={{8,0},{12,4},{16,8},{20,12},{24,16},{28,20},{32,24},{36,28},{40,32... | collective-permute-start | bytes 393224 | tf_op jit(solution)/shard_map/ppermute | solution.py:105
  106.7 1.0 copy-start.21
  108.7 19.7 %copy-start.6 = (bf16[256,256]{1,0:T(8,128)(2,1)}, bf16[256,256]{1,0:T(8,128)(2,1)S(1)}, u32[]{:S(2)}) copy-start(bf16[256,256]{1,0:T(8,128)(2,1)S(1)} %collective-permute-done.13.k2_ref.v2_ref) | copy-start | bytes 393220
  108.7 39.3 %collective-permute-start.10 = (bf16[2,256,128]{2,1,0:T(8,128)(2,1)S(1)}, bf16[2,256,128]{2,1,0:T(8,128)(2,1)S(1)}, u32[]{:S(2)}, u32[]{:S(2)}) collective-permute-start(bf16[2,256,128]{2,1,0:T(8,128)(2,1)S(1)} %convert_element_type.107), channel_id=1, source_target_pairs={{4,0},{8,4},{12,8},{16,12},{20,16},{24,20},{28,24},{32,28},{36,32}... | collective-permute-start | bytes 393224 | tf_op jit(solution)/shard_map/ppermute | solution.py:105
  117.7 10.7 %copy-start.7 = (bf16[256,256]{1,0:T(8,128)(2,1)}, bf16[256,256]{1,0:T(8,128)(2,1)S(1)}, u32[]{:S(2)}) copy-start(bf16[256,256]{1,0:T(8,128)(2,1)S(1)} %collective-permute-done.12.k1_ref.v1_ref) | copy-start | bytes 393220
  117.7 44.2 %collective-permute-start.7 = (bf16[2,256,128]{2,1,0:T(8,128)(2,1)S(1)}, bf16[2,256,128]{2,1,0:T(8,128)(2,1)S(1)}, u32[]{:S(2)}, u32[]{:S(2)}) collective-permute-start(bf16[2,256,128]{2,1,0:T(8,128)(2,1)S(1)} %convert_element_type.102), channel_id=1, source_target_pairs={{8,0},{12,4},{16,8},{20,12},{24,16},{28,20},{32,24},{36,28},{40,32... | collective-permute-start | bytes 393224 | tf_op jit(solution)/shard_map/ppermute | solution.py:105
  133.4 6.1 %copy-start.26 = (f32[2,256,128]{2,1,0:T(8,128)S(1)}, f32[2,256,128]{2,1,0:T(8,128)}, u32[]{:S(2)}) copy-start(f32[2,256,128]{2,1,0:T(8,128)} %get-tuple-element.20) | copy-start | bytes 786436
  134.3 27.6 %collective-permute-start.6 = (bf16[2,256,128]{2,1,0:T(8,128)(2,1)S(1)}, bf16[2,256,128]{2,1,0:T(8,128)(2,1)S(1)}, u32[]{:S(2)}, u32[]{:S(2)}) collective-permute-start(bf16[2,256,128]{2,1,0:T(8,128)(2,1)S(1)} %convert_element_type.100), channel_id=1, source_target_pairs={{4,0},{8,4},{12,8},{16,12},{20,16},{24,20},{28,24},{32,28},{36,32}... | collective-permute-start | bytes 393224 | tf_op jit(solution)/shard_map/ppermute | solution.py:105
  137.5 33.7 %collective-permute-start.15 = (bf16[2,256,128]{2,1,0:T(8,128)(2,1)S(1)}, bf16[2,256,128]{2,1,0:T(8,128)(2,1)S(1)}, u32[]{:S(2)}, u32[]{:S(2)}) collective-permute-start(bf16[2,256,128]{2,1,0:T(8,128)(2,1)S(1)} %convert_element_type.116), channel_id=1, source_target_pairs={{8,0},{12,4},{16,8},{20,12},{24,16},{28,20},{32,24},{36,28},{40,32... | collective-permute-start | bytes 393224 | tf_op jit(solution)/shard_map/ppermute | solution.py:105
  141.9 6.0 %copy-start.25 = (f32[2,256,128]{2,1,0:T(8,128)S(1)}, f32[2,256,128]{2,1,0:T(8,128)}, u32[]{:S(2)}) copy-start(f32[2,256,128]{2,1,0:T(8,128)} %get-tuple-element.28) | copy-start | bytes 786436
  141.9 16.5 %all-to-all-start.1 = ((bf16[4,2,16384]{2,1,0:T(2,128)(2,1)}), bf16[4,2,16384]{2,1,0:T(2,128)(2,1)S(1)}, u32[]{:S(2)}, u32[]{:S(2)}) async-start(bf16[4,2,16384]{2,1,0:T(2,128)(2,1)} %reshape.76), calls=%async_computation.1 | async-start | bytes 524288 | tf_op jit(solution)/shard_map/all_to_all | solution.py:132
  146.0 25.3 %collective-permute-start.14 = (bf16[2,256,128]{2,1,0:T(8,128)(2,1)S(1)}, bf16[2,256,128]{2,1,0:T(8,128)(2,1)S(1)}, u32[]{:S(2)}, u32[]{:S(2)}) collective-permute-start(bf16[2,256,128]{2,1,0:T(8,128)(2,1)S(1)} %convert_element_type.114), channel_id=1, source_target_pairs={{4,0},{8,4},{12,8},{16,12},{20,16},{24,20},{28,24},{32,28},{36,32}... | collective-permute-start | bytes 393224 | tf_op jit(solution)/shard_map/ppermute | solution.py:105
  149.8 12.1 %copy-start.24 = (f32[2,256,128]{2,1,0:T(8,128)S(1)}, f32[2,256,128]{2,1,0:T(8,128)}, u32[]{:S(2)}) copy-start(f32[2,256,128]{2,1,0:T(8,128)} %get-tuple-element.24) | copy-start | bytes 786436
  158.5 9.4 %all-to-all-start.5 = ((bf16[4,2,16384]{2,1,0:T(2,128)(2,1)}), bf16[4,2,16384]{2,1,0:T(2,128)(2,1)S(1)}, u32[]{:S(2)}, u32[]{:S(2)}) async-start(bf16[4,2,16384]{2,1,0:T(2,128)(2,1)} %reshape.72), calls=%async_computation.5 | async-start | bytes 524288 | tf_op jit(solution)/shard_map/all_to_all | solution.py:132
  163.7 7.5 %copy-start.23 = (f32[2,256,128]{2,1,0:T(8,128)S(1)}, f32[2,256,128]{2,1,0:T(8,128)}, u32[]{:S(2)}) copy-start(f32[2,256,128]{2,1,0:T(8,128)} %get-tuple-element.32) | copy-start | bytes 786436
  167.9 9.4 %all-to-all-start.3 = ((bf16[4,2,16384]{2,1,0:T(2,128)(2,1)}), bf16[4,2,16384]{2,1,0:T(2,128)(2,1)S(1)}, u32[]{:S(2)}, u32[]{:S(2)}) async-start(bf16[4,2,16384]{2,1,0:T(2,128)(2,1)} %reshape.74), calls=%async_computation.3 | async-start | bytes 524288 | tf_op jit(solution)/shard_map/all_to_all | solution.py:132
  177.2 9.4 %all-to-all-start.7 = ((bf16[4,2,16384]{2,1,0:T(2,128)(2,1)}), bf16[4,2,16384]{2,1,0:T(2,128)(2,1)S(1)}, u32[]{:S(2)}, u32[]{:S(2)}) async-start(bf16[4,2,16384]{2,1,0:T(2,128)(2,1)} %reshape.70), calls=%async_computation.7 | async-start | bytes 524288 | tf_op jit(solution)/shard_map/all_to_all | solution.py:132
  (4 other events, 3.9 us)

commit v9 on v6

--- a/solution.py
+++ b/solution.py
@@ -42,14 +42,15 @@
         m = jnp.max(scores[0], axis=1, keepdims=True)
         for d in range(1, 3):
             m = jnp.maximum(m, jnp.max(scores[d], axis=1, keepdims=True))
+        weights = [jnp.exp(scores[d] - m) for d in range(3)]
         tot = jnp.zeros_like(m)
         for d in range(3):
-            tot = tot + jnp.sum(jnp.exp(scores[d] - m), axis=1, keepdims=True)
-        lse = m + jnp.log(tot)
+            tot = tot + jnp.sum(weights[d], axis=1, keepdims=True)
+        inv_tot = 1.0 / tot
         probs, dprobs = [], []
         delta = jnp.zeros_like(m)
         for d in range(3):
-            p = jnp.exp(scores[d] - lse)
+            p = weights[d] * inv_tot
             dp = lax.dot_general(gj, vals[d], NT, preferred_element_type=jnp.float32)
             delta = delta + jnp.sum(p * dp, axis=1, keepdims=True)
             probs.append(p)
@@ -125,11 +126,10 @@
         kv_total = dkv0
         for distance, part in ((1, dkv1), (2, dkv2)):
             kv_total = kv_total + passed_along(part.astype(jnp.bfloat16), "ctx", -distance)
-    out_loc = jnp.concatenate(
+    return jnp.concatenate(
         [dq.astype(jnp.bfloat16), kv_total[0].astype(jnp.bfloat16), kv_total[1].astype(jnp.bfloat16)],
         axis=1,
-    )[:, None]
-    return lax.all_to_all(out_loc, "head", split_axis=0, concat_axis=1, tiled=True)
+    )
 
 
 def local(queries, normed_key_state, value_state_rows, output_gradient, doc_start):
@@ -150,7 +150,8 @@
     for chunk in range(CHUNKS):
         x_in = jnp.concatenate([p[:, :, chunk] for p in parts], axis=2)
         outs.append(chunk_pass(x_in, rel, kv_cols, q_cols))
-    out = jnp.stack(outs, axis=2)
+    out_loc = jnp.stack(outs, axis=1)[:, None]
+    out = lax.all_to_all(out_loc, "head", split_axis=0, concat_axis=1, tiled=True)
     grad_q = out[..., :q_cols].reshape(rows_in, heads_ax * CHUNKS * q_cols)
     grad_k = out[..., q_cols : q_cols + kv_cols].reshape(rows_in, heads_ax * CHUNKS * kv_cols)
     grad_v = out[..., q_cols + kv_cols :].reshape(rows_in, heads_ax * CHUNKS * kv_cols)

time: 153 us -> 156 us (1.020)
  blocking collectives: 0 us -> 23.7 us
  starting transfers between devices: 45.2 us -> 34.4 us
  waiting for transfers between devices: 68 us -> 62.7 us
  local copies, waits for them, and re-layouts: 17.6 us -> 14.8 us
    all_to_all x0 -> x1, blocking collectives: none -> 23.7 us  [local(): lax.all_to_all(out_loc, 'head', split_axis=0, concat_axis=1, tiled=True)]
    all_to_all x2 -> x0, waiting for transfers between devices: 13.3 us -> none  [chunk_pass(): lax.all_to_all(out_loc, 'head', split_axis=0, concat_axis=1, tiled=True)]
    all_to_all x2 -> x0, starting transfers between devices: 11 us -> none  [chunk_pass(): lax.all_to_all(out_loc, 'head', split_axis=0, concat_axis=1, tiled=True)]
    ppermute x8, waiting for transfers between devices: 43.4 us -> 50.6 us  [passed_along(): return lax.ppermute(block, axis, route)]
    unnamed x34 -> x26, local copies, waits for them, and re-layouts: 6.2 us -> 2.45 us
    broadcast_in_dim x4 -> x1, other arithmetic: 2.18 us -> 0.1 us  [local(): out_loc = jnp.stack(outs, axis=1)[:, None]]
  transfers between devices with their start and end apart: 12 -> 10, of which waited for: 8 -> 7; matrix products, arithmetic and copies ran while one was open for 8% -> 4% of each run, Pallas kernels for 8% -> 8%
where the time goes in v9:
time: 156 us
  waiting for transfers between devices  62.7 us (40%)
  starting transfers between devices  34.4 us (22%)
  blocking collectives  23.7 us (15%)
  local copies, waits for them, and re-layouts  14.8 us (9%)
  Pallas kernels  12.4 us (8%)
  other arithmetic  6.82 us (4%)
    ppermute x8, waiting for transfers between devices, passed_along(): return lax.ppermute(block, axis, route)  50.6 us
    ppermute x8, starting transfers between devices, passed_along(): return lax.ppermute(block, axis, route)  27.2 us
    all_to_all x1, blocking collectives, local(): lax.all_to_all(out_loc, 'head', split_axis=0, concat_axis=1, tiled=True)  23.7 us
    pallas_call x2, Pallas kernels, attend(): pl.pallas_call(attn_kernel, grid=(groups,), in_specs=[pl.BlockSpec((tok,...  12.4 us
    all_to_all x2, waiting for transfers between devices, chunk_pass(): lax.all_to_all(x_in, 'head', split_axis=1, concat_axis=0, tiled=True)  12.1 us
    all_to_all x2, starting transfers between devices, chunk_pass(): lax.all_to_all(x_in, 'head', split_axis=1, concat_axis=0, tiled=True)  7.13 us
    convert_element_type x4, other arithmetic, chunk_pass(): part.astype(jnp.bfloat16)  3.29 us
  transfers between devices with their start and end apart: 10, of which 7 were waited for; matrix products, arithmetic and copies ran while one was open for 4% of the time, Pallas kernels for 8%

profile of v9, /device:TPU:62, one launch (start us, length us, event | category | flops | bytes accessed | tf_op | source)
XLA Modules:
  0.0 155.7 jit_solution(15352612950417740148)
XLA Ops:
  0.6 1.1 reshape.43
  1.8 1.1 reshape.44
  2.9 0.4 fusion.4
  3.3 0.4 fusion.3
  3.7 0.3 copy-done.8
  4.0 0.4 reshape.45
  4.4 0.4 reshape.46
  4.8 0.7 fusion.2
  5.5 0.7 fusion.1
  6.3 0.3 copy_bitcast_fusion.2
  6.6 1.0 pad_maximum_fusion
  7.6 3.6 %all-to-all-start = ((bf16[64,4,1536]{2,0,1:T(8,128)(2,1)}), bf16[64,4,1536]{2,0,1:T(8,128)(2,1)S(1)}, u32[]{:S(2)}, u32[]{:S(2)}) async-start(bf16[64,4,1536]{2,0,1:T(8,128)(2,1)} %pad_maximum_fusion), calls=%async_computation | async-start | bytes 1572864 | tf_op jit(solution)/shard_map/all_to_all | solution.py:111
  11.3 0.3 copy_bitcast_fusion
  11.6 0.9 pad_maximum_fusion.1
  12.6 10.3 %all-to-all-done = bf16[64,4,1536]{2,0,1:T(8,128)(2,1)S(1)} async-done(((bf16[64,4,1536]{2,0,1:T(8,128)(2,1)}), bf16[64,4,1536]{2,0,1:T(8,128)(2,1)S(1)}, u32[]{:S(2)}, u32[]{:S(2)}) %all-to-all-start) | async-done | bytes 786464 | tf_op jit(solution)/shard_map/all_to_all | solution.py:111
  22.9 3.5 %all-to-all-start.1 = ((bf16[64,4,1536]{2,0,1:T(8,128)(2,1)}), bf16[64,4,1536]{2,0,1:T(8,128)(2,1)S(1)}, u32[]{:S(2)}, u32[]{:S(2)}) async-start(bf16[64,4,1536]{2,0,1:T(8,128)(2,1)} %pad_maximum_fusion.1), calls=%async_computation.1 | async-start | bytes 1572864 | tf_op jit(solution)/shard_map/all_to_all | solution.py:111
  26.4 6.2 %collective-permute-start.1 = (bf16[256,512]{1,0:T(8,128)(2,1)S(1)}, bf16[256,512]{1,0:T(8,128)(2,1)S(1)}, u32[]{:S(2)}, u32[]{:S(2)}) collective-permute-start(bf16[256,512]{1,0:T(8,128)(2,1)S(1)} %slice.76), channel_id=1, source_target_pairs={{0,8},{4,12},{8,16},{12,20},{16,24},{20,28},{24,32},{28,36},{32,40... | collective-permute-start | bytes 786440 | tf_op jit(solution)/shard_map/ppermute | solution.py:106
  32.6 3.5 %collective-permute-start = (bf16[256,512]{1,0:T(8,128)(2,1)S(1)}, bf16[256,512]{1,0:T(8,128)(2,1)S(1)}, u32[]{:S(2)}, u32[]{:S(2)}) collective-permute-start(bf16[256,512]{1,0:T(8,128)(2,1)S(1)} %slice.76), channel_id=1, source_target_pairs={{0,4},{4,8},{8,12},{12,16},{16,20},{20,24},{24,28},{28,32},{32,36}... | collective-permute-start | bytes 786440 | tf_op jit(solution)/shard_map/ppermute | solution.py:106
  36.2 1.8 %all-to-all-done.1 = bf16[64,4,1536]{2,0,1:T(8,128)(2,1)S(1)} async-done(((bf16[64,4,1536]{2,0,1:T(8,128)(2,1)}), bf16[64,4,1536]{2,0,1:T(8,128)(2,1)S(1)}, u32[]{:S(2)}, u32[]{:S(2)}) %all-to-all-start.1) | async-done | bytes 786464 | tf_op jit(solution)/shard_map/all_to_all | solution.py:111
  38.0 6.2 %collective-permute-start.5 = (bf16[256,512]{1,0:T(8,128)(2,1)S(1)}, bf16[256,512]{1,0:T(8,128)(2,1)S(1)}, u32[]{:S(2)}, u32[]{:S(2)}) collective-permute-start(bf16[256,512]{1,0:T(8,128)(2,1)S(1)} %slice.83), channel_id=1, source_target_pairs={{0,8},{4,12},{8,16},{12,20},{16,24},{20,28},{24,32},{28,36},{32,40... | collective-permute-start | bytes 786440 | tf_op jit(solution)/shard_map/ppermute | solution.py:106
  44.2 3.5 %collective-permute-start.4 = (bf16[256,512]{1,0:T(8,128)(2,1)S(1)}, bf16[256,512]{1,0:T(8,128)(2,1)S(1)}, u32[]{:S(2)}, u32[]{:S(2)}) collective-permute-start(bf16[256,512]{1,0:T(8,128)(2,1)S(1)} %slice.83), channel_id=1, source_target_pairs={{0,4},{4,8},{8,12},{12,16},{16,20},{20,24},{24,28},{28,32},{32,36}... | collective-permute-start | bytes 786440 | tf_op jit(solution)/shard_map/ppermute | solution.py:106
  47.7 0.8 copy.36.rel_ref
  48.5 15.0 %collective-permute-done.k1_ref.v1_ref = bf16[256,512]{1,0:T(8,128)(2,1)S(1)} collective-permute-done((bf16[256,512]{1,0:T(8,128)(2,1)S(1)}, bf16[256,512]{1,0:T(8,128)(2,1)S(1)}, u32[]{:S(2)}, u32[]{:S(2)}) %collective-permute-start) | collective-permute-done | bytes 262176 | tf_op jit(solution)/shard_map/ppermute | solution.py:106
  63.5 0.7 copy-done.5
  64.2 6.2 %shard_map.76 = (f32[256,512]{1,0:T(8,128)}, f32[2,256,256]{2,1,0:T(8,128)}, f32[2,256,256]{2,1,0:T(8,128)}, f32[2,256,256]{2,1,0:T(8,128)}) custom-call(s32[256,1]{1,0:T(8,128)} %copy.36.rel_ref, bf16[256,1536]{1,0:T(8,128)(2,1)} %bitcast.47, bf16[256,1536]{1,0:T(8,128)(2,1)} %bitcast.48, bf16[256,1536]{1,0:T(8,128)(2,1)} %bitcast.49, ...), custom_call_target="tpu_custom_call" | custom-call | tf_op jit(solution)/shard_map/pallas_call | solution.py:79
  70.4 1.1 convert_element_type.47
  71.5 1.1 convert_element_type.49
  72.6 1.9 %collective-permute-start.3 = (bf16[2,256,256]{2,1,0:T(8,128)(2,1)S(1)}, bf16[2,256,256]{2,1,0:T(8,128)(2,1)S(1)}, u32[]{:S(2)}, u32[]{:S(2)}) collective-permute-start(bf16[2,256,256]{2,1,0:T(8,128)(2,1)S(1)} %convert_element_type.49), channel_id=1, source_target_pairs={{8,0},{12,4},{16,8},{20,12},{24,16},{28,20},{32,24},{36,28},{40,32... | collective-permute-start | bytes 786440 | tf_op jit(solution)/shard_map/ppermute | solution.py:106
  74.5 1.9 %collective-permute-start.2 = (bf16[2,256,256]{2,1,0:T(8,128)(2,1)S(1)}, bf16[2,256,256]{2,1,0:T(8,128)(2,1)S(1)}, u32[]{:S(2)}, u32[]{:S(2)}) collective-permute-start(bf16[2,256,256]{2,1,0:T(8,128)(2,1)S(1)} %convert_element_type.47), channel_id=1, source_target_pairs={{4,0},{8,4},{12,8},{16,12},{20,16},{24,20},{28,24},{32,28},{36,32}... | collective-permute-start | bytes 786440 | tf_op jit(solution)/shard_map/ppermute | solution.py:106
  76.6 0.7 copy-done.2
  77.2 0.7 copy-done.4
  77.9 6.2 %shard_map.77 = (f32[256,512]{1,0:T(8,128)}, f32[2,256,256]{2,1,0:T(8,128)}, f32[2,256,256]{2,1,0:T(8,128)}, f32[2,256,256]{2,1,0:T(8,128)}) custom-call(s32[256,1]{1,0:T(8,128)} %copy.36.rel_ref, bf16[256,1536]{1,0:T(8,128)(2,1)} %bitcast.52, bf16[256,1536]{1,0:T(8,128)(2,1)} %bitcast.53, bf16[256,1536]{1,0:T(8,128)(2,1)} %bitcast.54, ...), custom_call_target="tpu_custom_call" | custom-call | tf_op jit(solution)/shard_map/pallas_call | solution.py:79
  84.1 1.2 convert_element_type.53
  85.3 1.1 convert_element_type.54
  86.4 2.1 %collective-permute-start.7 = (bf16[2,256,256]{2,1,0:T(8,128)(2,1)S(1)}, bf16[2,256,256]{2,1,0:T(8,128)(2,1)S(1)}, u32[]{:S(2)}, u32[]{:S(2)}) collective-permute-start(bf16[2,256,256]{2,1,0:T(8,128)(2,1)S(1)} %convert_element_type.56), channel_id=1, source_target_pairs={{8,0},{12,4},{16,8},{20,12},{24,16},{28,20},{32,24},{36,28},{40,32... | collective-permute-start | bytes 786440 | tf_op jit(solution)/shard_map/ppermute | solution.py:106
  88.5 1.9 %collective-permute-start.6 = (bf16[2,256,256]{2,1,0:T(8,128)(2,1)S(1)}, bf16[2,256,256]{2,1,0:T(8,128)(2,1)S(1)}, u32[]{:S(2)}, u32[]{:S(2)}) collective-permute-start(bf16[2,256,256]{2,1,0:T(8,128)(2,1)S(1)} %convert_element_type.54), channel_id=1, source_target_pairs={{4,0},{8,4},{12,8},{16,12},{20,16},{24,20},{28,24},{32,28},{36,32}... | collective-permute-start | bytes 786440 | tf_op jit(solution)/shard_map/ppermute | solution.py:106
  90.4 3.4 %collective-permute-done.3 = bf16[2,256,256]{2,1,0:T(8,128)(2,1)S(1)} collective-permute-done((bf16[2,256,256]{2,1,0:T(8,128)(2,1)S(1)}, bf16[2,256,256]{2,1,0:T(8,128)(2,1)S(1)}, u32[]{:S(2)}, u32[]{:S(2)}) %collective-permute-start.3) | collective-permute-done | bytes 262176 | tf_op jit(solution)/shard_map/ppermute | solution.py:106
  93.8 21.2 %collective-permute-done.2 = bf16[2,256,256]{2,1,0:T(8,128)(2,1)S(1)} collective-permute-done((bf16[2,256,256]{2,1,0:T(8,128)(2,1)S(1)}, bf16[2,256,256]{2,1,0:T(8,128)(2,1)S(1)}, u32[]{:S(2)}, u32[]{:S(2)}) %collective-permute-start.2) | collective-permute-done | bytes 262176 | tf_op jit(solution)/shard_map/ppermute | solution.py:106
  115.2 1.1 collective-permute-done.7
  116.3 9.8 %collective-permute-done.6 = bf16[2,256,256]{2,1,0:T(8,128)(2,1)S(1)} collective-permute-done((bf16[2,256,256]{2,1,0:T(8,128)(2,1)S(1)}, bf16[2,256,256]{2,1,0:T(8,128)(2,1)S(1)}, u32[]{:S(2)}, u32[]{:S(2)}) %collective-permute-start.6) | collective-permute-done | bytes 262176 | tf_op jit(solution)/shard_map/ppermute | solution.py:106
  126.5 1.1 copy.42
  127.6 23.7 %all_to_all.48 = bf16[256,1,2,1024]{3,2,1,0:T(2,128)(2,1)S(1)} all-to-all(bf16[256,1,2,1024]{3,2,1,0:T(2,128)(2,1)S(1)} %copy.42), channel_id=1, replica_groups=mesh['ctx'=128,'head'=4] {'head'}, dimensions={0} | all-to-all | bytes 2097152 | tf_op jit(solution)/shard_map/all_to_all | solution.py:154
  151.3 0.4 slice.86
  151.7 0.4 fusion
  152.2 0.9 reshape.51
  153.1 0.4 copy.43
  153.5 1.2 reshape.49
  154.8 0.9 reshape.50
  (41 shorter events, 1.2 us)
Async XLA Ops:
  2.9 1.0 copy-start.8
  3.3 1.1 copy-start.9
  7.6 15.3 %all-to-all-start = ((bf16[64,4,1536]{2,0,1:T(8,128)(2,1)}), bf16[64,4,1536]{2,0,1:T(8,128)(2,1)S(1)}, u32[]{:S(2)}, u32[]{:S(2)}) async-start(bf16[64,4,1536]{2,0,1:T(8,128)(2,1)} %pad_maximum_fusion), calls=%async_computation | async-start | bytes 1572864 | tf_op jit(solution)/shard_map/all_to_all | solution.py:111
  12.6 23.6 %copy-start.12 = (s32[256]{0:T(256)S(1)}, s32[256]{0:T(256)}, u32[]{:S(2)}) copy-start(s32[256]{0:T(256)} %param.9) | copy-start | bytes 3076
  22.9 3.5 %copy-start = (bf16[64,4,1536]{2,0,1:T(8,128)(2,1)}, bf16[64,4,1536]{2,0,1:T(8,128)(2,1)S(1)}, u32[]{:S(2)}) copy-start(bf16[64,4,1536]{2,0,1:T(8,128)(2,1)S(1)} %all-to-all-done) | copy-start | bytes 2359300
  22.9 15.1 %all-to-all-start.1 = ((bf16[64,4,1536]{2,0,1:T(8,128)(2,1)}), bf16[64,4,1536]{2,0,1:T(8,128)(2,1)S(1)}, u32[]{:S(2)}, u32[]{:S(2)}) async-start(bf16[64,4,1536]{2,0,1:T(8,128)(2,1)} %pad_maximum_fusion.1), calls=%async_computation.1 | async-start | bytes 1572864 | tf_op jit(solution)/shard_map/all_to_all | solution.py:111
  26.4 22.1 %collective-permute-start.1 = (bf16[256,512]{1,0:T(8,128)(2,1)S(1)}, bf16[256,512]{1,0:T(8,128)(2,1)S(1)}, u32[]{:S(2)}, u32[]{:S(2)}) collective-permute-start(bf16[256,512]{1,0:T(8,128)(2,1)S(1)} %slice.76), channel_id=1, source_target_pairs={{0,8},{4,12},{8,16},{12,20},{16,24},{20,28},{24,32},{28,36},{32,40... | collective-permute-start | bytes 786440 | tf_op jit(solution)/shard_map/ppermute | solution.py:106
  32.6 30.9 %collective-permute-start = (bf16[256,512]{1,0:T(8,128)(2,1)S(1)}, bf16[256,512]{1,0:T(8,128)(2,1)S(1)}, u32[]{:S(2)}, u32[]{:S(2)}) collective-permute-start(bf16[256,512]{1,0:T(8,128)(2,1)S(1)} %slice.76), channel_id=1, source_target_pairs={{0,4},{4,8},{8,12},{12,16},{16,20},{20,24},{24,28},{28,32},{32,36}... | collective-permute-start | bytes 786440 | tf_op jit(solution)/shard_map/ppermute | solution.py:106
  38.0 32.4 %copy-start.1 = (bf16[64,4,1536]{2,0,1:T(8,128)(2,1)}, bf16[64,4,1536]{2,0,1:T(8,128)(2,1)S(1)}, u32[]{:S(2)}) copy-start(bf16[64,4,1536]{2,0,1:T(8,128)(2,1)S(1)} %all-to-all-done.1) | copy-start | bytes 2359300
  38.0 38.5 %collective-permute-start.5 = (bf16[256,512]{1,0:T(8,128)(2,1)S(1)}, bf16[256,512]{1,0:T(8,128)(2,1)S(1)}, u32[]{:S(2)}, u32[]{:S(2)}) collective-permute-start(bf16[256,512]{1,0:T(8,128)(2,1)S(1)} %slice.83), channel_id=1, source_target_pairs={{0,8},{4,12},{8,16},{12,20},{16,24},{20,28},{24,32},{28,36},{32,40... | collective-permute-start | bytes 786440 | tf_op jit(solution)/shard_map/ppermute | solution.py:106
  44.2 32.3 %collective-permute-start.4 = (bf16[256,512]{1,0:T(8,128)(2,1)S(1)}, bf16[256,512]{1,0:T(8,128)(2,1)S(1)}, u32[]{:S(2)}, u32[]{:S(2)}) collective-permute-start(bf16[256,512]{1,0:T(8,128)(2,1)S(1)} %slice.83), channel_id=1, source_target_pairs={{0,4},{4,8},{8,12},{12,16},{16,20},{20,24},{24,28},{28,32},{32,36}... | collective-permute-start | bytes 786440 | tf_op jit(solution)/shard_map/ppermute | solution.py:106
  48.5 15.0 %copy-start.3 = (bf16[256,512]{1,0:T(8,128)(2,1)}, bf16[256,512]{1,0:T(8,128)(2,1)S(1)}, u32[]{:S(2)}) copy-start(bf16[256,512]{1,0:T(8,128)(2,1)S(1)} %collective-permute-done.1.k2_ref.v2_ref) | copy-start | bytes 786436
  63.5 0.7 copy-start.5
  70.4 6.1 %copy-start.6 = (f32[256,512]{1,0:T(8,128)S(1)}, f32[256,512]{1,0:T(8,128)}, u32[]{:S(2)}) copy-start(f32[256,512]{1,0:T(8,128)} %get-tuple-element.11) | copy-start | bytes 1572868
  72.6 21.2 %collective-permute-start.3 = (bf16[2,256,256]{2,1,0:T(8,128)(2,1)S(1)}, bf16[2,256,256]{2,1,0:T(8,128)(2,1)S(1)}, u32[]{:S(2)}, u32[]{:S(2)}) collective-permute-start(bf16[2,256,256]{2,1,0:T(8,128)(2,1)S(1)} %convert_element_type.49), channel_id=1, source_target_pairs={{8,0},{12,4},{16,8},{20,12},{24,16},{28,20},{32,24},{36,28},{40,32... | collective-permute-start | bytes 786440 | tf_op jit(solution)/shard_map/ppermute | solution.py:106
  74.5 40.5 %collective-permute-start.2 = (bf16[2,256,256]{2,1,0:T(8,128)(2,1)S(1)}, bf16[2,256,256]{2,1,0:T(8,128)(2,1)S(1)}, u32[]{:S(2)}, u32[]{:S(2)}) collective-permute-start(bf16[2,256,256]{2,1,0:T(8,128)(2,1)S(1)} %convert_element_type.47), channel_id=1, source_target_pairs={{4,0},{8,4},{12,8},{16,12},{20,16},{24,20},{28,24},{32,28},{36,32}... | collective-permute-start | bytes 786440 | tf_op jit(solution)/shard_map/ppermute | solution.py:106
  76.5 0.7 copy-start.2
  77.2 0.7 copy-start.4
  84.1 2.3 %copy-start.7 = (f32[2,256,256]{2,1,0:T(8,128)S(1)}, f32[2,256,256]{2,1,0:T(8,128)}, u32[]{:S(2)}) copy-start(f32[2,256,256]{2,1,0:T(8,128)} %get-tuple-element.18) | copy-start | bytes 1572868
  84.1 30.9 %copy-start.10 = (f32[2,256,256]{2,1,0:T(8,128)S(1)}, f32[2,256,256]{2,1,0:T(8,128)}, u32[]{:S(2)}) copy-start(f32[2,256,256]{2,1,0:T(8,128)} %get-tuple-element.12) | copy-start | bytes 1572868
  86.4 39.7 %copy-start.11 = (f32[2,256,256]{2,1,0:T(8,128)S(1)}, f32[2,256,256]{2,1,0:T(8,128)}, u32[]{:S(2)}) copy-start(f32[2,256,256]{2,1,0:T(8,128)} %get-tuple-element.16) | copy-start | bytes 1572868
  86.4 29.8 %collective-permute-start.7 = (bf16[2,256,256]{2,1,0:T(8,128)(2,1)S(1)}, bf16[2,256,256]{2,1,0:T(8,128)(2,1)S(1)}, u32[]{:S(2)}, u32[]{:S(2)}) collective-permute-start(bf16[2,256,256]{2,1,0:T(8,128)(2,1)S(1)} %convert_element_type.56), channel_id=1, source_target_pairs={{8,0},{12,4},{16,8},{20,12},{24,16},{28,20},{32,24},{36,28},{40,32... | collective-permute-start | bytes 786440 | tf_op jit(solution)/shard_map/ppermute | solution.py:106
  88.5 37.6 %collective-permute-start.6 = (bf16[2,256,256]{2,1,0:T(8,128)(2,1)S(1)}, bf16[2,256,256]{2,1,0:T(8,128)(2,1)S(1)}, u32[]{:S(2)}, u32[]{:S(2)}) collective-permute-start(bf16[2,256,256]{2,1,0:T(8,128)(2,1)S(1)} %convert_element_type.54), channel_id=1, source_target_pairs={{4,0},{8,4},{12,8},{16,12},{20,16},{24,20},{28,24},{32,28},{36,32}... | collective-permute-start | bytes 786440 | tf_op jit(solution)/shard_map/ppermute | solution.py:106

commit v10 on v6

--- a/solution.py
+++ b/solution.py
@@ -42,14 +42,15 @@
         m = jnp.max(scores[0], axis=1, keepdims=True)
         for d in range(1, 3):
             m = jnp.maximum(m, jnp.max(scores[d], axis=1, keepdims=True))
+        weights = [jnp.exp(scores[d] - m) for d in range(3)]
         tot = jnp.zeros_like(m)
         for d in range(3):
-            tot = tot + jnp.sum(jnp.exp(scores[d] - m), axis=1, keepdims=True)
-        lse = m + jnp.log(tot)
+            tot = tot + jnp.sum(weights[d], axis=1, keepdims=True)
+        inv_tot = 1.0 / tot
         probs, dprobs = [], []
         delta = jnp.zeros_like(m)
         for d in range(3):
-            p = jnp.exp(scores[d] - lse)
+            p = weights[d] * inv_tot
             dp = lax.dot_general(gj, vals[d], NT, preferred_element_type=jnp.float32)
             delta = delta + jnp.sum(p * dp, axis=1, keepdims=True)
             probs.append(p)

time: 153 us -> 153 us (level)
  no operation moved by 1% of the time
where the time goes in v10:
time: 153 us; the launch traced here: 152 us
  waiting for transfers between devices  68.1 us (45%)
  starting transfers between devices  45.5 us (30%)
  local copies, waits for them, and re-layouts  17.6 us (12%)
  Pallas kernels  12.4 us (8%)
  other arithmetic  7.82 us (5%)
    ppermute x8, waiting for transfers between devices, passed_along(): return lax.ppermute(block, axis, route)  43.3 us
    ppermute x8, starting transfers between devices, passed_along(): return lax.ppermute(block, axis, route)  27.1 us
    all_to_all x2, waiting for transfers between devices, chunk_pass(): lax.all_to_all(out_loc, 'head', split_axis=0, concat_axis=1, tiled=True)  13.5 us
    pallas_call x2, Pallas kernels, attend(): pl.pallas_call(attn_kernel, grid=(groups,), in_specs=[pl.BlockSpec((tok,...  12.4 us
    all_to_all x2, waiting for transfers between devices, chunk_pass(): lax.all_to_all(x_in, 'head', split_axis=1, concat_axis=0, tiled=True)  11.3 us
    all_to_all x2, starting transfers between devices, chunk_pass(): lax.all_to_all(out_loc, 'head', split_axis=0, concat_axis=1, tiled=True)  11.3 us
    all_to_all x2, starting transfers between devices, chunk_pass(): lax.all_to_all(x_in, 'head', split_axis=1, concat_axis=0, tiled=True)  7.13 us
    unnamed x34, local copies, waits for them, and re-layouts  6.2 us
  transfers between devices with their start and end apart: 12, of which 8 were waited for; matrix products, arithmetic and copies ran while one was open for 8% of the time, Pallas kernels for 8%

profile of v10, /device:TPU:62, one launch (start us, length us, event | category | flops | bytes accessed | tf_op | source)
XLA Modules:
  0.0 152.4 jit_solution(18343596293713750394)
XLA Ops:
  0.6 1.1 reshape.45
  1.8 1.1 reshape.46
  4.0 0.4 reshape.47
  4.4 0.4 reshape.48
  4.8 0.7 fusion.3
  5.5 0.7 fusion.2
  6.6 1.0 pad_maximum_fusion.1
  7.6 3.6 %all-to-all-start.2 = ((bf16[64,4,1536]{2,0,1:T(8,128)(2,1)}), bf16[64,4,1536]{2,0,1:T(8,128)(2,1)S(1)}, u32[]{:S(2)}, u32[]{:S(2)}) async-start(bf16[64,4,1536]{2,0,1:T(8,128)(2,1)} %pad_maximum_fusion.1), calls=%async_computation.2 | async-start | bytes 1572864 | tf_op jit(solution)/shard_map/all_to_all | solution.py:111
  11.6 0.9 pad_maximum_fusion
  12.6 10.3 %all-to-all-done.2 = bf16[64,4,1536]{2,0,1:T(8,128)(2,1)S(1)} async-done(((bf16[64,4,1536]{2,0,1:T(8,128)(2,1)}), bf16[64,4,1536]{2,0,1:T(8,128)(2,1)S(1)}, u32[]{:S(2)}, u32[]{:S(2)}) %all-to-all-start.2) | async-done | bytes 786464 | tf_op jit(solution)/shard_map/all_to_all | solution.py:111
  22.9 3.5 %all-to-all-start = ((bf16[64,4,1536]{2,0,1:T(8,128)(2,1)}), bf16[64,4,1536]{2,0,1:T(8,128)(2,1)S(1)}, u32[]{:S(2)}, u32[]{:S(2)}) async-start(bf16[64,4,1536]{2,0,1:T(8,128)(2,1)} %pad_maximum_fusion), calls=%async_computation | async-start | bytes 1572864 | tf_op jit(solution)/shard_map/all_to_all | solution.py:111
  26.4 6.2 %collective-permute-start.5 = (bf16[256,512]{1,0:T(8,128)(2,1)S(1)}, bf16[256,512]{1,0:T(8,128)(2,1)S(1)}, u32[]{:S(2)}, u32[]{:S(2)}) collective-permute-start(bf16[256,512]{1,0:T(8,128)(2,1)S(1)} %slice.83), channel_id=1, source_target_pairs={{0,8},{4,12},{8,16},{12,20},{16,24},{20,28},{24,32},{28,36},{32,40... | collective-permute-start | bytes 786440 | tf_op jit(solution)/shard_map/ppermute | solution.py:106
  32.6 3.5 %collective-permute-start.4 = (bf16[256,512]{1,0:T(8,128)(2,1)S(1)}, bf16[256,512]{1,0:T(8,128)(2,1)S(1)}, u32[]{:S(2)}, u32[]{:S(2)}) collective-permute-start(bf16[256,512]{1,0:T(8,128)(2,1)S(1)} %slice.83), channel_id=1, source_target_pairs={{0,4},{4,8},{8,12},{12,16},{16,20},{20,24},{24,28},{28,32},{32,36}... | collective-permute-start | bytes 786440 | tf_op jit(solution)/shard_map/ppermute | solution.py:106
  36.2 0.8 copy.63.rel_ref
  37.0 1.0 all-to-all-done
  38.0 6.2 %collective-permute-start.1 = (bf16[256,512]{1,0:T(8,128)(2,1)S(1)}, bf16[256,512]{1,0:T(8,128)(2,1)S(1)}, u32[]{:S(2)}, u32[]{:S(2)}) collective-permute-start(bf16[256,512]{1,0:T(8,128)(2,1)S(1)} %slice.76), channel_id=1, source_target_pairs={{0,8},{4,12},{8,16},{12,20},{16,24},{20,28},{24,32},{28,36},{32,40... | collective-permute-start | bytes 786440 | tf_op jit(solution)/shard_map/ppermute | solution.py:106
  44.2 3.5 %collective-permute-start = (bf16[256,512]{1,0:T(8,128)(2,1)S(1)}, bf16[256,512]{1,0:T(8,128)(2,1)S(1)}, u32[]{:S(2)}, u32[]{:S(2)}) collective-permute-start(bf16[256,512]{1,0:T(8,128)(2,1)S(1)} %slice.76), channel_id=1, source_target_pairs={{0,4},{4,8},{8,12},{12,16},{16,20},{20,24},{24,28},{28,32},{32,36}... | collective-permute-start | bytes 786440 | tf_op jit(solution)/shard_map/ppermute | solution.py:106
  47.7 15.8 %collective-permute-done.4.k1_ref.v1_ref = bf16[256,512]{1,0:T(8,128)(2,1)S(1)} collective-permute-done((bf16[256,512]{1,0:T(8,128)(2,1)S(1)}, bf16[256,512]{1,0:T(8,128)(2,1)S(1)}, u32[]{:S(2)}, u32[]{:S(2)}) %collective-permute-start.4) | collective-permute-done | bytes 262176 | tf_op jit(solution)/shard_map/ppermute | solution.py:106
  63.5 0.7 copy-done.4
  64.2 6.2 %shard_map.77 = (f32[256,512]{1,0:T(8,128)}, f32[2,256,256]{2,1,0:T(8,128)}, f32[2,256,256]{2,1,0:T(8,128)}, f32[2,256,256]{2,1,0:T(8,128)}) custom-call(s32[256,1]{1,0:T(8,128)} %copy.63.rel_ref, bf16[256,1536]{1,0:T(8,128)(2,1)} %bitcast.46, bf16[256,1536]{1,0:T(8,128)(2,1)} %bitcast.47, bf16[256,1536]{1,0:T(8,128)(2,1)} %bitcast.48, ...), custom_call_target="tpu_custom_call" | custom-call | tf_op jit(solution)/shard_map/pallas_call | solution.py:79
  70.4 1.1 convert_element_type.54
  71.5 1.1 convert_element_type.56
  72.6 1.9 %collective-permute-start.7 = (bf16[2,256,256]{2,1,0:T(8,128)(2,1)S(1)}, bf16[2,256,256]{2,1,0:T(8,128)(2,1)S(1)}, u32[]{:S(2)}, u32[]{:S(2)}) collective-permute-start(bf16[2,256,256]{2,1,0:T(8,128)(2,1)S(1)} %convert_element_type.56), channel_id=1, source_target_pairs={{8,0},{12,4},{16,8},{20,12},{24,16},{28,20},{32,24},{36,28},{40,32... | collective-permute-start | bytes 786440 | tf_op jit(solution)/shard_map/ppermute | solution.py:106
  74.5 1.9 %collective-permute-start.6 = (bf16[2,256,256]{2,1,0:T(8,128)(2,1)S(1)}, bf16[2,256,256]{2,1,0:T(8,128)(2,1)S(1)}, u32[]{:S(2)}, u32[]{:S(2)}) collective-permute-start(bf16[2,256,256]{2,1,0:T(8,128)(2,1)S(1)} %convert_element_type.54), channel_id=1, source_target_pairs={{4,0},{8,4},{12,8},{16,12},{20,16},{24,20},{28,24},{32,28},{36,32}... | collective-permute-start | bytes 786440 | tf_op jit(solution)/shard_map/ppermute | solution.py:106
  76.6 0.7 copy-done.3
  77.2 0.7 copy-done.5
  77.9 6.2 %shard_map.76 = (f32[256,512]{1,0:T(8,128)}, f32[2,256,256]{2,1,0:T(8,128)}, f32[2,256,256]{2,1,0:T(8,128)}, f32[2,256,256]{2,1,0:T(8,128)}) custom-call(s32[256,1]{1,0:T(8,128)} %copy.63.rel_ref, bf16[256,1536]{1,0:T(8,128)(2,1)} %bitcast.51, bf16[256,1536]{1,0:T(8,128)(2,1)} %bitcast.52, bf16[256,1536]{1,0:T(8,128)(2,1)} %bitcast.53, ...), custom_call_target="tpu_custom_call" | custom-call | tf_op jit(solution)/shard_map/pallas_call | solution.py:79
  84.1 1.2 convert_element_type.47
  85.3 1.9 %collective-permute-start.3 = (bf16[2,256,256]{2,1,0:T(8,128)(2,1)S(1)}, bf16[2,256,256]{2,1,0:T(8,128)(2,1)S(1)}, u32[]{:S(2)}, u32[]{:S(2)}) collective-permute-start(bf16[2,256,256]{2,1,0:T(8,128)(2,1)S(1)} %convert_element_type.49), channel_id=1, source_target_pairs={{8,0},{12,4},{16,8},{20,12},{24,16},{28,20},{32,24},{36,28},{40,32... | collective-permute-start | bytes 786440 | tf_op jit(solution)/shard_map/ppermute | solution.py:106
  87.3 1.9 %collective-permute-start.2 = (bf16[2,256,256]{2,1,0:T(8,128)(2,1)S(1)}, bf16[2,256,256]{2,1,0:T(8,128)(2,1)S(1)}, u32[]{:S(2)}, u32[]{:S(2)}) collective-permute-start(bf16[2,256,256]{2,1,0:T(8,128)(2,1)S(1)} %convert_element_type.47), channel_id=1, source_target_pairs={{4,0},{8,4},{12,8},{16,12},{20,16},{24,20},{28,24},{32,28},{36,32}... | collective-permute-start | bytes 786440 | tf_op jit(solution)/shard_map/ppermute | solution.py:106
  89.2 4.6 %collective-permute-done.7 = bf16[2,256,256]{2,1,0:T(8,128)(2,1)S(1)} collective-permute-done((bf16[2,256,256]{2,1,0:T(8,128)(2,1)S(1)}, bf16[2,256,256]{2,1,0:T(8,128)(2,1)S(1)}, u32[]{:S(2)}, u32[]{:S(2)}) %collective-permute-start.7) | collective-permute-done | bytes 262176 | tf_op jit(solution)/shard_map/ppermute | solution.py:106
  93.8 22.0 %collective-permute-done.6 = bf16[2,256,256]{2,1,0:T(8,128)(2,1)S(1)} collective-permute-done((bf16[2,256,256]{2,1,0:T(8,128)(2,1)S(1)}, bf16[2,256,256]{2,1,0:T(8,128)(2,1)S(1)}, u32[]{:S(2)}, u32[]{:S(2)}) %collective-permute-start.6) | collective-permute-done | bytes 262176 | tf_op jit(solution)/shard_map/ppermute | solution.py:106
  115.9 0.5 broadcast
  116.4 1.0 reduce.1
  117.5 1.2 reshape.56
  118.7 6.4 %all-to-all-start.3 = ((bf16[4,2,32768]{2,1,0:T(2,128)(2,1)}), bf16[4,2,32768]{2,1,0:T(2,128)(2,1)S(1)}, u32[]{:S(2)}, u32[]{:S(2)}) async-start(bf16[4,2,32768]{2,1,0:T(2,128)(2,1)} %reshape.56), calls=%async_computation.3 | async-start | bytes 1048576 | tf_op jit(solution)/shard_map/all_to_all | solution.py:133
  125.1 1.0 collective-permute-done.2
  126.3 1.0 reduce
  127.3 1.2 reshape.54
  128.5 5.4 %all-to-all-done.3 = bf16[4,2,32768]{2,1,0:T(2,128)(2,1)S(1)} async-done(((bf16[4,2,32768]{2,1,0:T(2,128)(2,1)}), bf16[4,2,32768]{2,1,0:T(2,128)(2,1)S(1)}, u32[]{:S(2)}, u32[]{:S(2)}) %all-to-all-start.3) | async-done | bytes 524320 | tf_op jit(solution)/shard_map/all_to_all | solution.py:133
  133.9 4.9 %all-to-all-start.1 = ((bf16[4,2,32768]{2,1,0:T(2,128)(2,1)}), bf16[4,2,32768]{2,1,0:T(2,128)(2,1)S(1)}, u32[]{:S(2)}, u32[]{:S(2)}) async-start(bf16[4,2,32768]{2,1,0:T(2,128)(2,1)} %reshape.54), calls=%async_computation.1 | async-start | bytes 1048576 | tf_op jit(solution)/shard_map/all_to_all | solution.py:133
  138.7 0.5 reshape.57
  139.4 8.1 %all-to-all-done.1 = bf16[4,2,32768]{2,1,0:T(2,128)(2,1)S(1)} async-done(((bf16[4,2,32768]{2,1,0:T(2,128)(2,1)}), bf16[4,2,32768]{2,1,0:T(2,128)(2,1)S(1)}, u32[]{:S(2)}, u32[]{:S(2)}) %all-to-all-start.1) | async-done | bytes 524320 | tf_op jit(solution)/shard_map/all_to_all | solution.py:133
  147.5 0.5 reshape.55
  148.6 0.9 reshape.53
  149.5 0.5 copy.71
  150.1 1.2 reshape.51
  151.5 0.9 reshape.52
  (53 shorter events, 3.3 us)
Async XLA Ops:
  2.9 1.0 copy-start.9
  3.3 1.1 copy-start.10
  7.6 15.3 %all-to-all-start.2 = ((bf16[64,4,1536]{2,0,1:T(8,128)(2,1)}), bf16[64,4,1536]{2,0,1:T(8,128)(2,1)S(1)}, u32[]{:S(2)}, u32[]{:S(2)}) async-start(bf16[64,4,1536]{2,0,1:T(8,128)(2,1)} %pad_maximum_fusion.1), calls=%async_computation.2 | async-start | bytes 1572864 | tf_op jit(solution)/shard_map/all_to_all | solution.py:111
  12.6 23.6 %copy-start.13 = (s32[256]{0:T(256)S(1)}, s32[256]{0:T(256)}, u32[]{:S(2)}) copy-start(s32[256]{0:T(256)} %param.9) | copy-start | bytes 3076
  22.9 3.5 %copy-start = (bf16[64,4,1536]{2,0,1:T(8,128)(2,1)}, bf16[64,4,1536]{2,0,1:T(8,128)(2,1)S(1)}, u32[]{:S(2)}) copy-start(bf16[64,4,1536]{2,0,1:T(8,128)(2,1)S(1)} %all-to-all-done.2) | copy-start | bytes 2359300
  22.9 15.1 %all-to-all-start = ((bf16[64,4,1536]{2,0,1:T(8,128)(2,1)}), bf16[64,4,1536]{2,0,1:T(8,128)(2,1)S(1)}, u32[]{:S(2)}, u32[]{:S(2)}) async-start(bf16[64,4,1536]{2,0,1:T(8,128)(2,1)} %pad_maximum_fusion), calls=%async_computation | async-start | bytes 1572864 | tf_op jit(solution)/shard_map/all_to_all | solution.py:111
  26.4 21.3 %collective-permute-start.5 = (bf16[256,512]{1,0:T(8,128)(2,1)S(1)}, bf16[256,512]{1,0:T(8,128)(2,1)S(1)}, u32[]{:S(2)}, u32[]{:S(2)}) collective-permute-start(bf16[256,512]{1,0:T(8,128)(2,1)S(1)} %slice.83), channel_id=1, source_target_pairs={{0,8},{4,12},{8,16},{12,20},{16,24},{20,28},{24,32},{28,36},{32,40... | collective-permute-start | bytes 786440 | tf_op jit(solution)/shard_map/ppermute | solution.py:106
  32.6 30.9 %collective-permute-start.4 = (bf16[256,512]{1,0:T(8,128)(2,1)S(1)}, bf16[256,512]{1,0:T(8,128)(2,1)S(1)}, u32[]{:S(2)}, u32[]{:S(2)}) collective-permute-start(bf16[256,512]{1,0:T(8,128)(2,1)S(1)} %slice.83), channel_id=1, source_target_pairs={{0,4},{4,8},{8,12},{12,16},{16,20},{20,24},{24,28},{28,32},{32,36}... | collective-permute-start | bytes 786440 | tf_op jit(solution)/shard_map/ppermute | solution.py:106
  38.0 32.4 %copy-start.1 = (bf16[64,4,1536]{2,0,1:T(8,128)(2,1)}, bf16[64,4,1536]{2,0,1:T(8,128)(2,1)S(1)}, u32[]{:S(2)}) copy-start(bf16[64,4,1536]{2,0,1:T(8,128)(2,1)S(1)} %all-to-all-done) | copy-start | bytes 2359300
  38.0 38.5 %collective-permute-start.1 = (bf16[256,512]{1,0:T(8,128)(2,1)S(1)}, bf16[256,512]{1,0:T(8,128)(2,1)S(1)}, u32[]{:S(2)}, u32[]{:S(2)}) collective-permute-start(bf16[256,512]{1,0:T(8,128)(2,1)S(1)} %slice.76), channel_id=1, source_target_pairs={{0,8},{4,12},{8,16},{12,20},{16,24},{20,28},{24,32},{28,36},{32,40... | collective-permute-start | bytes 786440 | tf_op jit(solution)/shard_map/ppermute | solution.py:106
  44.2 32.3 %collective-permute-start = (bf16[256,512]{1,0:T(8,128)(2,1)S(1)}, bf16[256,512]{1,0:T(8,128)(2,1)S(1)}, u32[]{:S(2)}, u32[]{:S(2)}) collective-permute-start(bf16[256,512]{1,0:T(8,128)(2,1)S(1)} %slice.76), channel_id=1, source_target_pairs={{0,4},{4,8},{8,12},{12,16},{16,20},{20,24},{24,28},{28,32},{32,36}... | collective-permute-start | bytes 786440 | tf_op jit(solution)/shard_map/ppermute | solution.py:106
  47.7 15.8 %copy-start.2 = (bf16[256,512]{1,0:T(8,128)(2,1)}, bf16[256,512]{1,0:T(8,128)(2,1)S(1)}, u32[]{:S(2)}) copy-start(bf16[256,512]{1,0:T(8,128)(2,1)S(1)} %collective-permute-done.5.k2_ref.v2_ref) | copy-start | bytes 786436
  63.5 0.7 copy-start.4
  70.4 6.1 %copy-start.7 = (f32[256,512]{1,0:T(8,128)S(1)}, f32[256,512]{1,0:T(8,128)}, u32[]{:S(2)}) copy-start(f32[256,512]{1,0:T(8,128)} %get-tuple-element.15) | copy-start | bytes 1572868
  72.6 21.2 %collective-permute-start.7 = (bf16[2,256,256]{2,1,0:T(8,128)(2,1)S(1)}, bf16[2,256,256]{2,1,0:T(8,128)(2,1)S(1)}, u32[]{:S(2)}, u32[]{:S(2)}) collective-permute-start(bf16[2,256,256]{2,1,0:T(8,128)(2,1)S(1)} %convert_element_type.56), channel_id=1, source_target_pairs={{8,0},{12,4},{16,8},{20,12},{24,16},{28,20},{32,24},{36,28},{40,32... | collective-permute-start | bytes 786440 | tf_op jit(solution)/shard_map/ppermute | solution.py:106
  74.5 41.2 %collective-permute-start.6 = (bf16[2,256,256]{2,1,0:T(8,128)(2,1)S(1)}, bf16[2,256,256]{2,1,0:T(8,128)(2,1)S(1)}, u32[]{:S(2)}, u32[]{:S(2)}) collective-permute-start(bf16[2,256,256]{2,1,0:T(8,128)(2,1)S(1)} %convert_element_type.54), channel_id=1, source_target_pairs={{4,0},{8,4},{12,8},{16,12},{20,16},{24,20},{28,24},{32,28},{36,32}... | collective-permute-start | bytes 786440 | tf_op jit(solution)/shard_map/ppermute | solution.py:106
  76.5 0.7 copy-start.3
  77.2 0.7 copy-start.5
  84.1 1.2 copy-start.8
  84.1 31.6 %copy-start.12 = (f32[2,256,256]{2,1,0:T(8,128)S(1)}, f32[2,256,256]{2,1,0:T(8,128)}, u32[]{:S(2)}) copy-start(f32[2,256,256]{2,1,0:T(8,128)} %get-tuple-element.16) | copy-start | bytes 1572868
  85.3 39.8 %collective-permute-start.3 = (bf16[2,256,256]{2,1,0:T(8,128)(2,1)S(1)}, bf16[2,256,256]{2,1,0:T(8,128)(2,1)S(1)}, u32[]{:S(2)}, u32[]{:S(2)}) collective-permute-start(bf16[2,256,256]{2,1,0:T(8,128)(2,1)S(1)} %convert_element_type.49), channel_id=1, source_target_pairs={{8,0},{12,4},{16,8},{20,12},{24,16},{28,20},{32,24},{36,28},{40,32... | collective-permute-start | bytes 786440 | tf_op jit(solution)/shard_map/ppermute | solution.py:106
  87.3 38.8 %collective-permute-start.2 = (bf16[2,256,256]{2,1,0:T(8,128)(2,1)S(1)}, bf16[2,256,256]{2,1,0:T(8,128)(2,1)S(1)}, u32[]{:S(2)}, u32[]{:S(2)}) collective-permute-start(bf16[2,256,256]{2,1,0:T(8,128)(2,1)S(1)} %convert_element_type.47), channel_id=1, source_target_pairs={{4,0},{8,4},{12,8},{16,12},{20,16},{24,20},{28,24},{32,28},{36,32}... | collective-permute-start | bytes 786440 | tf_op jit(solution)/shard_map/ppermute | solution.py:106
  117.5 7.6 %copy-start.6 = (f32[256,512]{1,0:T(8,128)S(1)}, f32[256,512]{1,0:T(8,128)}, u32[]{:S(2)}) copy-start(f32[256,512]{1,0:T(8,128)} %get-tuple-element.11) | copy-start | bytes 1572868
  118.7 7.4 %copy-start.11 = (f32[2,256,256]{2,1,0:T(8,128)S(1)}, f32[2,256,256]{2,1,0:T(8,128)}, u32[]{:S(2)}) copy-start(f32[2,256,256]{2,1,0:T(8,128)} %get-tuple-element.12) | copy-start | bytes 1572868
  118.7 15.2 %all-to-all-start.3 = ((bf16[4,2,32768]{2,1,0:T(2,128)(2,1)}), bf16[4,2,32768]{2,1,0:T(2,128)(2,1)S(1)}, u32[]{:S(2)}, u32[]{:S(2)}) async-start(bf16[4,2,32768]{2,1,0:T(2,128)(2,1)} %reshape.56), calls=%async_computation.3 | async-start | bytes 1048576 | tf_op jit(solution)/shard_map/all_to_all | solution.py:133
  133.9 13.7 %all-to-all-start.1 = ((bf16[4,2,32768]{2,1,0:T(2,128)(2,1)}), bf16[4,2,32768]{2,1,0:T(2,128)(2,1)S(1)}, u32[]{:S(2)}, u32[]{:S(2)}) async-start(bf16[4,2,32768]{2,1,0:T(2,128)(2,1)} %reshape.54), calls=%async_computation.1 | async-start | bytes 1048576 | tf_op jit(solution)/shard_map/all_to_all | solution.py:133

commit v11 on v5

--- a/solution.py
+++ b/solution.py
@@ -10,6 +10,7 @@
 WINDOW = 512
 SPAN = 2
 CHAIN = False
+CHUNKS = 2
 
 score_scale = 168.0 ** (-0.5)
 NT = (((1,), (1,)), ((), ()))
@@ -41,14 +42,15 @@
         m = jnp.max(scores[0], axis=1, keepdims=True)
         for d in range(1, 3):
             m = jnp.maximum(m, jnp.max(scores[d], axis=1, keepdims=True))
+        weights = [jnp.exp(scores[d] - m) for d in range(3)]
         tot = jnp.zeros_like(m)
         for d in range(3):
-            tot = tot + jnp.sum(jnp.exp(scores[d] - m), axis=1, keepdims=True)
-        lse = m + jnp.log(tot)
+            tot = tot + jnp.sum(weights[d], axis=1, keepdims=True)
+        inv_tot = 1.0 / tot
         probs, dprobs = [], []
         delta = jnp.zeros_like(m)
         for d in range(3):
-            p = jnp.exp(scores[d] - lse)
+            p = weights[d] * inv_tot
             dp = lax.dot_general(gj, vals[d], NT, preferred_element_type=jnp.float32)
             delta = delta + jnp.sum(p * dp, axis=1, keepdims=True)
             probs.append(p)
@@ -66,17 +68,18 @@
         dkv_refs[d][1] = dv[d]
 
 
-def attend(rel, x_all, kv_blocks):
+def attend(rel, x_all, kv_blocks, g0, ng):
     tok = x_all.shape[0]
     kvcols = kv_blocks[0].shape[1] // 2
     groups = kvcols // HEAD_SIZE
     qblk = 2 * kvcols // groups
-    col = lambda off: pl.BlockSpec((tok, HEAD_SIZE), lambda g: (0, off + g))
-    qcol = lambda off: pl.BlockSpec((tok, qblk), lambda g: (0, off + g))
+    col = lambda off: pl.BlockSpec((tok, HEAD_SIZE), lambda g: (0, off + g0 + g))
+    qcol = lambda off: pl.BlockSpec((tok, qblk), lambda g: (0, off + g0 + g))
     kv_spec = pl.BlockSpec((2, tok, HEAD_SIZE), lambda g: (0, 0, g))
+    out_cols = ng * HEAD_SIZE
     return pl.pallas_call(
         attn_kernel,
-        grid=(groups,),
+        grid=(ng,),
         in_specs=[
             pl.BlockSpec((tok, 1), lambda g: (0, 0)),
             qcol(2 * kvcols // qblk),
@@ -90,10 +93,10 @@
         ],
         out_specs=[pl.BlockSpec((tok, qblk), lambda g: (0, g)), kv_spec, kv_spec, kv_spec],
         out_shape=[
-            jax.ShapeDtypeStruct((tok, 2 * kvcols), jnp.float32),
-            jax.ShapeDtypeStruct((2, tok, kvcols), jnp.float32),
-            jax.ShapeDtypeStruct((2, tok, kvcols), jnp.float32),
-            jax.ShapeDtypeStruct((2, tok, kvcols), jnp.float32),
+            jax.ShapeDtypeStruct((tok, 2 * out_cols), jnp.float32),
+            jax.ShapeDtypeStruct((2, tok, out_cols), jnp.float32),
+            jax.ShapeDtypeStruct((2, tok, out_cols), jnp.float32),
+            jax.ShapeDtypeStruct((2, tok, out_cols), jnp.float32),
         ],
     )(rel, x_all, x_all, x_all, x_all, kv_blocks[0], kv_blocks[0], kv_blocks[1], kv_blocks[1])
 
@@ -110,6 +113,9 @@
     tok_rows = doc_start.shape[0]
     kv_cols = normed_key_state.shape[1] // heads_ax
     q_cols = queries.shape[1] // heads_ax
+    groups = kv_cols // HEAD_SIZE
+    shard_index = lax.axis_index("ctx")
+    rel = (doc_start - shard_index * tok_rows).reshape(tok_rows, 1)
     x_in = jnp.concatenate(
         [
             normed_key_state.reshape(rows_in, heads_ax, kv_cols),
@@ -122,31 +128,25 @@
     x_all = lax.all_to_all(x_in, "head", split_axis=1, concat_axis=0, tiled=True)
     x_all = x_all.reshape(tok_rows, 2 * kv_cols + 2 * q_cols)
     kv_local = x_all[:, : 2 * kv_cols]
-    if CHAIN:
-        kv1 = passed_along(kv_local, "ctx", 1)
-        kv2 = passed_along(kv1, "ctx", 1)
-    else:
-        kv1 = passed_along(kv_local, "ctx", 1)
-        kv2 = passed_along(kv_local, "ctx", 2)
-    shard_index = lax.axis_index("ctx")
-    rel = (doc_start - shard_index * tok_rows).reshape(tok_rows, 1)
-    dq, dkv0, dkv1, dkv2 = attend(rel, x_all, (kv1, kv2))
-    if CHAIN:
-        carried = passed_along(dkv2.astype(jnp.bfloat16), "ctx", -1)
-        carried = passed_along((dkv1 + carried).astype(jnp.bfloat16), "ctx", -1)
-        kv_total = dkv0 + carried
-    else:
+    kv1 = passed_along(kv_local, "ctx", 1)
+    kv2 = passed_along(kv_local, "ctx", 2)
+    step = groups // CHUNKS
+    outs = []
+    for chunk in range(CHUNKS):
+        dq, dkv0, dkv1, dkv2 = attend(rel, x_all, (kv1, kv2), chunk * step, step)
         kv_total = dkv0
         for distance, part in ((1, dkv1), (2, dkv2)):
             kv_total = kv_total + passed_along(part.astype(jnp.bfloat16), "ctx", -distance)
-    out_loc = jnp.concatenate(
-        [dq.astype(jnp.bfloat16), kv_total[0].astype(jnp.bfloat16), kv_total[1].astype(jnp.bfloat16)],
-        axis=1,
-    )[:, None]
-    out = lax.all_to_all(out_loc, "head", split_axis=0, concat_axis=1, tiled=True)
-    grad_q = out[:, :, :q_cols].reshape(rows_in, heads_ax * q_cols)
-    grad_k = out[:, :, q_cols : q_cols + kv_cols].reshape(rows_in, heads_ax * kv_cols)
-    grad_v = out[:, :, q_cols + kv_cols :].reshape(rows_in, heads_ax * kv_cols)
+        out_loc = jnp.concatenate(
+            [dq.astype(jnp.bfloat16), kv_total[0].astype(jnp.bfloat16), kv_total[1].astype(jnp.bfloat16)],
+            axis=1,
+        )[:, None]
+        outs.append(lax.all_to_all(out_loc, "head", split_axis=0, concat_axis=1, tiled=True))
+    out = jnp.stack(outs, axis=2)
+    qc, kc = q_cols // CHUNKS, kv_cols // CHUNKS
+    grad_q = out[..., :qc].reshape(rows_in, heads_ax * q_cols)
+    grad_k = out[..., qc : qc + kc].reshape(rows_in, heads_ax * kv_cols)
+    grad_v = out[..., qc + kc :].reshape(rows_in, heads_ax * kv_cols)
     return grad_q, grad_k, grad_v
 
 

time: 188 us -> 174 us (0.926)
  blocking collectives: 40.3 us -> 23.5 us
  waiting for transfers between devices: 110 us -> 93.9 us
  starting transfers between devices: 13 us -> 24 us
  local copies, waits for them, and re-layouts: 8.34 us -> 11.4 us
  other arithmetic: 4.68 us -> 7.13 us
  Pallas kernels: 10.5 us -> 12.5 us
    ppermute x4 -> x6, waiting for transfers between devices: 110 us -> 85.8 us  [passed_along(): return lax.ppermute(block, axis, route)]
    all_to_all x1 -> x0, blocking collectives: 16.9 us -> none  [local(): lax.all_to_all(out_loc, 'head', split_axis=0, concat_axis=1, tiled=True)]
    all_to_all x0 -> x2, waiting for transfers between devices: none -> 8.11 us  [local(): lax.all_to_all(out_loc, 'head', split_axis=0, concat_axis=1, tiled=True)]
    all_to_all x0 -> x2, starting transfers between devices: none -> 7.22 us  [local(): lax.all_to_all(out_loc, 'head', split_axis=0, concat_axis=1, tiled=True)]
    ppermute x4 -> x6, starting transfers between devices: 13 us -> 16.8 us  [passed_along(): return lax.ppermute(block, axis, route)]
    pallas_call x1 -> x2, Pallas kernels: 10.5 us -> 12.5 us  [attend(): pl.pallas_call(attn_kernel, grid=(ng,), in_specs=[pl.BlockSpec((tok, 1),...]
    convert_element_type x2 -> x4, other arithmetic: 2.73 us -> 4.39 us  [local(): part.astype(jnp.bfloat16)]
    unnamed x21 -> x26, local copies, waits for them, and re-layouts: 3.28 us -> 4.59 us
  transfers between devices with their start and end apart: 4 -> 8, of which waited for: 4 -> 6; matrix products, arithmetic and copies ran while one was open for 1% -> 6% of each run, Pallas kernels for 0% -> 4%
where the time goes in v11:
time: 174 us; the launch traced here: 173 us
  waiting for transfers between devices  93.9 us (54%)
  starting transfers between devices  24 us (14%)
  blocking collectives  23.5 us (14%)
  Pallas kernels  12.5 us (7%)
  local copies, waits for them, and re-layouts  11.4 us (7%)
  other arithmetic  7.13 us (4%)
    ppermute x6, waiting for transfers between devices, passed_along(): return lax.ppermute(block, axis, route)  85.8 us
    all_to_all x1, blocking collectives, local(): lax.all_to_all(x_in, 'head', split_axis=1, concat_axis=0, tiled=True)  23.5 us
    ppermute x6, starting transfers between devices, passed_along(): return lax.ppermute(block, axis, route)  16.8 us
    pallas_call x2, Pallas kernels, attend(): pl.pallas_call(attn_kernel, grid=(ng,), in_specs=[pl.BlockSpec((tok, 1),...  12.5 us
    all_to_all x2, waiting for transfers between devices, local(): lax.all_to_all(out_loc, 'head', split_axis=0, concat_axis=1, tiled=True)  8.11 us
    all_to_all x2, starting transfers between devices, local(): lax.all_to_all(out_loc, 'head', split_axis=0, concat_axis=1, tiled=True)  7.22 us
    unnamed x26, local copies, waits for them, and re-layouts  4.59 us
    convert_element_type x4, other arithmetic, local(): part.astype(jnp.bfloat16)  4.39 us
  transfers between devices with their start and end apart: 8, of which 6 were waited for; matrix products, arithmetic and copies ran while one was open for 6% of the time, Pallas kernels for 4%

profile of v11, /device:TPU:182, one launch (start us, length us, event | category | flops | bytes accessed | tf_op | source)
XLA Modules:
  0.0 173.4 jit_solution(10554753055176262065)
XLA Ops:
  0.7 1.3 copy_bitcast_fusion
  2.1 0.2 pad_maximum_fusion
  2.2 0.0 copy-start.9
  2.2 23.5 %all_to_all.45 = bf16[64,4,3072]{2,0,1:T(8,128)(2,1)S(1)} all-to-all(bf16[64,4,3072]{2,0,1:T(8,128)(2,1)S(1)} %pad_maximum_fusion), channel_id=1, replica_groups=mesh['ctx'=128,'head'=4] {'head'}, dimensions={1} | all-to-all | bytes 3145728 | tf_op jit(solution)/shard_map/all_to_all | solution.py:128
  25.8 2.6 %collective-permute-start = (bf16[256,1024]{1,0:T(8,128)(2,1)S(1)}, bf16[256,1024]{1,0:T(8,128)(2,1)S(1)}, u32[]{:S(2)}, u32[]{:S(2)}) collective-permute-start(bf16[256,1024]{1,0:T(8,128)(2,1)S(1)} %slice.36), channel_id=1, source_target_pairs={{0,4},{4,8},{8,12},{12,16},{16,20},{20,24},{24,28},{28,32},{32,36}... | collective-permute-start | bytes 1572872 | tf_op jit(solution)/shard_map/ppermute | solution.py:107
  28.4 6.5 %collective-permute-start.1 = (bf16[256,1024]{1,0:T(8,128)(2,1)S(1)}, bf16[256,1024]{1,0:T(8,128)(2,1)S(1)}, u32[]{:S(2)}, u32[]{:S(2)}) collective-permute-start(bf16[256,1024]{1,0:T(8,128)(2,1)S(1)} %slice.36), channel_id=1, source_target_pairs={{0,8},{4,12},{8,16},{12,20},{16,24},{20,28},{24,32},{28,36},{32,40... | collective-permute-start | bytes 1572872 | tf_op jit(solution)/shard_map/ppermute | solution.py:107
  34.9 0.8 copy.47.rel_ref
  35.7 18.0 %collective-permute-done.k1_ref.v1_ref = bf16[256,1024]{1,0:T(8,128)(2,1)S(1)} collective-permute-done((bf16[256,1024]{1,0:T(8,128)(2,1)S(1)}, bf16[256,1024]{1,0:T(8,128)(2,1)S(1)}, u32[]{:S(2)}, u32[]{:S(2)}) %collective-permute-start) | collective-permute-done | bytes 524320 | tf_op jit(solution)/shard_map/ppermute | solution.py:107
  53.7 15.7 %collective-permute-done.1.k2_ref.v2_ref = bf16[256,1024]{1,0:T(8,128)(2,1)S(1)} collective-permute-done((bf16[256,1024]{1,0:T(8,128)(2,1)S(1)}, bf16[256,1024]{1,0:T(8,128)(2,1)S(1)}, u32[]{:S(2)}, u32[]{:S(2)}) %collective-permute-start.1) | collective-permute-done | bytes 524320 | tf_op jit(solution)/shard_map/ppermute | solution.py:107
  69.4 0.8 copy-done.2
  70.2 6.2 %shard_map.77 = (f32[256,512]{1,0:T(8,128)}, f32[2,256,256]{2,1,0:T(8,128)}, f32[2,256,256]{2,1,0:T(8,128)}, f32[2,256,256]{2,1,0:T(8,128)}) custom-call(s32[256,1]{1,0:T(8,128)} %copy.47.rel_ref, bf16[256,3072]{1,0:T(8,128)(2,1)} %bitcast.37, bf16[256,3072]{1,0:T(8,128)(2,1)} %bitcast.38, bf16[256,3072]{1,0:T(8,128)(2,1)} %bitcast.39, ...), custom_call_target="tpu_custom_call" | custom-call | tf_op jit(solution)/shard_map/pallas_call | solution.py:80
  76.5 1.1 convert_element_type.54
  77.6 1.9 %collective-permute-start.4 = (bf16[2,256,256]{2,1,0:T(8,128)(2,1)S(1)}, bf16[2,256,256]{2,1,0:T(8,128)(2,1)S(1)}, u32[]{:S(2)}, u32[]{:S(2)}) collective-permute-start(bf16[2,256,256]{2,1,0:T(8,128)(2,1)S(1)} %convert_element_type.54), channel_id=1, source_target_pairs={{4,0},{8,4},{12,8},{16,12},{20,16},{24,20},{28,24},{32,28},{36,32}... | collective-permute-start | bytes 786440 | tf_op jit(solution)/shard_map/ppermute | solution.py:107
  79.5 1.1 convert_element_type.56
  80.6 1.9 %collective-permute-start.5 = (bf16[2,256,256]{2,1,0:T(8,128)(2,1)S(1)}, bf16[2,256,256]{2,1,0:T(8,128)(2,1)S(1)}, u32[]{:S(2)}, u32[]{:S(2)}) collective-permute-start(bf16[2,256,256]{2,1,0:T(8,128)(2,1)S(1)} %convert_element_type.56), channel_id=1, source_target_pairs={{8,0},{12,4},{16,8},{20,12},{24,16},{28,20},{32,24},{36,28},{40,32... | collective-permute-start | bytes 786440 | tf_op jit(solution)/shard_map/ppermute | solution.py:107
  82.6 6.2 %shard_map.76 = (f32[256,512]{1,0:T(8,128)}, f32[2,256,256]{2,1,0:T(8,128)}, f32[2,256,256]{2,1,0:T(8,128)}, f32[2,256,256]{2,1,0:T(8,128)}) custom-call(s32[256,1]{1,0:T(8,128)} %copy.47.rel_ref, bf16[256,3072]{1,0:T(8,128)(2,1)} %bitcast.41, bf16[256,3072]{1,0:T(8,128)(2,1)} %bitcast.42, bf16[256,3072]{1,0:T(8,128)(2,1)} %bitcast.43, ...), custom_call_target="tpu_custom_call" | custom-call | tf_op jit(solution)/shard_map/pallas_call | solution.py:80
  88.8 1.1 convert_element_type.47
  89.9 1.9 %collective-permute-start.2 = (bf16[2,256,256]{2,1,0:T(8,128)(2,1)S(1)}, bf16[2,256,256]{2,1,0:T(8,128)(2,1)S(1)}, u32[]{:S(2)}, u32[]{:S(2)}) collective-permute-start(bf16[2,256,256]{2,1,0:T(8,128)(2,1)S(1)} %convert_element_type.47), channel_id=1, source_target_pairs={{4,0},{8,4},{12,8},{16,12},{20,16},{24,20},{28,24},{32,28},{36,32}... | collective-permute-start | bytes 786440 | tf_op jit(solution)/shard_map/ppermute | solution.py:107
  91.9 1.1 convert_element_type.49
  92.9 1.9 %collective-permute-start.3 = (bf16[2,256,256]{2,1,0:T(8,128)(2,1)S(1)}, bf16[2,256,256]{2,1,0:T(8,128)(2,1)S(1)}, u32[]{:S(2)}, u32[]{:S(2)}) collective-permute-start(bf16[2,256,256]{2,1,0:T(8,128)(2,1)S(1)} %convert_element_type.49), channel_id=1, source_target_pairs={{8,0},{12,4},{16,8},{20,12},{24,16},{28,20},{32,24},{36,28},{40,32... | collective-permute-start | bytes 786440 | tf_op jit(solution)/shard_map/ppermute | solution.py:107
  94.9 17.5 %collective-permute-done.4 = bf16[2,256,256]{2,1,0:T(8,128)(2,1)S(1)} collective-permute-done((bf16[2,256,256]{2,1,0:T(8,128)(2,1)S(1)}, bf16[2,256,256]{2,1,0:T(8,128)(2,1)S(1)}, u32[]{:S(2)}, u32[]{:S(2)}) %collective-permute-start.4) | collective-permute-done | bytes 262176 | tf_op jit(solution)/shard_map/ppermute | solution.py:107
  112.3 19.2 %collective-permute-done.5 = bf16[2,256,256]{2,1,0:T(8,128)(2,1)S(1)} collective-permute-done((bf16[2,256,256]{2,1,0:T(8,128)(2,1)S(1)}, bf16[2,256,256]{2,1,0:T(8,128)(2,1)S(1)}, u32[]{:S(2)}, u32[]{:S(2)}) %collective-permute-start.5) | collective-permute-done | bytes 262176 | tf_op jit(solution)/shard_map/ppermute | solution.py:107
  131.5 0.1 add_convert_fusion
  131.6 0.1 maximum_bitcast_fusion.1
  131.7 0.5 broadcast
  132.2 1.1 reduce.1
  133.3 1.2 reshape.51
  134.5 3.5 %all-to-all-start.2 = ((bf16[4,2,32768]{2,1,0:T(2,128)(2,1)}), bf16[4,2,32768]{2,1,0:T(2,128)(2,1)S(1)}, u32[]{:S(2)}, u32[]{:S(2)}) async-start(bf16[4,2,32768]{2,1,0:T(2,128)(2,1)} %reshape.51), calls=%async_computation.2 | async-start | bytes 1048576 | tf_op jit(solution)/shard_map/all_to_all | solution.py:144
  138.0 0.0 collective-permute-done.2
  138.1 15.5 %collective-permute-done.3 = bf16[2,256,256]{2,1,0:T(8,128)(2,1)S(1)} collective-permute-done((bf16[2,256,256]{2,1,0:T(8,128)(2,1)S(1)}, bf16[2,256,256]{2,1,0:T(8,128)(2,1)S(1)}, u32[]{:S(2)}, u32[]{:S(2)}) %collective-permute-start.3) | collective-permute-done | bytes 262176 | tf_op jit(solution)/shard_map/ppermute | solution.py:107
  153.5 0.1 add_convert_fusion.1
  153.7 0.1 maximum_bitcast_fusion
  153.7 1.0 reduce
  154.8 1.2 reshape.49
  155.9 0.0 all-to-all-done.2
  155.9 3.7 %all-to-all-start.1 = ((bf16[4,2,32768]{2,1,0:T(2,128)(2,1)}), bf16[4,2,32768]{2,1,0:T(2,128)(2,1)S(1)}, u32[]{:S(2)}, u32[]{:S(2)}) async-start(bf16[4,2,32768]{2,1,0:T(2,128)(2,1)} %reshape.49), calls=%async_computation.1 | async-start | bytes 1048576 | tf_op jit(solution)/shard_map/all_to_all | solution.py:144
  159.7 0.5 reshape.52
  160.2 0.2 copy.55
  160.4 8.1 %all-to-all-done.1 = bf16[4,2,32768]{2,1,0:T(2,128)(2,1)S(1)} async-done(((bf16[4,2,32768]{2,1,0:T(2,128)(2,1)}), bf16[4,2,32768]{2,1,0:T(2,128)(2,1)S(1)}, u32[]{:S(2)}, u32[]{:S(2)}) %all-to-all-start.1) | async-done | bytes 524320 | tf_op jit(solution)/shard_map/all_to_all | solution.py:144
  168.5 0.5 reshape.50
  169.0 0.2 copy.54
  169.2 0.1 fusion
  169.3 0.3 copy.52
  169.6 0.9 reshape.47
  170.5 0.3 copy.53
  170.8 0.9 reshape.48
  171.6 0.5 copy.51
  172.2 1.2 reshape.46
  (26 shorter events, 0.3 us)
Async XLA Ops:
  0.6 1.4 copy-start.8
  0.6 1.4 copy-start.7
  2.2 32.7 %copy-start.9 = (s32[256]{0:T(256)S(1)}, s32[256]{0:T(256)}, u32[]{:S(2)}) copy-start(s32[256]{0:T(256)} %param.9) | copy-start | bytes 3076
  25.7 43.7 %copy-start = (bf16[64,4,3072]{2,0,1:T(8,128)(2,1)}, bf16[64,4,3072]{2,0,1:T(8,128)(2,1)S(1)}, u32[]{:S(2)}) copy-start(bf16[64,4,3072]{2,0,1:T(8,128)(2,1)S(1)} %all_to_all.45) | copy-start | bytes 4718596
  25.8 27.9 %collective-permute-start = (bf16[256,1024]{1,0:T(8,128)(2,1)S(1)}, bf16[256,1024]{1,0:T(8,128)(2,1)S(1)}, u32[]{:S(2)}, u32[]{:S(2)}) collective-permute-start(bf16[256,1024]{1,0:T(8,128)(2,1)S(1)} %slice.36), channel_id=1, source_target_pairs={{0,4},{4,8},{8,12},{12,16},{16,20},{20,24},{24,28},{28,32},{32,36}... | collective-permute-start | bytes 1572872 | tf_op jit(solution)/shard_map/ppermute | solution.py:107
  28.4 41.0 %collective-permute-start.1 = (bf16[256,1024]{1,0:T(8,128)(2,1)S(1)}, bf16[256,1024]{1,0:T(8,128)(2,1)S(1)}, u32[]{:S(2)}, u32[]{:S(2)}) collective-permute-start(bf16[256,1024]{1,0:T(8,128)(2,1)S(1)} %slice.36), channel_id=1, source_target_pairs={{0,8},{4,12},{8,16},{12,20},{16,24},{20,28},{24,32},{28,36},{32,40... | collective-permute-start | bytes 1572872 | tf_op jit(solution)/shard_map/ppermute | solution.py:107
  53.7 15.7 %copy-start.1 = (bf16[256,1024]{1,0:T(8,128)(2,1)}, bf16[256,1024]{1,0:T(8,128)(2,1)S(1)}, u32[]{:S(2)}) copy-start(bf16[256,1024]{1,0:T(8,128)(2,1)S(1)} %collective-permute-done.k1_ref.v1_ref) | copy-start | bytes 1572868
  69.4 0.8 copy-start.2
  76.5 6.1 %copy-start.4 = (f32[256,512]{1,0:T(8,128)S(1)}, f32[256,512]{1,0:T(8,128)}, u32[]{:S(2)}) copy-start(f32[256,512]{1,0:T(8,128)} %get-tuple-element.15) | copy-start | bytes 1572868
  77.6 34.8 %collective-permute-start.4 = (bf16[2,256,256]{2,1,0:T(8,128)(2,1)S(1)}, bf16[2,256,256]{2,1,0:T(8,128)(2,1)S(1)}, u32[]{:S(2)}, u32[]{:S(2)}) collective-permute-start(bf16[2,256,256]{2,1,0:T(8,128)(2,1)S(1)} %convert_element_type.54), channel_id=1, source_target_pairs={{4,0},{8,4},{12,8},{16,12},{20,16},{24,20},{28,24},{32,28},{36,32}... | collective-permute-start | bytes 786440 | tf_op jit(solution)/shard_map/ppermute | solution.py:107
  80.6 50.9 %collective-permute-start.5 = (bf16[2,256,256]{2,1,0:T(8,128)(2,1)S(1)}, bf16[2,256,256]{2,1,0:T(8,128)(2,1)S(1)}, u32[]{:S(2)}, u32[]{:S(2)}) collective-permute-start(bf16[2,256,256]{2,1,0:T(8,128)(2,1)S(1)} %convert_element_type.56), channel_id=1, source_target_pairs={{8,0},{12,4},{16,8},{20,12},{24,16},{28,20},{32,24},{36,28},{40,32... | collective-permute-start | bytes 786440 | tf_op jit(solution)/shard_map/ppermute | solution.py:107
  88.8 42.7 %copy-start.6 = (f32[2,256,256]{2,1,0:T(8,128)S(1)}, f32[2,256,256]{2,1,0:T(8,128)}, u32[]{:S(2)}) copy-start(f32[2,256,256]{2,1,0:T(8,128)} %get-tuple-element.16) | copy-start | bytes 1572868
  89.9 48.1 %collective-permute-start.2 = (bf16[2,256,256]{2,1,0:T(8,128)(2,1)S(1)}, bf16[2,256,256]{2,1,0:T(8,128)(2,1)S(1)}, u32[]{:S(2)}, u32[]{:S(2)}) collective-permute-start(bf16[2,256,256]{2,1,0:T(8,128)(2,1)S(1)} %convert_element_type.47), channel_id=1, source_target_pairs={{4,0},{8,4},{12,8},{16,12},{20,16},{24,20},{28,24},{32,28},{36,32}... | collective-permute-start | bytes 786440 | tf_op jit(solution)/shard_map/ppermute | solution.py:107
  92.9 60.6 %collective-permute-start.3 = (bf16[2,256,256]{2,1,0:T(8,128)(2,1)S(1)}, bf16[2,256,256]{2,1,0:T(8,128)(2,1)S(1)}, u32[]{:S(2)}, u32[]{:S(2)}) collective-permute-start(bf16[2,256,256]{2,1,0:T(8,128)(2,1)S(1)} %convert_element_type.49), channel_id=1, source_target_pairs={{8,0},{12,4},{16,8},{20,12},{24,16},{28,20},{32,24},{36,28},{40,32... | collective-permute-start | bytes 786440 | tf_op jit(solution)/shard_map/ppermute | solution.py:107
  132.2 5.8 %copy-start.3 = (f32[256,512]{1,0:T(8,128)S(1)}, f32[256,512]{1,0:T(8,128)}, u32[]{:S(2)}) copy-start(f32[256,512]{1,0:T(8,128)} %get-tuple-element.11) | copy-start | bytes 1572868
  133.3 20.2 %copy-start.5 = (f32[2,256,256]{2,1,0:T(8,128)S(1)}, f32[2,256,256]{2,1,0:T(8,128)}, u32[]{:S(2)}) copy-start(f32[2,256,256]{2,1,0:T(8,128)} %get-tuple-element.12) | copy-start | bytes 1572868
  134.5 21.4 %all-to-all-start.2 = ((bf16[4,2,32768]{2,1,0:T(2,128)(2,1)}), bf16[4,2,32768]{2,1,0:T(2,128)(2,1)S(1)}, u32[]{:S(2)}, u32[]{:S(2)}) async-start(bf16[4,2,32768]{2,1,0:T(2,128)(2,1)} %reshape.51), calls=%async_computation.2 | async-start | bytes 1048576 | tf_op jit(solution)/shard_map/all_to_all | solution.py:144
  155.9 12.6 %all-to-all-start.1 = ((bf16[4,2,32768]{2,1,0:T(2,128)(2,1)}), bf16[4,2,32768]{2,1,0:T(2,128)(2,1)S(1)}, u32[]{:S(2)}, u32[]{:S(2)}) async-start(bf16[4,2,32768]{2,1,0:T(2,128)(2,1)} %reshape.49), calls=%async_computation.1 | async-start | bytes 1048576 | tf_op jit(solution)/shard_map/all_to_all | solution.py:144

commit v12 on v10

--- a/solution.py
+++ b/solution.py
@@ -115,8 +115,8 @@
         kv1 = passed_along(kv_local, "ctx", 1)
         kv2 = passed_along(kv1, "ctx", 1)
     else:
+        kv2 = passed_along(kv_local, "ctx", 2)
         kv1 = passed_along(kv_local, "ctx", 1)
-        kv2 = passed_along(kv_local, "ctx", 2)
     dq, dkv0, dkv1, dkv2 = attend(rel, x_all, (kv1, kv2))
     if CHAIN:
         carried = passed_along(dkv2.astype(jnp.bfloat16), "ctx", -1)
@@ -124,7 +124,7 @@
         kv_total = dkv0 + carried
     else:
         kv_total = dkv0
-        for distance, part in ((1, dkv1), (2, dkv2)):
+        for distance, part in ((2, dkv2), (1, dkv1)):
             kv_total = kv_total + passed_along(part.astype(jnp.bfloat16), "ctx", -distance)
     out_loc = jnp.concatenate(
         [dq.astype(jnp.bfloat16), kv_total[0].astype(jnp.bfloat16), kv_total[1].astype(jnp.bfloat16)],

time: 153 us -> 158 us (1.033)
  the two profiles are of different devices: /device:TPU:62 before, /device:TPU:182 now
where the time goes in v12:
time: 158 us; the launch traced here: 157 us
  waiting for transfers between devices  72.3 us (46%)
  starting transfers between devices  46.3 us (29%)
  local copies, waits for them, and re-layouts  16.9 us (11%)
  Pallas kernels  12.3 us (8%)
  other arithmetic  7.82 us (5%)
    ppermute x8, waiting for transfers between devices, passed_along(): return lax.ppermute(block, axis, route)  53.2 us
    ppermute x8, starting transfers between devices, passed_along(): return lax.ppermute(block, axis, route)  31.9 us
    pallas_call x2, Pallas kernels, attend(): pl.pallas_call(attn_kernel, grid=(groups,), in_specs=[pl.BlockSpec((tok,...  12.3 us
    all_to_all x2, waiting for transfers between devices, chunk_pass(): lax.all_to_all(x_in, 'head', split_axis=1, concat_axis=0, tiled=True)  11.2 us
    all_to_all x2, waiting for transfers between devices, chunk_pass(): lax.all_to_all(out_loc, 'head', split_axis=0, concat_axis=1, tiled=True)  7.88 us
    all_to_all x2, starting transfers between devices, chunk_pass(): lax.all_to_all(out_loc, 'head', split_axis=0, concat_axis=1, tiled=True)  7.25 us
    all_to_all x2, starting transfers between devices, chunk_pass(): lax.all_to_all(x_in, 'head', split_axis=1, concat_axis=0, tiled=True)  7.13 us
    unnamed x34, local copies, waits for them, and re-layouts  5.54 us
  transfers between devices with their start and end apart: 12, of which 8 were waited for; matrix products, arithmetic and copies ran while one was open for 7% of the time, Pallas kernels for 8%

profile of v12, /device:TPU:182, one launch (start us, length us, event | category | flops | bytes accessed | tf_op | source)
XLA Modules:
  0.0 156.8 jit_solution(4778467255005627685)
XLA Ops:
  0.6 1.1 reshape.45
  1.8 1.1 reshape.46
  2.9 0.4 fusion.5
  4.0 0.4 reshape.47
  4.4 0.4 reshape.48
  4.8 0.7 fusion.3
  5.5 0.7 fusion.2
  6.6 1.0 pad_maximum_fusion.1
  7.6 3.6 %all-to-all-start.2 = ((bf16[64,4,1536]{2,0,1:T(8,128)(2,1)}), bf16[64,4,1536]{2,0,1:T(8,128)(2,1)S(1)}, u32[]{:S(2)}, u32[]{:S(2)}) async-start(bf16[64,4,1536]{2,0,1:T(8,128)(2,1)} %pad_maximum_fusion.1), calls=%async_computation.2 | async-start | bytes 1572864 | tf_op jit(solution)/shard_map/all_to_all | solution.py:111
  11.6 0.9 pad_maximum_fusion
  12.6 10.3 %all-to-all-done.2 = bf16[64,4,1536]{2,0,1:T(8,128)(2,1)S(1)} async-done(((bf16[64,4,1536]{2,0,1:T(8,128)(2,1)}), bf16[64,4,1536]{2,0,1:T(8,128)(2,1)S(1)}, u32[]{:S(2)}, u32[]{:S(2)}) %all-to-all-start.2) | async-done | bytes 786464 | tf_op jit(solution)/shard_map/all_to_all | solution.py:111
  22.9 3.5 %all-to-all-start = ((bf16[64,4,1536]{2,0,1:T(8,128)(2,1)}), bf16[64,4,1536]{2,0,1:T(8,128)(2,1)S(1)}, u32[]{:S(2)}, u32[]{:S(2)}) async-start(bf16[64,4,1536]{2,0,1:T(8,128)(2,1)} %pad_maximum_fusion), calls=%async_computation | async-start | bytes 1572864 | tf_op jit(solution)/shard_map/all_to_all | solution.py:111
  26.4 6.4 %collective-permute-start.5 = (bf16[256,512]{1,0:T(8,128)(2,1)S(1)}, bf16[256,512]{1,0:T(8,128)(2,1)S(1)}, u32[]{:S(2)}, u32[]{:S(2)}) collective-permute-start(bf16[256,512]{1,0:T(8,128)(2,1)S(1)} %slice.83), channel_id=1, source_target_pairs={{0,8},{4,12},{8,16},{12,20},{16,24},{20,28},{24,32},{28,36},{32,40... | collective-permute-start | bytes 786440 | tf_op jit(solution)/shard_map/ppermute | solution.py:106
  32.8 3.5 %collective-permute-start.4 = (bf16[256,512]{1,0:T(8,128)(2,1)S(1)}, bf16[256,512]{1,0:T(8,128)(2,1)S(1)}, u32[]{:S(2)}, u32[]{:S(2)}) collective-permute-start(bf16[256,512]{1,0:T(8,128)(2,1)S(1)} %slice.83), channel_id=1, source_target_pairs={{0,4},{4,8},{8,12},{12,16},{16,20},{20,24},{24,28},{28,32},{32,36}... | collective-permute-start | bytes 786440 | tf_op jit(solution)/shard_map/ppermute | solution.py:106
  36.3 0.8 copy.63.rel_ref
  37.1 0.9 all-to-all-done
  38.0 6.4 %collective-permute-start.1 = (bf16[256,512]{1,0:T(8,128)(2,1)S(1)}, bf16[256,512]{1,0:T(8,128)(2,1)S(1)}, u32[]{:S(2)}, u32[]{:S(2)}) collective-permute-start(bf16[256,512]{1,0:T(8,128)(2,1)S(1)} %slice.76), channel_id=1, source_target_pairs={{0,8},{4,12},{8,16},{12,20},{16,24},{20,28},{24,32},{28,36},{32,40... | collective-permute-start | bytes 786440 | tf_op jit(solution)/shard_map/ppermute | solution.py:106
  44.4 3.5 %collective-permute-start = (bf16[256,512]{1,0:T(8,128)(2,1)S(1)}, bf16[256,512]{1,0:T(8,128)(2,1)S(1)}, u32[]{:S(2)}, u32[]{:S(2)}) collective-permute-start(bf16[256,512]{1,0:T(8,128)(2,1)S(1)} %slice.76), channel_id=1, source_target_pairs={{0,4},{4,8},{8,12},{12,16},{16,20},{20,24},{24,28},{28,32},{32,36}... | collective-permute-start | bytes 786440 | tf_op jit(solution)/shard_map/ppermute | solution.py:106
  47.9 2.8 %collective-permute-done.4.k1_ref.v1_ref = bf16[256,512]{1,0:T(8,128)(2,1)S(1)} collective-permute-done((bf16[256,512]{1,0:T(8,128)(2,1)S(1)}, bf16[256,512]{1,0:T(8,128)(2,1)S(1)}, u32[]{:S(2)}, u32[]{:S(2)}) %collective-permute-start.4) | collective-permute-done | bytes 262176 | tf_op jit(solution)/shard_map/ppermute | solution.py:106
  50.7 0.7 copy-done.4
  51.4 6.2 %shard_map.77 = (f32[256,512]{1,0:T(8,128)}, f32[2,256,256]{2,1,0:T(8,128)}, f32[2,256,256]{2,1,0:T(8,128)}, f32[2,256,256]{2,1,0:T(8,128)}) custom-call(s32[256,1]{1,0:T(8,128)} %copy.63.rel_ref, bf16[256,1536]{1,0:T(8,128)(2,1)} %bitcast.46, bf16[256,1536]{1,0:T(8,128)(2,1)} %bitcast.47, bf16[256,1536]{1,0:T(8,128)(2,1)} %bitcast.48, ...), custom_call_target="tpu_custom_call" | custom-call | tf_op jit(solution)/shard_map/pallas_call | solution.py:79
  57.6 1.1 convert_element_type.54
  58.7 1.1 convert_element_type.56
  59.8 1.9 %collective-permute-start.7 = (bf16[2,256,256]{2,1,0:T(8,128)(2,1)S(1)}, bf16[2,256,256]{2,1,0:T(8,128)(2,1)S(1)}, u32[]{:S(2)}, u32[]{:S(2)}) collective-permute-start(bf16[2,256,256]{2,1,0:T(8,128)(2,1)S(1)} %convert_element_type.56), channel_id=1, source_target_pairs={{4,0},{8,4},{12,8},{16,12},{20,16},{24,20},{28,24},{32,28},{36,32}... | collective-permute-start | bytes 786440 | tf_op jit(solution)/shard_map/ppermute | solution.py:106
  61.7 4.8 %collective-permute-start.6 = (bf16[2,256,256]{2,1,0:T(8,128)(2,1)S(1)}, bf16[2,256,256]{2,1,0:T(8,128)(2,1)S(1)}, u32[]{:S(2)}, u32[]{:S(2)}) collective-permute-start(bf16[2,256,256]{2,1,0:T(8,128)(2,1)S(1)} %convert_element_type.54), channel_id=1, source_target_pairs={{8,0},{12,4},{16,8},{20,12},{24,16},{28,20},{32,24},{36,28},{40,32... | collective-permute-start | bytes 786440 | tf_op jit(solution)/shard_map/ppermute | solution.py:106
  66.6 1.6 %collective-permute-done.k1_ref.v1_ref = bf16[256,512]{1,0:T(8,128)(2,1)S(1)} collective-permute-done((bf16[256,512]{1,0:T(8,128)(2,1)S(1)}, bf16[256,512]{1,0:T(8,128)(2,1)S(1)}, u32[]{:S(2)}, u32[]{:S(2)}) %collective-permute-start) | collective-permute-done | bytes 262176 | tf_op jit(solution)/shard_map/ppermute | solution.py:106
  68.2 0.7 copy-done.5
  68.9 6.2 %shard_map.76 = (f32[256,512]{1,0:T(8,128)}, f32[2,256,256]{2,1,0:T(8,128)}, f32[2,256,256]{2,1,0:T(8,128)}, f32[2,256,256]{2,1,0:T(8,128)}) custom-call(s32[256,1]{1,0:T(8,128)} %copy.63.rel_ref, bf16[256,1536]{1,0:T(8,128)(2,1)} %bitcast.51, bf16[256,1536]{1,0:T(8,128)(2,1)} %bitcast.52, bf16[256,1536]{1,0:T(8,128)(2,1)} %bitcast.53, ...), custom_call_target="tpu_custom_call" | custom-call | tf_op jit(solution)/shard_map/pallas_call | solution.py:79
  75.1 1.2 convert_element_type.47
  76.3 1.9 %collective-permute-start.3 = (bf16[2,256,256]{2,1,0:T(8,128)(2,1)S(1)}, bf16[2,256,256]{2,1,0:T(8,128)(2,1)S(1)}, u32[]{:S(2)}, u32[]{:S(2)}) collective-permute-start(bf16[2,256,256]{2,1,0:T(8,128)(2,1)S(1)} %convert_element_type.49), channel_id=1, source_target_pairs={{4,0},{8,4},{12,8},{16,12},{20,16},{24,20},{28,24},{32,28},{36,32}... | collective-permute-start | bytes 786440 | tf_op jit(solution)/shard_map/ppermute | solution.py:106
  78.2 3.6 %collective-permute-start.2 = (bf16[2,256,256]{2,1,0:T(8,128)(2,1)S(1)}, bf16[2,256,256]{2,1,0:T(8,128)(2,1)S(1)}, u32[]{:S(2)}, u32[]{:S(2)}) collective-permute-start(bf16[2,256,256]{2,1,0:T(8,128)(2,1)S(1)} %convert_element_type.47), channel_id=1, source_target_pairs={{8,0},{12,4},{16,8},{20,12},{24,16},{28,20},{32,24},{36,28},{40,32... | collective-permute-start | bytes 786440 | tf_op jit(solution)/shard_map/ppermute | solution.py:106
  81.8 1.9 %collective-permute-done.7 = bf16[2,256,256]{2,1,0:T(8,128)(2,1)S(1)} collective-permute-done((bf16[2,256,256]{2,1,0:T(8,128)(2,1)S(1)}, bf16[2,256,256]{2,1,0:T(8,128)(2,1)S(1)}, u32[]{:S(2)}, u32[]{:S(2)}) %collective-permute-start.7) | collective-permute-done | bytes 262176 | tf_op jit(solution)/shard_map/ppermute | solution.py:106
  83.7 27.9 %collective-permute-done.6 = bf16[2,256,256]{2,1,0:T(8,128)(2,1)S(1)} collective-permute-done((bf16[2,256,256]{2,1,0:T(8,128)(2,1)S(1)}, bf16[2,256,256]{2,1,0:T(8,128)(2,1)S(1)}, u32[]{:S(2)}, u32[]{:S(2)}) %collective-permute-start.6) | collective-permute-done | bytes 262176 | tf_op jit(solution)/shard_map/ppermute | solution.py:106
  111.8 0.5 broadcast
  112.3 1.0 reduce.1
  113.3 1.2 reshape.56
  114.5 3.6 %all-to-all-start.3 = ((bf16[4,2,32768]{2,1,0:T(2,128)(2,1)}), bf16[4,2,32768]{2,1,0:T(2,128)(2,1)S(1)}, u32[]{:S(2)}, u32[]{:S(2)}) async-start(bf16[4,2,32768]{2,1,0:T(2,128)(2,1)} %reshape.56), calls=%async_computation.3 | async-start | bytes 1048576 | tf_op jit(solution)/shard_map/all_to_all | solution.py:133
  118.2 19.1 %collective-permute-done.2 = bf16[2,256,256]{2,1,0:T(8,128)(2,1)S(1)} collective-permute-done((bf16[2,256,256]{2,1,0:T(8,128)(2,1)S(1)}, bf16[2,256,256]{2,1,0:T(8,128)(2,1)S(1)}, u32[]{:S(2)}, u32[]{:S(2)}) %collective-permute-start.2) | collective-permute-done | bytes 262176 | tf_op jit(solution)/shard_map/ppermute | solution.py:106
  137.4 1.0 reduce
  138.5 1.2 reshape.54
  139.6 3.7 %all-to-all-start.1 = ((bf16[4,2,32768]{2,1,0:T(2,128)(2,1)}), bf16[4,2,32768]{2,1,0:T(2,128)(2,1)S(1)}, u32[]{:S(2)}, u32[]{:S(2)}) async-start(bf16[4,2,32768]{2,1,0:T(2,128)(2,1)} %reshape.54), calls=%async_computation.1 | async-start | bytes 1048576 | tf_op jit(solution)/shard_map/all_to_all | solution.py:133
  143.3 0.5 reshape.57
  144.0 7.9 %all-to-all-done.1 = bf16[4,2,32768]{2,1,0:T(2,128)(2,1)S(1)} async-done(((bf16[4,2,32768]{2,1,0:T(2,128)(2,1)}), bf16[4,2,32768]{2,1,0:T(2,128)(2,1)S(1)}, u32[]{:S(2)}, u32[]{:S(2)}) %all-to-all-start.1) | async-done | bytes 524320 | tf_op jit(solution)/shard_map/all_to_all | solution.py:133
  151.9 0.5 reshape.55
  153.0 0.9 reshape.53
  153.9 0.5 copy.71
  154.4 1.2 reshape.51
  155.9 0.9 reshape.52
  (53 shorter events, 3.0 us)
Async XLA Ops:
  2.9 1.0 copy-start.9
  3.3 1.1 copy-start.10
  7.6 15.3 %all-to-all-start.2 = ((bf16[64,4,1536]{2,0,1:T(8,128)(2,1)}), bf16[64,4,1536]{2,0,1:T(8,128)(2,1)S(1)}, u32[]{:S(2)}, u32[]{:S(2)}) async-start(bf16[64,4,1536]{2,0,1:T(8,128)(2,1)} %pad_maximum_fusion.1), calls=%async_computation.2 | async-start | bytes 1572864 | tf_op jit(solution)/shard_map/all_to_all | solution.py:111
  12.6 23.7 %copy-start.13 = (s32[256]{0:T(256)S(1)}, s32[256]{0:T(256)}, u32[]{:S(2)}) copy-start(s32[256]{0:T(256)} %param.9) | copy-start | bytes 3076
  22.9 3.5 %copy-start = (bf16[64,4,1536]{2,0,1:T(8,128)(2,1)}, bf16[64,4,1536]{2,0,1:T(8,128)(2,1)S(1)}, u32[]{:S(2)}) copy-start(bf16[64,4,1536]{2,0,1:T(8,128)(2,1)S(1)} %all-to-all-done.2) | copy-start | bytes 2359300
  22.9 15.1 %all-to-all-start = ((bf16[64,4,1536]{2,0,1:T(8,128)(2,1)}), bf16[64,4,1536]{2,0,1:T(8,128)(2,1)S(1)}, u32[]{:S(2)}, u32[]{:S(2)}) async-start(bf16[64,4,1536]{2,0,1:T(8,128)(2,1)} %pad_maximum_fusion), calls=%async_computation | async-start | bytes 1572864 | tf_op jit(solution)/shard_map/all_to_all | solution.py:111
  26.4 21.4 %collective-permute-start.5 = (bf16[256,512]{1,0:T(8,128)(2,1)S(1)}, bf16[256,512]{1,0:T(8,128)(2,1)S(1)}, u32[]{:S(2)}, u32[]{:S(2)}) collective-permute-start(bf16[256,512]{1,0:T(8,128)(2,1)S(1)} %slice.83), channel_id=1, source_target_pairs={{0,8},{4,12},{8,16},{12,20},{16,24},{20,28},{24,32},{28,36},{32,40... | collective-permute-start | bytes 786440 | tf_op jit(solution)/shard_map/ppermute | solution.py:106
  32.8 17.9 %collective-permute-start.4 = (bf16[256,512]{1,0:T(8,128)(2,1)S(1)}, bf16[256,512]{1,0:T(8,128)(2,1)S(1)}, u32[]{:S(2)}, u32[]{:S(2)}) collective-permute-start(bf16[256,512]{1,0:T(8,128)(2,1)S(1)} %slice.83), channel_id=1, source_target_pairs={{0,4},{4,8},{8,12},{12,16},{16,20},{20,24},{24,28},{28,32},{32,36}... | collective-permute-start | bytes 786440 | tf_op jit(solution)/shard_map/ppermute | solution.py:106
  38.0 19.6 %copy-start.1 = (bf16[64,4,1536]{2,0,1:T(8,128)(2,1)}, bf16[64,4,1536]{2,0,1:T(8,128)(2,1)S(1)}, u32[]{:S(2)}) copy-start(bf16[64,4,1536]{2,0,1:T(8,128)(2,1)S(1)} %all-to-all-done) | copy-start | bytes 2359300
  38.0 28.6 %collective-permute-start.1 = (bf16[256,512]{1,0:T(8,128)(2,1)S(1)}, bf16[256,512]{1,0:T(8,128)(2,1)S(1)}, u32[]{:S(2)}, u32[]{:S(2)}) collective-permute-start(bf16[256,512]{1,0:T(8,128)(2,1)S(1)} %slice.76), channel_id=1, source_target_pairs={{0,8},{4,12},{8,16},{12,20},{16,24},{20,28},{24,32},{28,36},{32,40... | collective-permute-start | bytes 786440 | tf_op jit(solution)/shard_map/ppermute | solution.py:106
  44.4 23.9 %collective-permute-start = (bf16[256,512]{1,0:T(8,128)(2,1)S(1)}, bf16[256,512]{1,0:T(8,128)(2,1)S(1)}, u32[]{:S(2)}, u32[]{:S(2)}) collective-permute-start(bf16[256,512]{1,0:T(8,128)(2,1)S(1)} %slice.76), channel_id=1, source_target_pairs={{0,4},{4,8},{8,12},{12,16},{16,20},{20,24},{24,28},{28,32},{32,36}... | collective-permute-start | bytes 786440 | tf_op jit(solution)/shard_map/ppermute | solution.py:106
  47.9 2.8 %copy-start.2 = (bf16[256,512]{1,0:T(8,128)(2,1)}, bf16[256,512]{1,0:T(8,128)(2,1)S(1)}, u32[]{:S(2)}) copy-start(bf16[256,512]{1,0:T(8,128)(2,1)S(1)} %collective-permute-done.5.k2_ref.v2_ref) | copy-start | bytes 786436
  50.7 0.7 copy-start.4
  57.6 9.0 %copy-start.7 = (f32[256,512]{1,0:T(8,128)S(1)}, f32[256,512]{1,0:T(8,128)}, u32[]{:S(2)}) copy-start(f32[256,512]{1,0:T(8,128)} %get-tuple-element.15) | copy-start | bytes 1572868
  59.8 23.9 %collective-permute-start.7 = (bf16[2,256,256]{2,1,0:T(8,128)(2,1)S(1)}, bf16[2,256,256]{2,1,0:T(8,128)(2,1)S(1)}, u32[]{:S(2)}, u32[]{:S(2)}) collective-permute-start(bf16[2,256,256]{2,1,0:T(8,128)(2,1)S(1)} %convert_element_type.56), channel_id=1, source_target_pairs={{4,0},{8,4},{12,8},{16,12},{20,16},{24,20},{28,24},{32,28},{36,32}... | collective-permute-start | bytes 786440 | tf_op jit(solution)/shard_map/ppermute | solution.py:106
  61.7 49.9 %collective-permute-start.6 = (bf16[2,256,256]{2,1,0:T(8,128)(2,1)S(1)}, bf16[2,256,256]{2,1,0:T(8,128)(2,1)S(1)}, u32[]{:S(2)}, u32[]{:S(2)}) collective-permute-start(bf16[2,256,256]{2,1,0:T(8,128)(2,1)S(1)} %convert_element_type.54), channel_id=1, source_target_pairs={{8,0},{12,4},{16,8},{20,12},{24,16},{28,20},{32,24},{36,28},{40,32... | collective-permute-start | bytes 786440 | tf_op jit(solution)/shard_map/ppermute | solution.py:106
  66.6 1.6 %copy-start.3 = (bf16[256,512]{1,0:T(8,128)(2,1)}, bf16[256,512]{1,0:T(8,128)(2,1)S(1)}, u32[]{:S(2)}) copy-start(bf16[256,512]{1,0:T(8,128)(2,1)S(1)} %collective-permute-done.1.k2_ref.v2_ref) | copy-start | bytes 786436
  68.2 0.7 copy-start.5
  75.1 1.2 copy-start.8
  75.1 36.5 %copy-start.12 = (f32[2,256,256]{2,1,0:T(8,128)S(1)}, f32[2,256,256]{2,1,0:T(8,128)}, u32[]{:S(2)}) copy-start(f32[2,256,256]{2,1,0:T(8,128)} %get-tuple-element.16) | copy-start | bytes 1572868
  76.3 41.9 %collective-permute-start.3 = (bf16[2,256,256]{2,1,0:T(8,128)(2,1)S(1)}, bf16[2,256,256]{2,1,0:T(8,128)(2,1)S(1)}, u32[]{:S(2)}, u32[]{:S(2)}) collective-permute-start(bf16[2,256,256]{2,1,0:T(8,128)(2,1)S(1)} %convert_element_type.49), channel_id=1, source_target_pairs={{4,0},{8,4},{12,8},{16,12},{20,16},{24,20},{28,24},{32,28},{36,32}... | collective-permute-start | bytes 786440 | tf_op jit(solution)/shard_map/ppermute | solution.py:106
  78.2 59.0 %collective-permute-start.2 = (bf16[2,256,256]{2,1,0:T(8,128)(2,1)S(1)}, bf16[2,256,256]{2,1,0:T(8,128)(2,1)S(1)}, u32[]{:S(2)}, u32[]{:S(2)}) collective-permute-start(bf16[2,256,256]{2,1,0:T(8,128)(2,1)S(1)} %convert_element_type.47), channel_id=1, source_target_pairs={{8,0},{12,4},{16,8},{20,12},{24,16},{28,20},{32,24},{36,28},{40,32... | collective-permute-start | bytes 786440 | tf_op jit(solution)/shard_map/ppermute | solution.py:106
  113.3 4.8 %copy-start.6 = (f32[256,512]{1,0:T(8,128)S(1)}, f32[256,512]{1,0:T(8,128)}, u32[]{:S(2)}) copy-start(f32[256,512]{1,0:T(8,128)} %get-tuple-element.11) | copy-start | bytes 1572868
  114.5 22.7 %copy-start.11 = (f32[2,256,256]{2,1,0:T(8,128)S(1)}, f32[2,256,256]{2,1,0:T(8,128)}, u32[]{:S(2)}) copy-start(f32[2,256,256]{2,1,0:T(8,128)} %get-tuple-element.12) | copy-start | bytes 1572868
  114.5 25.1 %all-to-all-start.3 = ((bf16[4,2,32768]{2,1,0:T(2,128)(2,1)}), bf16[4,2,32768]{2,1,0:T(2,128)(2,1)S(1)}, u32[]{:S(2)}, u32[]{:S(2)}) async-start(bf16[4,2,32768]{2,1,0:T(2,128)(2,1)} %reshape.56), calls=%async_computation.3 | async-start | bytes 1048576 | tf_op jit(solution)/shard_map/all_to_all | solution.py:133
  139.6 12.3 %all-to-all-start.1 = ((bf16[4,2,32768]{2,1,0:T(2,128)(2,1)}), bf16[4,2,32768]{2,1,0:T(2,128)(2,1)S(1)}, u32[]{:S(2)}, u32[]{:S(2)}) async-start(bf16[4,2,32768]{2,1,0:T(2,128)(2,1)} %reshape.54), calls=%async_computation.1 | async-start | bytes 1048576 | tf_op jit(solution)/shard_map/all_to_all | solution.py:133
